TPU v7x, 32 devices: a whole 2x2x4 slice. The times are simulated.
32 devices in a mesh: vert: 16 (over z, y, x), eig: 2 (over core).
Axes of the slice: x: 2, y: 2, z: 4, core: 2. Of those that a mesh axis runs over, the one named last changes fastest.
Arguments:
- eig_table: bfloat16 [32768, 2048], P('vert', 'eig'), may hold values from -0.1875 to 0.1875
- obs_ids: int32 [49152], P('vert'), may hold values from 0 to 2047
- counts: int32 [16], P('vert'), may hold values from 512 to 3072, as said below
- noise_var: float32 [49152], P('vert'), may hold values from 0.05 to 0.5
- eigenvalues: float32 [2048], P('eig'), may hold values from 0.01 to 4
- rhs: float32 [256, 49152], P('eig', 'vert'), may hold values from -6 to 6
Outputs:
- solution: float32 [256, 49152], P('eig', 'vert')
- residual: float32 [256, 49152], P('eig', 'vert')
Inputs may be any that keep to these rules, and one draw needn't show every extreme that they name: `counts`: slots of a shard are filled from its first slot on; the busiest shard fills all 3072.
All inputs are finite; a program needn't handle non-finite values.
Results may differ from a plain program's by a relative error of at most 0.039.
Values may be sent and summed in bfloat16 or wider, within the bound.
No kernel may reach another device: no remote copies, remote signals or barrier semaphores. Data moves between devices by JAX's collectives and lax.ppermute only.
A program may use at most 64 MiB of HBM per device.

v0:
```python
import jax
import jax.numpy as jnp
from jax import lax
from jax.sharding import PartitionSpec as P

ITERS = 2
PIECES = 2


def vert_sum(x, n_vert, finish, encode, decode, side=()):
    side = list(side)

    def beside(k, sent, received):
        if k >= len(side):
            return received
        out = side[k](sent)
        received, out = lax.optimization_barrier((received, out))
        side[k] = out
        return received

    bits = n_vert.bit_length() - 1
    rounds = [list(range(b, min(b + 2, bits))) for b in range(0, bits, 2)]
    me = lax.axis_index("vert")
    cur = x
    plan = []
    for group in rounds:
        n = 1 << len(group)
        digit = sum(((me >> b) & 1) << i for i, b in enumerate(group))
        masks = [sum(((t >> i) & 1) << b for i, b in enumerate(group)) for t in range(n)]
        width = cur.shape[1] // n
        total = lax.dynamic_slice_in_dim(cur, digit * width, width, axis=1)
        sends = [
            encode(lax.dynamic_slice_in_dim(cur, (digit ^ t) * width, width, axis=1))
            for t in range(1, n)
        ]
        gots = [
            lax.ppermute(send, "vert", [(i, i ^ masks[t + 1]) for i in range(n_vert)])
            for t, send in enumerate(sends)
        ]
        gots = beside(len(plan), sends[0], gots)
        for got in gots:
            total = total + decode(got)
        cur = total
        plan.append((n, digit, masks))
    cur = finish(cur)
    for k, (n, digit, masks) in enumerate(reversed(plan), len(plan)):
        width = cur.shape[1]
        out = jnp.zeros((cur.shape[0], width * n), cur.dtype)
        out = lax.dynamic_update_slice_in_dim(out, cur, digit * width, axis=1)
        gots = [
            lax.ppermute(cur, "vert", [(i, i ^ masks[t]) for i in range(n_vert)]) for t in range(1, n)
        ]
        gots = beside(k, cur, gots)
        for t, got in enumerate(gots, 1):
            out = lax.dynamic_update_slice_in_dim(out, got, (digit ^ t) * width, axis=1)
        cur = out
    return cur, side


def make_shards(n_vert, n_eig):
    pair = n_eig == 2
    swap = [(0, 1), (1, 0)]

    def shards(eig_table, obs_ids, counts, noise_var, eigenvalues, rhs):
        capacity = obs_ids.shape[0]
        own = rhs.shape[0]
        samples = own * n_eig
        group = eig_table.shape[1]
        filled = jnp.arange(capacity, dtype=jnp.int32) < counts[0]
        vertices = jnp.arange(eig_table.shape[0], dtype=jnp.int32)
        picker = (obs_ids[:, None] == vertices[None, :]).astype(jnp.bfloat16)
        pieces = PIECES if capacity % (8 * PIECES) == 0 else 1
        span = capacity // pieces

        def piece(p):
            def work(anchor):
                ids, _ = lax.optimization_barrier((obs_ids[p * span : (p + 1) * span], anchor))
                rows = (ids[:, None] == vertices[None, :]).astype(jnp.bfloat16)
                return jnp.dot(rows, eig_table, preferred_element_type=jnp.float32).astype(jnp.bfloat16)

            return work

        built = []

        def coeff_from_table(rows):
            summed = jnp.dot(rows, picker, preferred_element_type=jnp.float32)
            high = summed.astype(jnp.bfloat16)
            low = (summed - high.astype(jnp.float32)).astype(jnp.bfloat16)
            both = jnp.dot(
                jnp.concatenate([high, low], 0), eig_table, preferred_element_type=jnp.float32
            )
            return both[: rows.shape[0]] + both[rows.shape[0] :]
        spectrum = 5.0 * jnp.power(3.0 + eigenvalues, -1.5)
        me_eig = lax.axis_index("eig")

        def finish(piece):
            weights = piece[:samples].astype(jnp.bfloat16)
            sums = piece[samples:]
            high = sums.astype(jnp.bfloat16)
            low = (sums - high.astype(jnp.float32)).astype(jnp.bfloat16)
            return jnp.concatenate([weights, high, low], 0)

        def decode(block):
            return jnp.concatenate(
                [
                    block[:samples].astype(jnp.float32),
                    block[samples : samples + 8].astype(jnp.float32)
                    + block[samples + 8 :].astype(jnp.float32),
                ],
                0,
            )

        def operate(vector, first=False):
            lowered = vector.astype(jnp.bfloat16)
            if pair:
                rows = jnp.concatenate([lowered, lax.ppermute(lowered, "eig", swap)], 0)
            else:
                rows = lax.all_gather(lowered, "eig", axis=0, tiled=True)
            if first:
                coeff = coeff_from_table(rows)
            else:
                coeff = jnp.dot(rows, built[0], preferred_element_type=jnp.float32)
            sums = jnp.zeros((8, group), jnp.float32)
            sums = sums.at[0, :own].set(jnp.sum(vector * vector, axis=1))
            sums = sums.at[1, :own].set(jnp.sum(noise_var[None, :] * vector * vector, axis=1))
            gathered, side = vert_sum(
                jnp.concatenate([coeff * spectrum[None, :], sums], 0),
                n_vert,
                finish,
                finish,
                decode,
                [piece(p) for p in range(pieces)] if first else (),
            )
            if first:
                built.append(jnp.concatenate(side, 0))
            features = built[0]
            weights = gathered[:samples]
            sums = gathered[samples : samples + 8].astype(jnp.float32) + gathered[
                samples + 8 : samples + 16
            ].astype(jnp.float32)
            wide = weights.astype(jnp.float32)
            energy = jnp.sum(wide * wide / spectrum[None, :], axis=1)
            partials = lax.dot_general(
                weights, features, (((1,), (1,)), ((), ())), preferred_element_type=jnp.float32
            ).astype(jnp.bfloat16)
            if pair:
                energy = energy[:own] + lax.ppermute(energy[own:], "eig", swap)
                image = partials[:own].astype(jnp.float32) + lax.ppermute(
                    partials[own:], "eig", swap
                ).astype(jnp.float32)
            else:
                energy = lax.psum_scatter(energy, "eig", scatter_dimension=0, tiled=True)
                image = lax.psum_scatter(
                    partials, "eig", scatter_dimension=0, tiled=True
                ).astype(jnp.float32)
            image = jnp.where(filled[None, :], image, jnp.zeros((), jnp.float32))
            norm = sums[0, :own]
            product = sums[1, :own] + energy
            return image + noise_var[None, :] * vector, norm, product

        residual = jnp.where(filled[None, :], rhs, jnp.zeros((), jnp.float32))
        solution = jnp.zeros_like(residual)
        applied, norm_now, product = operate(residual, first=True)
        step_size = norm_now / product
        direction, along = (residual, applied)
        for iteration in range(ITERS):
            solution = solution + step_size[:, None] * direction
            residual = residual - step_size[:, None] * along
            if iteration + 1 < ITERS:
                applied, norm_next, product = operate(residual)
                beta_ratio = norm_next / norm_now
                step_size = norm_next / (product - beta_ratio * norm_next / step_size)
                direction = residual + beta_ratio[:, None] * direction
                along = applied + beta_ratio[:, None] * along
                norm_now = norm_next
        return (solution, residual)

    return shards


def solution(mesh):
    return jax.shard_map(
        make_shards(mesh.shape["vert"], mesh.shape["eig"]),
        mesh=mesh,
        in_specs=(P("vert", "eig"), P("vert"), P("vert"), P("vert"), P("eig"), P("eig", "vert")),
        out_specs=(P("eig", "vert"), P("eig", "vert")),
        check_vma=False,
    )
```

profile of v0, /device:TPU:0, one launch (start us, length us, event | category | flops | bytes accessed | tf_op | source)
XLA Modules:
  0.0 126.9 jit_solution(10667744475538322233)
XLA Ops:
  1.5 1.5 %select_convert_fusion = bf16[128,3072]{1,0:T(8,128)(2,1)S(1)} fusion(f32[128,3072]{1,0:T(8,128)} %param.19, pred[3072]{0:T(1024)(128)(4,1)S(1)} %iota_compare_fusion.10), kind=kLoop, calls=%fused_computation.47 | loop fusion | flops 393216 | bytes 2362368 | tf_op jit(solution)/shard_map/convert_element_type | solution.py:114
  3.0 0.6 collective-permute-start
  3.6 0.4 fusion.12
  4.3 1.1 collective-permute-done
  5.5 5.1 %subtract_convert_fusion = (bf16[256,2048]{1,0:T(8,128)(2,1)S(1)}, bf16[256,2048]{1,0:T(8,128)(2,1)S(1)}) fusion(s32[3072]{0:T(1024)S(1)} %copy-done.6, bf16[128,3072]{1,0:T(8,128)(2,1)S(1)} %collective-permute-done, bf16[128,3072]{1,0:T(8,128)(2,1)S(1)} %select_convert_fusion), kind=kOutput, calls=%fused_computation.29 | convolution fusion | flops 3232759808 | bytes 3682304 | tf_op jit(solution)/shard_map/dot_general | solution.py:86
  10.6 2.4 %fusion.8 = f32[512,1024]{1,0:T(8,128)S(1)} fusion(bf16[2048,1024]{1,0:T(8,128)(2,1)S(1)} %copy-done.10, bf16[256,2048]{1,0:T(8,128)(2,1)S(1)} %get-tuple-element.105, bf16[256,2048]{1,0:T(8,128)(2,1)S(1)} %get-tuple-element.106), kind=kOutput, calls=%fused_computation.25 | convolution fusion | flops 2151677952 | bytes 8388608 | tf_op jit(solution)/shard_map/dot_general | solution.py:89
  13.3 2.9 %collective-permute-start.1 = (bf16[272,256]{1,0:T(8,128)(2,1)S(1)}, bf16[272,256]{1,0:T(8,128)(2,1)S(1)}, u32[]{:S(2)}, u32[]{:S(2)}) collective-permute-start(bf16[272,256]{1,0:T(8,128)(2,1)S(1)} %pad_maximum_fusion), channel_id=1, source_target_pairs={{0,2},{2,0},{4,6},{6,4},{8,10},{10,8},{12,14},{14,12},{16,18},{18,... | collective-permute-start | bytes 417800 | tf_op jit(solution)/shard_map/ppermute | solution.py:37
  16.3 1.6 %collective-permute-start.2 = (bf16[272,256]{1,0:T(8,128)(2,1)S(1)}, bf16[272,256]{1,0:T(8,128)(2,1)S(1)}, u32[]{:S(2)}, u32[]{:S(2)}) collective-permute-start(bf16[272,256]{1,0:T(8,128)(2,1)S(1)} %pad_maximum_fusion.1), channel_id=1, source_target_pairs={{0,4},{2,6},{4,0},{6,2},{8,12},{10,14},{12,8},{14,10},{16,20},{18,... | collective-permute-start | bytes 417800 | tf_op jit(solution)/shard_map/ppermute | solution.py:37
  17.9 7.2 %fusion.7 = bf16[1536,1024]{1,0:T(8,128)(2,1)S(1)} fusion(bf16[2048,1024]{1,0:T(8,128)(2,1)S(1)} %copy-done.10, s32[1536]{0:T(1024)S(1)} %get-tuple-element.60), kind=kOutput, calls=%fused_computation.12 | convolution fusion | flops 6447169536 | bytes 7346176 | tf_op jit(solution)/shard_map/dot_general | solution.py:79
  25.6 2.1 %collective-permute-start.4 = (bf16[272,64]{1,0:T(8,128)(2,1)S(1)}, bf16[272,64]{1,0:T(8,128)(2,1)S(1)}, u32[]{:S(2)}, u32[]{:S(2)}) collective-permute-start(bf16[272,64]{1,0:T(8,128)(2,1)S(1)} %pad_maximum_fusion.6), channel_id=1, source_target_pairs={{0,8},{2,10},{4,12},{6,14},{8,0},{10,2},{12,4},{14,6},{16,24},{18,... | collective-permute-start | bytes 104456 | tf_op jit(solution)/shard_map/ppermute | solution.py:37
  27.7 2.7 %collective-permute-start.5 = (bf16[272,64]{1,0:T(8,128)(2,1)S(1)}, bf16[272,64]{1,0:T(8,128)(2,1)S(1)}, u32[]{:S(2)}, u32[]{:S(2)}) collective-permute-start(bf16[272,64]{1,0:T(8,128)(2,1)S(1)} %pad_maximum_fusion.7), channel_id=1, source_target_pairs={{0,16},{2,18},{4,20},{6,22},{8,24},{10,26},{12,28},{14,30},{16,0},... | collective-permute-start | bytes 104456 | tf_op jit(solution)/shard_map/ppermute | solution.py:37
  30.5 8.6 %fusion.6 = bf16[1536,1024]{1,0:T(8,128)(2,1)} fusion(bf16[2048,1024]{1,0:T(8,128)(2,1)S(1)} %copy-done.10, s32[1536]{0:T(1024)S(1)} %get-tuple-element.64), kind=kOutput, calls=%fused_computation.11 | convolution fusion | flops 6447169536 | bytes 7346176 | tf_op jit(solution)/shard_map/dot_general | solution.py:79
  39.3 0.7 collective-permute-start.7
  40.1 3.5 %collective-permute-start.8 = (bf16[272,64]{1,0:T(8,128)(2,1)S(1)}, bf16[272,64]{1,0:T(8,128)(2,1)S(1)}, u32[]{:S(2)}, u32[]{:S(2)}) collective-permute-start(bf16[272,64]{1,0:T(8,128)(2,1)S(1)} %pad_maximum_fusion.9), channel_id=1, source_target_pairs={{0,16},{2,18},{4,20},{6,22},{8,24},{10,26},{12,28},{14,30},{16,0},... | collective-permute-start | bytes 104456 | tf_op jit(solution)/shard_map/ppermute | solution.py:51
  43.8 2.0 %constant_dynamic-update-slice_fusion.9 = bf16[3072,1024]{1,0:T(8,128)(2,1)} fusion(bf16[1536,1024]{1,0:T(8,128)(2,1)S(1)} %fusion.7), kind=kLoop, calls=%fused_computation.154 | loop fusion | bytes 6291456
  45.7 0.3 dynamic_update_slice.48
  46.1 0.6 dynamic_update_slice.49
  46.7 0.6 collective-permute-done.8
  47.3 0.3 dynamic_update_slice.50
  47.6 2.1 %collective-permute-done.9 = bf16[272,64]{1,0:T(8,128)(2,1)S(1)} collective-permute-done((bf16[272,64]{1,0:T(8,128)(2,1)S(1)}, bf16[272,64]{1,0:T(8,128)(2,1)S(1)}, u32[]{:S(2)}, u32[]{:S(2)}) %collective-permute-start.9) | collective-permute-done | bytes 34848 | tf_op jit(solution)/shard_map/ppermute | solution.py:51
  49.7 0.5 dynamic_update_slice.51
  50.2 1.6 %collective-permute-start.10 = (bf16[272,256]{1,0:T(8,128)(2,1)S(1)}, bf16[272,256]{1,0:T(8,128)(2,1)S(1)}, u32[]{:S(2)}, u32[]{:S(2)}) collective-permute-start(bf16[272,256]{1,0:T(8,128)(2,1)S(1)} %dynamic_update_slice.51), channel_id=1, source_target_pairs={{0,2},{2,0},{4,6},{6,4},{8,10},{10,8},{12,14},{14,12},{16,18},{18,... | collective-permute-start | bytes 417800 | tf_op jit(solution)/shard_map/ppermute | solution.py:51
  51.8 3.9 %constant_dynamic-update-slice_fusion.8 = bf16[3072,1024]{1,0:T(8,128)(2,1)} fusion(bf16[3072,1024]{1,0:T(8,128)(2,1)} %constant_dynamic-update-slice_fusion.9, bf16[1536,1024]{1,0:T(8,128)(2,1)} %fusion.6), kind=kLoop, calls=%fused_computation.153 | loop fusion | bytes 6291456 | tf_op jit(solution)/shard_map/concatenate | solution.py:135
  55.7 1.5 %collective-permute-start.11 = (bf16[272,256]{1,0:T(8,128)(2,1)S(1)}, bf16[272,256]{1,0:T(8,128)(2,1)S(1)}, u32[]{:S(2)}, u32[]{:S(2)}) collective-permute-start(bf16[272,256]{1,0:T(8,128)(2,1)S(1)} %dynamic_update_slice.51), channel_id=1, source_target_pairs={{0,4},{2,6},{4,0},{6,2},{8,12},{10,14},{12,8},{14,10},{16,20},{18,... | collective-permute-start | bytes 417800 | tf_op jit(solution)/shard_map/ppermute | solution.py:51
  57.2 0.5 collective-permute-start.12
  57.8 2.9 %collective-permute-done.11 = bf16[272,256]{1,0:T(8,128)(2,1)S(1)} collective-permute-done((bf16[272,256]{1,0:T(8,128)(2,1)S(1)}, bf16[272,256]{1,0:T(8,128)(2,1)S(1)}, u32[]{:S(2)}, u32[]{:S(2)}) %collective-permute-start.11) | collective-permute-done | bytes 139296 | tf_op jit(solution)/shard_map/ppermute | solution.py:51
  60.7 2.4 %collective-permute-done.12 = bf16[272,256]{1,0:T(8,128)(2,1)S(1)} collective-permute-done((bf16[272,256]{1,0:T(8,128)(2,1)S(1)}, bf16[272,256]{1,0:T(8,128)(2,1)S(1)}, u32[]{:S(2)}, u32[]{:S(2)}) %collective-permute-start.12) | collective-permute-done | bytes 139296 | tf_op jit(solution)/shard_map/ppermute | solution.py:51
  63.2 4.6 %convolution_convert_fusion.1 = bf16[256,3072]{1,0:T(8,128)(2,1)S(1)} fusion(bf16[3072,1024]{1,0:T(8,128)(2,1)} %constant_dynamic-update-slice_fusion.8, bf16[272,1024]{1,0:T(8,128)(2,1)S(1)} %constant_dynamic-update-slice_fusion.4), kind=kOutput, calls=%fused_computation.10 | convolution fusion | flops 1611399168 | bytes 8388608 | tf_op jit(solution)/shard_map/dot_general | solution.py:143
  68.2 0.6 collective-permute-start.13
  68.7 1.5 %collective-permute-done.13 = f32[128]{0:T(128)S(1)} collective-permute-done((f32[128]{0:T(128)S(1)}, f32[128]{0:T(128)S(1)}, u32[]{:S(2)}, u32[]{:S(2)}) %collective-permute-start.13) | collective-permute-done | bytes 544 | tf_op jit(solution)/shard_map/ppermute | solution.py:147
  70.2 0.6 copy-done.8
  70.8 0.9 fusion.13
  71.7 1.0 convert_element_type.359
  72.9 0.4 scatter.19
  73.2 2.1 %collective-permute-done.15 = bf16[128,3072]{1,0:T(8,128)(2,1)} collective-permute-done((bf16[128,3072]{1,0:T(8,128)(2,1)}, bf16[128,3072]{1,0:T(8,128)(2,1)}, u32[]{:S(2)}, u32[]{:S(2)}) %collective-permute-start.15) | collective-permute-done | bytes 786464 | tf_op jit(solution)/shard_map/ppermute | solution.py:116
  75.3 5.1 %fusion.24 = f32[256,1024]{1,0:T(8,128)S(1)} fusion(bf16[3072,1024]{1,0:T(8,128)(2,1)} %constant_dynamic-update-slice_fusion.8, bf16[128,3072]{1,0:T(8,128)(2,1)} %collective-permute-done.15, bf16[128,3072]{1,0:T(8,128)(2,1)} %convert_element_type.359, f32[1024]{0:T(1024)S(1)} %power_multiply_fusion), kind=kOutput, calls=%fused_computation.46 | convolution fusion | flops 1614020608 | bytes 8916992 | tf_op jit(solution)/shard_map/dot_general | solution.py:122
  80.6 0.6 collective-permute-start.16
  81.2 0.7 collective-permute-start.17
  81.9 2.4 %collective-permute-start.18 = (bf16[272,256]{1,0:T(8,128)(2,1)S(1)}, bf16[272,256]{1,0:T(8,128)(2,1)S(1)}, u32[]{:S(2)}, u32[]{:S(2)}) collective-permute-start(bf16[272,256]{1,0:T(8,128)(2,1)S(1)} %pad_maximum_fusion.5), channel_id=1, source_target_pairs={{0,6},{2,4},{4,2},{6,0},{8,14},{10,12},{12,10},{14,8},{16,22},{18,... | collective-permute-start | bytes 417800 | tf_op jit(solution)/shard_map/ppermute | solution.py:37
  84.3 2.9 %collective-permute-done.16 = bf16[272,256]{1,0:T(8,128)(2,1)S(1)} collective-permute-done((bf16[272,256]{1,0:T(8,128)(2,1)S(1)}, bf16[272,256]{1,0:T(8,128)(2,1)S(1)}, u32[]{:S(2)}, u32[]{:S(2)}) %collective-permute-start.16) | collective-permute-done | bytes 139296 | tf_op jit(solution)/shard_map/ppermute | solution.py:37
  87.2 2.5 %collective-permute-done.17 = bf16[272,256]{1,0:T(8,128)(2,1)S(1)} collective-permute-done((bf16[272,256]{1,0:T(8,128)(2,1)S(1)}, bf16[272,256]{1,0:T(8,128)(2,1)S(1)}, u32[]{:S(2)}, u32[]{:S(2)}) %collective-permute-start.17) | collective-permute-done | bytes 139296 | tf_op jit(solution)/shard_map/ppermute | solution.py:37
  90.3 1.7 %collective-permute-start.20 = (bf16[272,64]{1,0:T(8,128)(2,1)S(1)}, bf16[272,64]{1,0:T(8,128)(2,1)S(1)}, u32[]{:S(2)}, u32[]{:S(2)}) collective-permute-start(bf16[272,64]{1,0:T(8,128)(2,1)S(1)} %pad_maximum_fusion.11), channel_id=1, source_target_pairs={{0,16},{2,18},{4,20},{6,22},{8,24},{10,26},{12,28},{14,30},{16,0},... | collective-permute-start | bytes 104456 | tf_op jit(solution)/shard_map/ppermute | solution.py:37
  91.9 2.8 %collective-permute-start.21 = (bf16[272,64]{1,0:T(8,128)(2,1)S(1)}, bf16[272,64]{1,0:T(8,128)(2,1)S(1)}, u32[]{:S(2)}, u32[]{:S(2)}) collective-permute-start(bf16[272,64]{1,0:T(8,128)(2,1)S(1)} %pad_maximum_fusion.12), channel_id=1, source_target_pairs={{0,24},{2,26},{4,28},{6,30},{8,16},{10,18},{12,20},{14,22},{16,8},... | collective-permute-start | bytes 104456 | tf_op jit(solution)/shard_map/ppermute | solution.py:37
  94.8 2.5 %collective-permute-done.20 = bf16[272,64]{1,0:T(8,128)(2,1)S(1)} collective-permute-done((bf16[272,64]{1,0:T(8,128)(2,1)S(1)}, bf16[272,64]{1,0:T(8,128)(2,1)S(1)}, u32[]{:S(2)}, u32[]{:S(2)}) %collective-permute-start.20) | collective-permute-done | bytes 34848 | tf_op jit(solution)/shard_map/ppermute | solution.py:37
  97.4 0.7 collective-permute-done.21
  98.3 1.3 %collective-permute-start.22 = (bf16[272,64]{1,0:T(8,128)(2,1)S(1)}, bf16[272,64]{1,0:T(8,128)(2,1)}, u32[]{:S(2)}, u32[]{:S(2)}) collective-permute-start(bf16[272,64]{1,0:T(8,128)(2,1)S(1)} %pad_maximum_fusion.13), channel_id=1, source_target_pairs={{0,8},{2,10},{4,12},{6,14},{8,0},{10,2},{12,4},{14,6},{16,24},{18,... | collective-permute-start | bytes 104456 | tf_op jit(solution)/shard_map/ppermute | solution.py:51
  99.7 2.1 %collective-permute-start.23 = (bf16[272,64]{1,0:T(8,128)(2,1)S(1)}, bf16[272,64]{1,0:T(8,128)(2,1)S(1)}, u32[]{:S(2)}, u32[]{:S(2)}) collective-permute-start(bf16[272,64]{1,0:T(8,128)(2,1)S(1)} %pad_maximum_fusion.13), channel_id=1, source_target_pairs={{0,16},{2,18},{4,20},{6,22},{8,24},{10,26},{12,28},{14,30},{16,0},... | collective-permute-start | bytes 104456 | tf_op jit(solution)/shard_map/ppermute | solution.py:51
  101.8 1.0 collective-permute-start.24
  102.8 0.3 dynamic_update_slice.56
  103.1 1.4 %dynamic_update_slice.57 = bf16[272,256]{1,0:T(8,128)(2,1)S(1)} dynamic-update-slice(bf16[272,256]{1,0:T(8,128)(2,1)S(1)} %dynamic_update_slice.56, bf16[272,64]{1,0:T(8,128)(2,1)} %collective-permute-done.22, s32[]{:T(128)} %constant.112.clone.1, s32[]{:T(128)S(6)} %select_n.32) | dynamic-update-slice | bytes 69636 | tf_op jit(solution)/shard_map/dynamic_update_slice | solution.py:55
  104.6 1.2 collective-permute-done.23
  105.8 0.3 dynamic_update_slice.58
  106.0 1.9 %collective-permute-done.24 = bf16[272,64]{1,0:T(8,128)(2,1)S(1)} collective-permute-done((bf16[272,64]{1,0:T(8,128)(2,1)S(1)}, bf16[272,64]{1,0:T(8,128)(2,1)S(1)}, u32[]{:S(2)}, u32[]{:S(2)}) %collective-permute-start.24) | collective-permute-done | bytes 34848 | tf_op jit(solution)/shard_map/ppermute | solution.py:51
  107.9 0.5 dynamic_update_slice.59
  108.5 1.5 %collective-permute-start.25 = (bf16[272,256]{1,0:T(8,128)(2,1)S(1)}, bf16[272,256]{1,0:T(8,128)(2,1)S(1)}, u32[]{:S(2)}, u32[]{:S(2)}) collective-permute-start(bf16[272,256]{1,0:T(8,128)(2,1)S(1)} %dynamic_update_slice.59), channel_id=1, source_target_pairs={{0,2},{2,0},{4,6},{6,4},{8,10},{10,8},{12,14},{14,12},{16,18},{18,... | collective-permute-start | bytes 417800 | tf_op jit(solution)/shard_map/ppermute | solution.py:51
  110.0 0.8 collective-permute-start.26
  110.8 1.3 collective-permute-start.27
  112.1 1.5 %collective-permute-done.25 = bf16[272,256]{1,0:T(8,128)(2,1)S(1)} collective-permute-done((bf16[272,256]{1,0:T(8,128)(2,1)S(1)}, bf16[272,256]{1,0:T(8,128)(2,1)S(1)}, u32[]{:S(2)}, u32[]{:S(2)}) %collective-permute-start.25) | collective-permute-done | bytes 139296 | tf_op jit(solution)/shard_map/ppermute | solution.py:51
  113.6 1.5 %collective-permute-done.26 = bf16[272,256]{1,0:T(8,128)(2,1)S(1)} collective-permute-done((bf16[272,256]{1,0:T(8,128)(2,1)S(1)}, bf16[272,256]{1,0:T(8,128)(2,1)S(1)}, u32[]{:S(2)}, u32[]{:S(2)}) %collective-permute-start.26) | collective-permute-done | bytes 139296 | tf_op jit(solution)/shard_map/ppermute | solution.py:51
  115.1 1.6 %collective-permute-done.27 = bf16[272,256]{1,0:T(8,128)(2,1)S(1)} collective-permute-done((bf16[272,256]{1,0:T(8,128)(2,1)S(1)}, bf16[272,256]{1,0:T(8,128)(2,1)S(1)}, u32[]{:S(2)}, u32[]{:S(2)}) %collective-permute-start.27) | collective-permute-done | bytes 139296 | tf_op jit(solution)/shard_map/ppermute | solution.py:51
  116.8 4.7 %convolution_convert_fusion = bf16[256,3072]{1,0:T(8,128)(2,1)S(1)} fusion(bf16[3072,1024]{1,0:T(8,128)(2,1)} %constant_dynamic-update-slice_fusion.8, bf16[272,1024]{1,0:T(8,128)(2,1)S(1)} %constant_dynamic-update-slice_fusion), kind=kOutput, calls=%fused_computation.9 | convolution fusion | flops 1611399168 | bytes 8388608 | tf_op jit(solution)/shard_map/dot_general | solution.py:143
  121.8 0.6 collective-permute-start.28
  122.4 1.5 %collective-permute-done.28 = f32[128]{0:T(128)S(1)} collective-permute-done((f32[128]{0:T(128)S(1)}, f32[128]{0:T(128)S(1)}, u32[]{:S(2)}, u32[]{:S(2)}) %collective-permute-start.28) | collective-permute-done | bytes 544 | tf_op jit(solution)/shard_map/ppermute | solution.py:147
  123.9 2.9 %fusion.16 = (f32[128,3072]{1,0:T(8,128)}, f32[128,3072]{1,0:T(8,128)}) fusion(f32[128,3072]{1,0:T(8,128)S(1)} %get-tuple-element.90, bf16[128,3072]{1,0:T(8,128)(2,1)S(1)} %collective-permute-done.29, bf16[128,3072]{1,0:T(8,128)(2,1)S(1)} %copy-done.4, f32[128,3072]{1,0:T(8,128)S(1)} %copy-done, bf16[256,3072]{1,0:T(8,128)(2,1)S(1)} %convolution_convert_fusion, ...), kind=kLoop, calls=%fused_computation.34 | loop fusion | flops 8650752 | bytes 9454080 | tf_op jit(solution)/shard_map/sub | solution.py:168
  (132 shorter events, 3.7 us)
Async XLA Ops:
  0.6 2.9 %copy-start = (f32[128,3072]{1,0:T(8,128)S(1)}, f32[128,3072]{1,0:T(8,128)}, u32[]{:S(2)}) copy-start(f32[128,3072]{1,0:T(8,128)} %param.19) | copy-start | bytes 4718596
  0.6 2.9 %copy-start.5 = (f32[3072]{0:T(1024)S(1)}, f32[3072]{0:T(1024)}, u32[]{:S(2)}) copy-start(f32[3072]{0:T(1024)} %param.17) | copy-start | bytes 36868
  1.4 2.8 %copy-start.7 = (f32[1024]{0:T(1024)S(1)}, f32[1024]{0:T(1024)}, u32[]{:S(2)}) copy-start(f32[1024]{0:T(1024)} %param.18) | copy-start | bytes 12292
  1.4 2.8 %copy-start.6 = (s32[3072]{0:T(1024)S(1)}, s32[3072]{0:T(1024)}, u32[]{:S(2)}) copy-start(s32[3072]{0:T(1024)} %param.15) | copy-start | bytes 36868
  3.0 2.5 %collective-permute-start = (bf16[128,3072]{1,0:T(8,128)(2,1)S(1)}, bf16[128,3072]{1,0:T(8,128)(2,1)S(1)}, u32[]{:S(2)}, u32[]{:S(2)}) collective-permute-start(bf16[128,3072]{1,0:T(8,128)(2,1)S(1)} %select_convert_fusion), channel_id=1, source_target_pairs={{0,1},{1,0},{2,3},{3,2},{4,5},{5,4},{6,7},{7,6},{8,9},{9,8},{10,11... | collective-permute-start | bytes 2359304 | tf_op jit(solution)/shard_map/ppermute | solution.py:116
  4.3 6.3 %copy-start.10 = (bf16[2048,1024]{1,0:T(8,128)(2,1)S(1)}, bf16[2048,1024]{1,0:T(8,128)(2,1)}, u32[]{:S(2)}) copy-start(bf16[2048,1024]{1,0:T(8,128)(2,1)} %param.14) | copy-start | bytes 12582916
  13.3 11.8 %collective-permute-start.1 = (bf16[272,256]{1,0:T(8,128)(2,1)S(1)}, bf16[272,256]{1,0:T(8,128)(2,1)S(1)}, u32[]{:S(2)}, u32[]{:S(2)}) collective-permute-start(bf16[272,256]{1,0:T(8,128)(2,1)S(1)} %pad_maximum_fusion), channel_id=1, source_target_pairs={{0,2},{2,0},{4,6},{6,4},{8,10},{10,8},{12,14},{14,12},{16,18},{18,... | collective-permute-start | bytes 417800 | tf_op jit(solution)/shard_map/ppermute | solution.py:37
  16.3 8.9 %collective-permute-start.2 = (bf16[272,256]{1,0:T(8,128)(2,1)S(1)}, bf16[272,256]{1,0:T(8,128)(2,1)S(1)}, u32[]{:S(2)}, u32[]{:S(2)}) collective-permute-start(bf16[272,256]{1,0:T(8,128)(2,1)S(1)} %pad_maximum_fusion.1), channel_id=1, source_target_pairs={{0,4},{2,6},{4,0},{6,2},{8,12},{10,14},{12,8},{14,10},{16,20},{18,... | collective-permute-start | bytes 417800 | tf_op jit(solution)/shard_map/ppermute | solution.py:37
  17.9 7.3 %collective-permute-start.3 = (bf16[272,256]{1,0:T(8,128)(2,1)S(1)}, bf16[272,256]{1,0:T(8,128)(2,1)S(1)}, u32[]{:S(2)}, u32[]{:S(2)}) collective-permute-start(bf16[272,256]{1,0:T(8,128)(2,1)S(1)} %pad_maximum_fusion.2), channel_id=1, source_target_pairs={{0,6},{2,4},{4,2},{6,0},{8,14},{10,12},{12,10},{14,8},{16,22},{18,... | collective-permute-start | bytes 417800 | tf_op jit(solution)/shard_map/ppermute | solution.py:37
  25.6 13.4 %collective-permute-start.4 = (bf16[272,64]{1,0:T(8,128)(2,1)S(1)}, bf16[272,64]{1,0:T(8,128)(2,1)S(1)}, u32[]{:S(2)}, u32[]{:S(2)}) collective-permute-start(bf16[272,64]{1,0:T(8,128)(2,1)S(1)} %pad_maximum_fusion.6), channel_id=1, source_target_pairs={{0,8},{2,10},{4,12},{6,14},{8,0},{10,2},{12,4},{14,6},{16,24},{18,... | collective-permute-start | bytes 104456 | tf_op jit(solution)/shard_map/ppermute | solution.py:37
  27.7 11.3 %collective-permute-start.5 = (bf16[272,64]{1,0:T(8,128)(2,1)S(1)}, bf16[272,64]{1,0:T(8,128)(2,1)S(1)}, u32[]{:S(2)}, u32[]{:S(2)}) collective-permute-start(bf16[272,64]{1,0:T(8,128)(2,1)S(1)} %pad_maximum_fusion.7), channel_id=1, source_target_pairs={{0,16},{2,18},{4,20},{6,22},{8,24},{10,26},{12,28},{14,30},{16,0},... | collective-permute-start | bytes 104456 | tf_op jit(solution)/shard_map/ppermute | solution.py:37
  30.4 8.7 %collective-permute-start.6 = (bf16[272,64]{1,0:T(8,128)(2,1)S(1)}, bf16[272,64]{1,0:T(8,128)(2,1)S(1)}, u32[]{:S(2)}, u32[]{:S(2)}) collective-permute-start(bf16[272,64]{1,0:T(8,128)(2,1)S(1)} %pad_maximum_fusion.8), channel_id=1, source_target_pairs={{0,24},{2,26},{4,28},{6,30},{8,16},{10,18},{12,20},{14,22},{16,8},... | collective-permute-start | bytes 104456 | tf_op jit(solution)/shard_map/ppermute | solution.py:37
  39.3 6.8 %collective-permute-start.7 = (bf16[272,64]{1,0:T(8,128)(2,1)S(1)}, bf16[272,64]{1,0:T(8,128)(2,1)S(1)}, u32[]{:S(2)}, u32[]{:S(2)}) collective-permute-start(bf16[272,64]{1,0:T(8,128)(2,1)S(1)} %pad_maximum_fusion.9), channel_id=1, source_target_pairs={{0,8},{2,10},{4,12},{6,14},{8,0},{10,2},{12,4},{14,6},{16,24},{18,... | collective-permute-start | bytes 104456 | tf_op jit(solution)/shard_map/ppermute | solution.py:51
  40.1 7.3 %collective-permute-start.8 = (bf16[272,64]{1,0:T(8,128)(2,1)S(1)}, bf16[272,64]{1,0:T(8,128)(2,1)S(1)}, u32[]{:S(2)}, u32[]{:S(2)}) collective-permute-start(bf16[272,64]{1,0:T(8,128)(2,1)S(1)} %pad_maximum_fusion.9), channel_id=1, source_target_pairs={{0,16},{2,18},{4,20},{6,22},{8,24},{10,26},{12,28},{14,30},{16,0},... | collective-permute-start | bytes 104456 | tf_op jit(solution)/shard_map/ppermute | solution.py:51
  43.6 6.1 %collective-permute-start.9 = (bf16[272,64]{1,0:T(8,128)(2,1)S(1)}, bf16[272,64]{1,0:T(8,128)(2,1)S(1)}, u32[]{:S(2)}, u32[]{:S(2)}) collective-permute-start(bf16[272,64]{1,0:T(8,128)(2,1)S(1)} %pad_maximum_fusion.9), channel_id=1, source_target_pairs={{0,24},{2,26},{4,28},{6,30},{8,16},{10,18},{12,20},{14,22},{16,8},... | collective-permute-start | bytes 104456 | tf_op jit(solution)/shard_map/ppermute | solution.py:51
  50.2 7.5 %collective-permute-start.10 = (bf16[272,256]{1,0:T(8,128)(2,1)S(1)}, bf16[272,256]{1,0:T(8,128)(2,1)S(1)}, u32[]{:S(2)}, u32[]{:S(2)}) collective-permute-start(bf16[272,256]{1,0:T(8,128)(2,1)S(1)} %dynamic_update_slice.51), channel_id=1, source_target_pairs={{0,2},{2,0},{4,6},{6,4},{8,10},{10,8},{12,14},{14,12},{16,18},{18,... | collective-permute-start | bytes 417800 | tf_op jit(solution)/shard_map/ppermute | solution.py:51
  55.7 5.1 %collective-permute-start.11 = (bf16[272,256]{1,0:T(8,128)(2,1)S(1)}, bf16[272,256]{1,0:T(8,128)(2,1)S(1)}, u32[]{:S(2)}, u32[]{:S(2)}) collective-permute-start(bf16[272,256]{1,0:T(8,128)(2,1)S(1)} %dynamic_update_slice.51), channel_id=1, source_target_pairs={{0,4},{2,6},{4,0},{6,2},{8,12},{10,14},{12,8},{14,10},{16,20},{18,... | collective-permute-start | bytes 417800 | tf_op jit(solution)/shard_map/ppermute | solution.py:51
  57.2 6.0 %collective-permute-start.12 = (bf16[272,256]{1,0:T(8,128)(2,1)S(1)}, bf16[272,256]{1,0:T(8,128)(2,1)S(1)}, u32[]{:S(2)}, u32[]{:S(2)}) collective-permute-start(bf16[272,256]{1,0:T(8,128)(2,1)S(1)} %dynamic_update_slice.51), channel_id=1, source_target_pairs={{0,6},{2,4},{4,2},{6,0},{8,14},{10,12},{12,10},{14,8},{16,22},{18,... | collective-permute-start | bytes 417800 | tf_op jit(solution)/shard_map/ppermute | solution.py:51
  67.8 3.9 %copy-start.1 = (bf16[256,3072]{1,0:T(8,128)(2,1)}, bf16[256,3072]{1,0:T(8,128)(2,1)S(1)}, u32[]{:S(2)}) copy-start(bf16[256,3072]{1,0:T(8,128)(2,1)S(1)} %convolution_convert_fusion.1) | copy-start | bytes 4718596
  67.9 2.9 %collective-permute-start.14 = (bf16[128,3072]{1,0:T(8,128)(2,1)S(1)}, bf16[128,3072]{1,0:T(8,128)(2,1)S(1)}, u32[]{:S(2)}, u32[]{:S(2)}) collective-permute-start(bf16[128,3072]{1,0:T(8,128)(2,1)S(1)} %slice.442), channel_id=1, source_target_pairs={{0,1},{1,0},{2,3},{3,2},{4,5},{5,4},{6,7},{7,6},{8,9},{9,8},{10,11... | collective-permute-start | bytes 2359304 | tf_op jit(solution)/shard_map/ppermute | solution.py:148
  68.2 2.0 %collective-permute-start.13 = (f32[128]{0:T(128)S(1)}, f32[128]{0:T(128)S(1)}, u32[]{:S(2)}, u32[]{:S(2)}) collective-permute-start(f32[128]{0:T(128)S(1)} %slice.382), channel_id=1, source_target_pairs={{0,1},{1,0},{2,3},{3,2},{4,5},{5,4},{6,7},{7,6},{8,9},{9,8},{10,11... | collective-permute-start | bytes 1544 | tf_op jit(solution)/shard_map/ppermute | solution.py:147
  70.2 0.6 copy-start.8
  70.8 0.9 copy-start.3
  72.7 2.6 %collective-permute-start.15 = (bf16[128,3072]{1,0:T(8,128)(2,1)}, bf16[128,3072]{1,0:T(8,128)(2,1)}, u32[]{:S(2)}, u32[]{:S(2)}) collective-permute-start(bf16[128,3072]{1,0:T(8,128)(2,1)} %convert_element_type.359), channel_id=1, source_target_pairs={{0,1},{1,0},{2,3},{3,2},{4,5},{5,4},{6,7},{7,6},{8,9},{9,8},{10,11... | collective-permute-start | bytes 2359304 | tf_op jit(solution)/shard_map/ppermute | solution.py:116
  80.6 6.6 %collective-permute-start.16 = (bf16[272,256]{1,0:T(8,128)(2,1)S(1)}, bf16[272,256]{1,0:T(8,128)(2,1)S(1)}, u32[]{:S(2)}, u32[]{:S(2)}) collective-permute-start(bf16[272,256]{1,0:T(8,128)(2,1)S(1)} %pad_maximum_fusion.3), channel_id=1, source_target_pairs={{0,2},{2,0},{4,6},{6,4},{8,10},{10,8},{12,14},{14,12},{16,18},{18,... | collective-permute-start | bytes 417800 | tf_op jit(solution)/shard_map/ppermute | solution.py:37
  81.2 8.5 %collective-permute-start.17 = (bf16[272,256]{1,0:T(8,128)(2,1)S(1)}, bf16[272,256]{1,0:T(8,128)(2,1)S(1)}, u32[]{:S(2)}, u32[]{:S(2)}) collective-permute-start(bf16[272,256]{1,0:T(8,128)(2,1)S(1)} %pad_maximum_fusion.4), channel_id=1, source_target_pairs={{0,4},{2,6},{4,0},{6,2},{8,12},{10,14},{12,8},{14,10},{16,20},{18,... | collective-permute-start | bytes 417800 | tf_op jit(solution)/shard_map/ppermute | solution.py:37
  81.9 7.8 %collective-permute-start.18 = (bf16[272,256]{1,0:T(8,128)(2,1)S(1)}, bf16[272,256]{1,0:T(8,128)(2,1)S(1)}, u32[]{:S(2)}, u32[]{:S(2)}) collective-permute-start(bf16[272,256]{1,0:T(8,128)(2,1)S(1)} %pad_maximum_fusion.5), channel_id=1, source_target_pairs={{0,6},{2,4},{4,2},{6,0},{8,14},{10,12},{12,10},{14,8},{16,22},{18,... | collective-permute-start | bytes 417800 | tf_op jit(solution)/shard_map/ppermute | solution.py:37
  90.2 4.6 %collective-permute-start.19 = (bf16[272,64]{1,0:T(8,128)(2,1)S(1)}, bf16[272,64]{1,0:T(8,128)(2,1)S(1)}, u32[]{:S(2)}, u32[]{:S(2)}) collective-permute-start(bf16[272,64]{1,0:T(8,128)(2,1)S(1)} %pad_maximum_fusion.10), channel_id=1, source_target_pairs={{0,8},{2,10},{4,12},{6,14},{8,0},{10,2},{12,4},{14,6},{16,24},{18,... | collective-permute-start | bytes 104456 | tf_op jit(solution)/shard_map/ppermute | solution.py:37
  90.3 7.1 %collective-permute-start.20 = (bf16[272,64]{1,0:T(8,128)(2,1)S(1)}, bf16[272,64]{1,0:T(8,128)(2,1)S(1)}, u32[]{:S(2)}, u32[]{:S(2)}) collective-permute-start(bf16[272,64]{1,0:T(8,128)(2,1)S(1)} %pad_maximum_fusion.11), channel_id=1, source_target_pairs={{0,16},{2,18},{4,20},{6,22},{8,24},{10,26},{12,28},{14,30},{16,0},... | collective-permute-start | bytes 104456 | tf_op jit(solution)/shard_map/ppermute | solution.py:37
  91.9 6.2 %collective-permute-start.21 = (bf16[272,64]{1,0:T(8,128)(2,1)S(1)}, bf16[272,64]{1,0:T(8,128)(2,1)S(1)}, u32[]{:S(2)}, u32[]{:S(2)}) collective-permute-start(bf16[272,64]{1,0:T(8,128)(2,1)S(1)} %pad_maximum_fusion.12), channel_id=1, source_target_pairs={{0,24},{2,26},{4,28},{6,30},{8,16},{10,18},{12,20},{14,22},{16,8},... | collective-permute-start | bytes 104456 | tf_op jit(solution)/shard_map/ppermute | solution.py:37
  98.3 4.8 %collective-permute-start.22 = (bf16[272,64]{1,0:T(8,128)(2,1)S(1)}, bf16[272,64]{1,0:T(8,128)(2,1)}, u32[]{:S(2)}, u32[]{:S(2)}) collective-permute-start(bf16[272,64]{1,0:T(8,128)(2,1)S(1)} %pad_maximum_fusion.13), channel_id=1, source_target_pairs={{0,8},{2,10},{4,12},{6,14},{8,0},{10,2},{12,4},{14,6},{16,24},{18,... | collective-permute-start | bytes 104456 | tf_op jit(solution)/shard_map/ppermute | solution.py:51
  99.7 6.1 %collective-permute-start.23 = (bf16[272,64]{1,0:T(8,128)(2,1)S(1)}, bf16[272,64]{1,0:T(8,128)(2,1)S(1)}, u32[]{:S(2)}, u32[]{:S(2)}) collective-permute-start(bf16[272,64]{1,0:T(8,128)(2,1)S(1)} %pad_maximum_fusion.13), channel_id=1, source_target_pairs={{0,16},{2,18},{4,20},{6,22},{8,24},{10,26},{12,28},{14,30},{16,0},... | collective-permute-start | bytes 104456 | tf_op jit(solution)/shard_map/ppermute | solution.py:51
  101.8 6.1 %collective-permute-start.24 = (bf16[272,64]{1,0:T(8,128)(2,1)S(1)}, bf16[272,64]{1,0:T(8,128)(2,1)S(1)}, u32[]{:S(2)}, u32[]{:S(2)}) collective-permute-start(bf16[272,64]{1,0:T(8,128)(2,1)S(1)} %pad_maximum_fusion.13), channel_id=1, source_target_pairs={{0,24},{2,26},{4,28},{6,30},{8,16},{10,18},{12,20},{14,22},{16,8},... | collective-permute-start | bytes 104456 | tf_op jit(solution)/shard_map/ppermute | solution.py:51
  108.5 5.1 %collective-permute-start.25 = (bf16[272,256]{1,0:T(8,128)(2,1)S(1)}, bf16[272,256]{1,0:T(8,128)(2,1)S(1)}, u32[]{:S(2)}, u32[]{:S(2)}) collective-permute-start(bf16[272,256]{1,0:T(8,128)(2,1)S(1)} %dynamic_update_slice.59), channel_id=1, source_target_pairs={{0,2},{2,0},{4,6},{6,4},{8,10},{10,8},{12,14},{14,12},{16,18},{18,... | collective-permute-start | bytes 417800 | tf_op jit(solution)/shard_map/ppermute | solution.py:51
  110.0 5.1 %collective-permute-start.26 = (bf16[272,256]{1,0:T(8,128)(2,1)S(1)}, bf16[272,256]{1,0:T(8,128)(2,1)S(1)}, u32[]{:S(2)}, u32[]{:S(2)}) collective-permute-start(bf16[272,256]{1,0:T(8,128)(2,1)S(1)} %dynamic_update_slice.59), channel_id=1, source_target_pairs={{0,4},{2,6},{4,0},{6,2},{8,12},{10,14},{12,8},{14,10},{16,20},{18,... | collective-permute-start | bytes 417800 | tf_op jit(solution)/shard_map/ppermute | solution.py:51
  110.8 6.0 %collective-permute-start.27 = (bf16[272,256]{1,0:T(8,128)(2,1)S(1)}, bf16[272,256]{1,0:T(8,128)(2,1)S(1)}, u32[]{:S(2)}, u32[]{:S(2)}) collective-permute-start(bf16[272,256]{1,0:T(8,128)(2,1)S(1)} %dynamic_update_slice.59), channel_id=1, source_target_pairs={{0,6},{2,4},{4,2},{6,0},{8,14},{10,12},{12,10},{14,8},{16,22},{18,... | collective-permute-start | bytes 417800 | tf_op jit(solution)/shard_map/ppermute | solution.py:51
  116.7 7.2 %copy-start.4 = (bf16[128,3072]{1,0:T(8,128)(2,1)S(1)}, bf16[128,3072]{1,0:T(8,128)(2,1)}, u32[]{:S(2)}) copy-start(bf16[128,3072]{1,0:T(8,128)(2,1)} %copy-done.3) | copy-start | bytes 2359300
  121.4 2.4 %copy-start.9 = (f32[128]{0:T(128)S(1)}, f32[128]{0:T(128)}, u32[]{:S(2)}) copy-start(f32[128]{0:T(128)} %copy-done.8) | copy-start | bytes 1540
  121.5 2.5 %copy-start.2 = (bf16[256,3072]{1,0:T(8,128)(2,1)S(1)}, bf16[256,3072]{1,0:T(8,128)(2,1)}, u32[]{:S(2)}) copy-start(bf16[256,3072]{1,0:T(8,128)(2,1)} %copy-done.1) | copy-start | bytes 4718596
  121.5 2.4 %collective-permute-start.29 = (bf16[128,3072]{1,0:T(8,128)(2,1)S(1)}, bf16[128,3072]{1,0:T(8,128)(2,1)S(1)}, u32[]{:S(2)}, u32[]{:S(2)}) collective-permute-start(bf16[128,3072]{1,0:T(8,128)(2,1)S(1)} %slice.475), channel_id=1, source_target_pairs={{0,1},{1,0},{2,3},{3,2},{4,5},{5,4},{6,7},{7,6},{8,9},{9,8},{10,11... | collective-permute-start | bytes 2359304 | tf_op jit(solution)/shard_map/ppermute | solution.py:148
  121.8 2.0 %collective-permute-start.28 = (f32[128]{0:T(128)S(1)}, f32[128]{0:T(128)S(1)}, u32[]{:S(2)}, u32[]{:S(2)}) collective-permute-start(f32[128]{0:T(128)S(1)} %slice.423), channel_id=1, source_target_pairs={{0,1},{1,0},{2,3},{3,2},{4,5},{5,4},{6,7},{7,6},{8,9},{9,8},{10,11... | collective-permute-start | bytes 1544 | tf_op jit(solution)/shard_map/ppermute | solution.py:147
where the time goes:
time: 127 us
  matrix products  37.6 us (30%)
  starting transfers between devices  35.6 us (28%)
  waiting for transfers between devices  30.5 us (24%)
  local copies, waits for them, and re-layouts  12.2 us (10%)
  other arithmetic  8.73 us (7%)
  between operations  2.28 us (2%)
    ppermute x12, starting transfers between devices, vert_sum(): lax.ppermute(send, 'vert', [(i, i ^ masks[t + 1]) for i in range(n_vert)])  17.6 us
    ppermute x12, starting transfers between devices, vert_sum(): lax.ppermute(cur, 'vert', [(i, i ^ masks[t]) for i in range(n_vert)])  16 us
    dot_general x2, matrix products, work(): jnp.dot(rows, eig_table, preferred_element_type=jnp.float32)  15.8 us
    ppermute x12, waiting for transfers between devices, vert_sum(): lax.ppermute(cur, 'vert', [(i, i ^ masks[t]) for i in range(n_vert)])  15.7 us
    dot_general x2, matrix products, operate(): lax.dot_general(weights, features, (((1,), (1,)), ((), ())), preferred_el...  9.3 us
    ppermute x12, waiting for transfers between devices, vert_sum(): lax.ppermute(send, 'vert', [(i, i ^ masks[t + 1]) for i in range(n_vert)])  8.65 us
    dot_general x1, matrix products, coeff_from_table(): summed = jnp.dot(rows, picker, preferred_element_type=jnp.float32)  5.09 us
    dot_general x1, matrix products, operate(): coeff = jnp.dot(rows, built[0], preferred_element_type=jnp.float32)  5.07 us
  transfers between devices with their start and end apart: 30, of which 17 were waited for; matrix products, arithmetic and copies ran while one was open for 21% of the time, Pallas kernels for 0%

commit v1 on v0

--- a/solution.py
+++ b/solution.py
@@ -4,7 +4,7 @@
 from jax.sharding import PartitionSpec as P
 
 ITERS = 2
-PIECES = 2
+PIECES = 3
 
 
 def vert_sum(x, n_vert, finish, encode, decode, side=()):

time: 127 us -> 124 us (0.976)
  waiting for transfers between devices: 30.5 us -> 26.9 us
    ppermute x12, waiting for transfers between devices: 15.7 us -> 6.46 us  [vert_sum(): lax.ppermute(cur, 'vert', [(i, i ^ masks[t]) for i in range(n_vert)])]
    ppermute x12, waiting for transfers between devices: 8.65 us -> 14.3 us  [vert_sum(): lax.ppermute(send, 'vert', [(i, i ^ masks[t + 1]) for i in range(n_vert)])]
    unnamed x23 -> x26, local copies, waits for them, and re-layouts: 2.57 us -> 3.57 us
    dot_general x2 -> x3, matrix products: 15.8 us -> 16 us  [work(): jnp.dot(rows, eig_table, preferred_element_type=jnp.float32)]
  transfers between devices with their start and end apart: 30 -> 30, of which waited for: 17 -> 15; matrix products, arithmetic and copies ran while one was open for 21% -> 19% of each run, Pallas kernels for 0% -> 0%
where the time goes in v1:
time: 124 us
  matrix products  37.8 us (30%)
  starting transfers between devices  35.4 us (29%)
  waiting for transfers between devices  26.9 us (22%)
  local copies, waits for them, and re-layouts  12.5 us (10%)
  other arithmetic  8.79 us (7%)
  between operations  2.33 us (2%)
    ppermute x12, starting transfers between devices, vert_sum(): lax.ppermute(send, 'vert', [(i, i ^ masks[t + 1]) for i in range(n_vert)])  17.4 us
    ppermute x12, starting transfers between devices, vert_sum(): lax.ppermute(cur, 'vert', [(i, i ^ masks[t]) for i in range(n_vert)])  16 us
    dot_general x3, matrix products, work(): jnp.dot(rows, eig_table, preferred_element_type=jnp.float32)  16 us
    ppermute x12, waiting for transfers between devices, vert_sum(): lax.ppermute(send, 'vert', [(i, i ^ masks[t + 1]) for i in range(n_vert)])  14.3 us
    dot_general x2, matrix products, operate(): lax.dot_general(weights, features, (((1,), (1,)), ((), ())), preferred_el...  9.3 us
    ppermute x12, waiting for transfers between devices, vert_sum(): lax.ppermute(cur, 'vert', [(i, i ^ masks[t]) for i in range(n_vert)])  6.46 us
    dot_general x1, matrix products, coeff_from_table(): summed = jnp.dot(rows, picker, preferred_element_type=jnp.float32)  5.09 us
    dot_general x1, matrix products, operate(): coeff = jnp.dot(rows, built[0], preferred_element_type=jnp.float32)  5.07 us
  transfers between devices with their start and end apart: 30, of which 15 were waited for; matrix products, arithmetic and copies ran while one was open for 19% of the time, Pallas kernels for 0%

profile of v1, /device:TPU:0, one launch (start us, length us, event | category | flops | bytes accessed | tf_op | source)
XLA Modules:
  0.0 123.7 jit_solution(4901078264650660585)
XLA Ops:
  1.5 1.5 %select_convert_fusion = bf16[128,3072]{1,0:T(8,128)(2,1)S(1)} fusion(f32[128,3072]{1,0:T(8,128)} %param.19, pred[3072]{0:T(1024)(128)(4,1)S(1)} %iota_compare_fusion.14), kind=kLoop, calls=%fused_computation.51 | loop fusion | flops 393216 | bytes 2362368 | tf_op jit(solution)/shard_map/convert_element_type | solution.py:114
  3.0 0.6 collective-permute-start
  3.6 0.4 fusion.15
  4.0 0.2 scatter.15
  4.3 1.1 collective-permute-done
  5.5 5.1 %subtract_convert_fusion = (bf16[256,2048]{1,0:T(8,128)(2,1)S(1)}, bf16[256,2048]{1,0:T(8,128)(2,1)S(1)}) fusion(s32[3072]{0:T(1024)S(1)} %copy-done.7, bf16[128,3072]{1,0:T(8,128)(2,1)S(1)} %collective-permute-done, bf16[128,3072]{1,0:T(8,128)(2,1)S(1)} %select_convert_fusion), kind=kOutput, calls=%fused_computation.30 | convolution fusion | flops 3232759808 | bytes 3682304 | tf_op jit(solution)/shard_map/dot_general | solution.py:86
  10.6 2.4 %fusion.8 = f32[512,1024]{1,0:T(8,128)S(1)} fusion(bf16[2048,1024]{1,0:T(8,128)(2,1)S(1)} %copy-done.11, bf16[256,2048]{1,0:T(8,128)(2,1)S(1)} %get-tuple-element.115, bf16[256,2048]{1,0:T(8,128)(2,1)S(1)} %get-tuple-element.116), kind=kOutput, calls=%fused_computation.26 | convolution fusion | flops 2151677952 | bytes 8388608 | tf_op jit(solution)/shard_map/dot_general | solution.py:89
  13.4 2.9 %collective-permute-start.1 = (bf16[272,256]{1,0:T(8,128)(2,1)S(1)}, bf16[272,256]{1,0:T(8,128)(2,1)S(1)}, u32[]{:S(2)}, u32[]{:S(2)}) collective-permute-start(bf16[272,256]{1,0:T(8,128)(2,1)S(1)} %pad_maximum_fusion), channel_id=1, source_target_pairs={{0,2},{2,0},{4,6},{6,4},{8,10},{10,8},{12,14},{14,12},{16,18},{18,... | collective-permute-start | bytes 417800 | tf_op jit(solution)/shard_map/ppermute | solution.py:37
  16.3 1.6 %collective-permute-start.2 = (bf16[272,256]{1,0:T(8,128)(2,1)S(1)}, bf16[272,256]{1,0:T(8,128)(2,1)S(1)}, u32[]{:S(2)}, u32[]{:S(2)}) collective-permute-start(bf16[272,256]{1,0:T(8,128)(2,1)S(1)} %pad_maximum_fusion.1), channel_id=1, source_target_pairs={{0,4},{2,6},{4,0},{6,2},{8,12},{10,14},{12,8},{14,10},{16,20},{18,... | collective-permute-start | bytes 417800 | tf_op jit(solution)/shard_map/ppermute | solution.py:37
  18.0 5.0 %fusion.14 = bf16[1024,1024]{1,0:T(8,128)(2,1)S(1)} fusion(bf16[2048,1024]{1,0:T(8,128)(2,1)S(1)} %copy-done.11, s32[1024]{0:T(1024)S(1)} %get-tuple-element.65), kind=kOutput, calls=%fused_computation.33 | convolution fusion | flops 4298113024 | bytes 6295552 | tf_op jit(solution)/shard_map/dot_general | solution.py:79
  23.0 1.8 %collective-permute-done.2 = bf16[272,256]{1,0:T(8,128)(2,1)S(1)} collective-permute-done((bf16[272,256]{1,0:T(8,128)(2,1)S(1)}, bf16[272,256]{1,0:T(8,128)(2,1)S(1)}, u32[]{:S(2)}, u32[]{:S(2)}) %collective-permute-start.2) | collective-permute-done | bytes 139296 | tf_op jit(solution)/shard_map/ppermute | solution.py:37
  25.2 1.6 %collective-permute-start.4 = (bf16[272,64]{1,0:T(8,128)(2,1)S(1)}, bf16[272,64]{1,0:T(8,128)(2,1)S(1)}, u32[]{:S(2)}, u32[]{:S(2)}) collective-permute-start(bf16[272,64]{1,0:T(8,128)(2,1)S(1)} %pad_maximum_fusion.6), channel_id=1, source_target_pairs={{0,8},{2,10},{4,12},{6,14},{8,0},{10,2},{12,4},{14,6},{16,24},{18,... | collective-permute-start | bytes 104456 | tf_op jit(solution)/shard_map/ppermute | solution.py:37
  26.9 2.7 %collective-permute-start.5 = (bf16[272,64]{1,0:T(8,128)(2,1)S(1)}, bf16[272,64]{1,0:T(8,128)(2,1)S(1)}, u32[]{:S(2)}, u32[]{:S(2)}) collective-permute-start(bf16[272,64]{1,0:T(8,128)(2,1)S(1)} %pad_maximum_fusion.7), channel_id=1, source_target_pairs={{0,16},{2,18},{4,20},{6,22},{8,24},{10,26},{12,28},{14,30},{16,0},... | collective-permute-start | bytes 104456 | tf_op jit(solution)/shard_map/ppermute | solution.py:37
  29.6 0.3 collective-permute-start.6
  29.9 5.0 %fusion.13 = bf16[1024,1024]{1,0:T(8,128)(2,1)S(1)} fusion(bf16[2048,1024]{1,0:T(8,128)(2,1)S(1)} %copy-done.11, s32[1024]{0:T(1024)S(1)} %get-tuple-element.69), kind=kOutput, calls=%fused_computation.32 | convolution fusion | flops 4298113024 | bytes 6295552 | tf_op jit(solution)/shard_map/dot_general | solution.py:79
  35.0 0.7 collective-permute-done.6
  36.1 3.5 %collective-permute-start.8 = (bf16[272,64]{1,0:T(8,128)(2,1)S(1)}, bf16[272,64]{1,0:T(8,128)(2,1)S(1)}, u32[]{:S(2)}, u32[]{:S(2)}) collective-permute-start(bf16[272,64]{1,0:T(8,128)(2,1)S(1)} %pad_maximum_fusion.9), channel_id=1, source_target_pairs={{0,16},{2,18},{4,20},{6,22},{8,24},{10,26},{12,28},{14,30},{16,0},... | collective-permute-start | bytes 104456 | tf_op jit(solution)/shard_map/ppermute | solution.py:51
  39.6 0.9 collective-permute-start.9
  40.5 6.0 %fusion.12 = bf16[1024,1024]{1,0:T(8,128)(2,1)} fusion(bf16[2048,1024]{1,0:T(8,128)(2,1)S(1)} %copy-done.11, s32[1024]{0:T(1024)S(1)} %get-tuple-element.73), kind=kOutput, calls=%fused_computation.31 | convolution fusion | flops 4298113024 | bytes 6295552 | tf_op jit(solution)/shard_map/dot_general | solution.py:79
  46.6 2.7 %copy-done.5 = bf16[3072,1024]{1,0:T(8,128)(2,1)} copy-done((bf16[3072,1024]{1,0:T(8,128)(2,1)}, bf16[3072,1024]{1,0:T(8,128)(2,1)S(1)}, u32[]{:S(2)}) %copy-start.5) | copy-done | bytes 6291480
  49.3 0.3 dynamic_update_slice.48
  49.7 0.6 dynamic_update_slice.49
  50.4 0.3 dynamic_update_slice.50
  50.7 0.6 dynamic_update_slice.51
  51.2 1.2 collective-permute-start.10
  52.5 0.9 collective-permute-start.11
  53.4 1.4 %collective-permute-start.12 = (bf16[272,256]{1,0:T(8,128)(2,1)S(1)}, bf16[272,256]{1,0:T(8,128)(2,1)S(1)}, u32[]{:S(2)}, u32[]{:S(2)}) collective-permute-start(bf16[272,256]{1,0:T(8,128)(2,1)S(1)} %dynamic_update_slice.51), channel_id=1, source_target_pairs={{0,6},{2,4},{4,2},{6,0},{8,14},{10,12},{12,10},{14,8},{16,22},{18,... | collective-permute-start | bytes 417800 | tf_op jit(solution)/shard_map/ppermute | solution.py:51
  54.8 3.1 %constant_dynamic-update-slice_fusion = bf16[3072,1024]{1,0:T(8,128)(2,1)} fusion(bf16[3072,1024]{1,0:T(8,128)(2,1)} %copy-done.5, bf16[1024,1024]{1,0:T(8,128)(2,1)} %fusion.12), kind=kLoop, calls=%fused_computation.131 | loop fusion | bytes 4194304 | tf_op jit(solution)/shard_map/concatenate | solution.py:135
  58.1 1.2 %collective-permute-done.12 = bf16[272,256]{1,0:T(8,128)(2,1)S(1)} collective-permute-done((bf16[272,256]{1,0:T(8,128)(2,1)S(1)}, bf16[272,256]{1,0:T(8,128)(2,1)S(1)}, u32[]{:S(2)}, u32[]{:S(2)}) %collective-permute-start.12) | collective-permute-done | bytes 139296 | tf_op jit(solution)/shard_map/ppermute | solution.py:51
  59.4 4.6 %convolution_convert_fusion.1 = bf16[256,3072]{1,0:T(8,128)(2,1)S(1)} fusion(bf16[3072,1024]{1,0:T(8,128)(2,1)} %constant_dynamic-update-slice_fusion, bf16[272,1024]{1,0:T(8,128)(2,1)S(1)} %constant_dynamic-update-slice_fusion.7), kind=kOutput, calls=%fused_computation.13 | convolution fusion | flops 1611399168 | bytes 8388608 | tf_op jit(solution)/shard_map/dot_general | solution.py:143
  64.4 0.6 collective-permute-start.13
  64.9 1.5 %collective-permute-done.13 = f32[128]{0:T(128)S(1)} collective-permute-done((f32[128]{0:T(128)S(1)}, f32[128]{0:T(128)S(1)}, u32[]{:S(2)}, u32[]{:S(2)}) %collective-permute-start.13) | collective-permute-done | bytes 544 | tf_op jit(solution)/shard_map/ppermute | solution.py:147
  66.4 0.5 copy-done.9
  66.9 0.9 fusion.16
  67.9 1.0 convert_element_type.364
  69.0 0.4 scatter.19
  69.4 2.1 %collective-permute-done.15 = bf16[128,3072]{1,0:T(8,128)(2,1)} collective-permute-done((bf16[128,3072]{1,0:T(8,128)(2,1)}, bf16[128,3072]{1,0:T(8,128)(2,1)}, u32[]{:S(2)}, u32[]{:S(2)}) %collective-permute-start.15) | collective-permute-done | bytes 786464 | tf_op jit(solution)/shard_map/ppermute | solution.py:116
  71.5 5.1 %fusion.27 = f32[256,1024]{1,0:T(8,128)S(1)} fusion(bf16[3072,1024]{1,0:T(8,128)(2,1)} %constant_dynamic-update-slice_fusion, bf16[128,3072]{1,0:T(8,128)(2,1)} %collective-permute-done.15, bf16[128,3072]{1,0:T(8,128)(2,1)} %convert_element_type.364, f32[1024]{0:T(1024)S(1)} %power_multiply_fusion), kind=kOutput, calls=%fused_computation.50 | convolution fusion | flops 1614020608 | bytes 8916992 | tf_op jit(solution)/shard_map/dot_general | solution.py:122
  76.7 1.5 %collective-permute-start.16 = (bf16[272,256]{1,0:T(8,128)(2,1)S(1)}, bf16[272,256]{1,0:T(8,128)(2,1)S(1)}, u32[]{:S(2)}, u32[]{:S(2)}) collective-permute-start(bf16[272,256]{1,0:T(8,128)(2,1)S(1)} %pad_maximum_fusion.3), channel_id=1, source_target_pairs={{0,2},{2,0},{4,6},{6,4},{8,10},{10,8},{12,14},{14,12},{16,18},{18,... | collective-permute-start | bytes 417800 | tf_op jit(solution)/shard_map/ppermute | solution.py:37
  78.3 0.7 collective-permute-start.17
  79.0 1.5 %collective-permute-start.18 = (bf16[272,256]{1,0:T(8,128)(2,1)S(1)}, bf16[272,256]{1,0:T(8,128)(2,1)S(1)}, u32[]{:S(2)}, u32[]{:S(2)}) collective-permute-start(bf16[272,256]{1,0:T(8,128)(2,1)S(1)} %pad_maximum_fusion.5), channel_id=1, source_target_pairs={{0,6},{2,4},{4,2},{6,0},{8,14},{10,12},{12,10},{14,8},{16,22},{18,... | collective-permute-start | bytes 417800 | tf_op jit(solution)/shard_map/ppermute | solution.py:37
  80.5 2.5 %collective-permute-done.16 = bf16[272,256]{1,0:T(8,128)(2,1)S(1)} collective-permute-done((bf16[272,256]{1,0:T(8,128)(2,1)S(1)}, bf16[272,256]{1,0:T(8,128)(2,1)S(1)}, u32[]{:S(2)}, u32[]{:S(2)}) %collective-permute-start.16) | collective-permute-done | bytes 139296 | tf_op jit(solution)/shard_map/ppermute | solution.py:37
  83.0 3.8 %collective-permute-done.17 = bf16[272,256]{1,0:T(8,128)(2,1)S(1)} collective-permute-done((bf16[272,256]{1,0:T(8,128)(2,1)S(1)}, bf16[272,256]{1,0:T(8,128)(2,1)S(1)}, u32[]{:S(2)}, u32[]{:S(2)}) %collective-permute-start.17) | collective-permute-done | bytes 139296 | tf_op jit(solution)/shard_map/ppermute | solution.py:37
  87.3 3.5 %collective-permute-start.20 = (bf16[272,64]{1,0:T(8,128)(2,1)S(1)}, bf16[272,64]{1,0:T(8,128)(2,1)S(1)}, u32[]{:S(2)}, u32[]{:S(2)}) collective-permute-start(bf16[272,64]{1,0:T(8,128)(2,1)S(1)} %pad_maximum_fusion.11), channel_id=1, source_target_pairs={{0,16},{2,18},{4,20},{6,22},{8,24},{10,26},{12,28},{14,30},{16,0},... | collective-permute-start | bytes 104456 | tf_op jit(solution)/shard_map/ppermute | solution.py:37
  90.9 1.0 collective-permute-start.21
  91.9 1.3 %collective-permute-done.20 = bf16[272,64]{1,0:T(8,128)(2,1)S(1)} collective-permute-done((bf16[272,64]{1,0:T(8,128)(2,1)S(1)}, bf16[272,64]{1,0:T(8,128)(2,1)S(1)}, u32[]{:S(2)}, u32[]{:S(2)}) %collective-permute-start.20) | collective-permute-done | bytes 34848 | tf_op jit(solution)/shard_map/ppermute | solution.py:37
  93.2 4.2 %collective-permute-done.21 = bf16[272,64]{1,0:T(8,128)(2,1)S(1)} collective-permute-done((bf16[272,64]{1,0:T(8,128)(2,1)S(1)}, bf16[272,64]{1,0:T(8,128)(2,1)S(1)}, u32[]{:S(2)}, u32[]{:S(2)}) %collective-permute-start.21) | collective-permute-done | bytes 34848 | tf_op jit(solution)/shard_map/ppermute | solution.py:37
  97.6 1.2 collective-permute-start.23
  98.8 3.2 %collective-permute-start.24 = (bf16[272,64]{1,0:T(8,128)(2,1)S(1)}, bf16[272,64]{1,0:T(8,128)(2,1)S(1)}, u32[]{:S(2)}, u32[]{:S(2)}) collective-permute-start(bf16[272,64]{1,0:T(8,128)(2,1)S(1)} %pad_maximum_fusion.13), channel_id=1, source_target_pairs={{0,24},{2,26},{4,28},{6,30},{8,16},{10,18},{12,20},{14,22},{16,8},... | collective-permute-start | bytes 104456 | tf_op jit(solution)/shard_map/ppermute | solution.py:51
  102.0 0.3 dynamic_update_slice.56
  102.4 1.4 %dynamic_update_slice.57 = bf16[272,256]{1,0:T(8,128)(2,1)S(1)} dynamic-update-slice(bf16[272,256]{1,0:T(8,128)(2,1)S(1)} %dynamic_update_slice.56, bf16[272,64]{1,0:T(8,128)(2,1)} %collective-permute-done.22, s32[]{:T(128)} %constant.112.clone.1, s32[]{:T(128)S(6)} %select_n.32) | dynamic-update-slice | bytes 69636 | tf_op jit(solution)/shard_map/dynamic_update_slice | solution.py:55
  103.8 0.3 dynamic_update_slice.58
  104.1 1.0 collective-permute-done.24
  105.1 0.5 dynamic_update_slice.59
  105.7 0.4 collective-permute-start.25
  106.1 1.5 %collective-permute-start.26 = (bf16[272,256]{1,0:T(8,128)(2,1)S(1)}, bf16[272,256]{1,0:T(8,128)(2,1)S(1)}, u32[]{:S(2)}, u32[]{:S(2)}) collective-permute-start(bf16[272,256]{1,0:T(8,128)(2,1)S(1)} %dynamic_update_slice.59), channel_id=1, source_target_pairs={{0,4},{2,6},{4,0},{6,2},{8,12},{10,14},{12,8},{14,10},{16,20},{18,... | collective-permute-start | bytes 417800 | tf_op jit(solution)/shard_map/ppermute | solution.py:51
  107.6 1.7 %collective-permute-start.27 = (bf16[272,256]{1,0:T(8,128)(2,1)S(1)}, bf16[272,256]{1,0:T(8,128)(2,1)S(1)}, u32[]{:S(2)}, u32[]{:S(2)}) collective-permute-start(bf16[272,256]{1,0:T(8,128)(2,1)S(1)} %dynamic_update_slice.59), channel_id=1, source_target_pairs={{0,6},{2,4},{4,2},{6,0},{8,14},{10,12},{12,10},{14,8},{16,22},{18,... | collective-permute-start | bytes 417800 | tf_op jit(solution)/shard_map/ppermute | solution.py:51
  109.3 1.5 %collective-permute-done.25 = bf16[272,256]{1,0:T(8,128)(2,1)S(1)} collective-permute-done((bf16[272,256]{1,0:T(8,128)(2,1)S(1)}, bf16[272,256]{1,0:T(8,128)(2,1)S(1)}, u32[]{:S(2)}, u32[]{:S(2)}) %collective-permute-start.25) | collective-permute-done | bytes 139296 | tf_op jit(solution)/shard_map/ppermute | solution.py:51
  110.8 0.3 collective-permute-done.26
  111.2 2.4 %collective-permute-done.27 = bf16[272,256]{1,0:T(8,128)(2,1)S(1)} collective-permute-done((bf16[272,256]{1,0:T(8,128)(2,1)S(1)}, bf16[272,256]{1,0:T(8,128)(2,1)S(1)}, u32[]{:S(2)}, u32[]{:S(2)}) %collective-permute-start.27) | collective-permute-done | bytes 139296 | tf_op jit(solution)/shard_map/ppermute | solution.py:51
  113.6 4.7 %convolution_convert_fusion = bf16[256,3072]{1,0:T(8,128)(2,1)S(1)} fusion(bf16[3072,1024]{1,0:T(8,128)(2,1)} %constant_dynamic-update-slice_fusion, bf16[272,1024]{1,0:T(8,128)(2,1)S(1)} %constant_dynamic-update-slice_fusion.3), kind=kOutput, calls=%fused_computation.12 | convolution fusion | flops 1611399168 | bytes 8388608 | tf_op jit(solution)/shard_map/dot_general | solution.py:143
  118.6 0.6 collective-permute-start.28
  119.2 1.5 %collective-permute-done.28 = f32[128]{0:T(128)S(1)} collective-permute-done((f32[128]{0:T(128)S(1)}, f32[128]{0:T(128)S(1)}, u32[]{:S(2)}, u32[]{:S(2)}) %collective-permute-start.28) | collective-permute-done | bytes 544 | tf_op jit(solution)/shard_map/ppermute | solution.py:147
  120.7 2.9 %fusion.19 = (f32[128,3072]{1,0:T(8,128)}, f32[128,3072]{1,0:T(8,128)}) fusion(f32[128,3072]{1,0:T(8,128)S(1)} %get-tuple-element.100, bf16[128,3072]{1,0:T(8,128)(2,1)S(1)} %collective-permute-done.29, bf16[128,3072]{1,0:T(8,128)(2,1)S(1)} %copy-done.4, f32[128,3072]{1,0:T(8,128)S(1)} %copy-done, bf16[256,3072]{1,0:T(8,128)(2,1)S(1)} %convolution_convert_fusion, ...), kind=kLoop, calls=%fused_computation.38 | loop fusion | flops 8650752 | bytes 9454080 | tf_op jit(solution)/shard_map/sub | solution.py:168
  (136 shorter events, 3.7 us)
Async XLA Ops:
  0.6 2.9 %copy-start = (f32[128,3072]{1,0:T(8,128)S(1)}, f32[128,3072]{1,0:T(8,128)}, u32[]{:S(2)}) copy-start(f32[128,3072]{1,0:T(8,128)} %param.19) | copy-start | bytes 4718596
  0.6 2.9 %copy-start.6 = (f32[3072]{0:T(1024)S(1)}, f32[3072]{0:T(1024)}, u32[]{:S(2)}) copy-start(f32[3072]{0:T(1024)} %param.17) | copy-start | bytes 36868
  1.4 2.8 %copy-start.8 = (f32[1024]{0:T(1024)S(1)}, f32[1024]{0:T(1024)}, u32[]{:S(2)}) copy-start(f32[1024]{0:T(1024)} %param.18) | copy-start | bytes 12292
  1.4 2.8 %copy-start.7 = (s32[3072]{0:T(1024)S(1)}, s32[3072]{0:T(1024)}, u32[]{:S(2)}) copy-start(s32[3072]{0:T(1024)} %param.15) | copy-start | bytes 36868
  3.0 2.5 %collective-permute-start = (bf16[128,3072]{1,0:T(8,128)(2,1)S(1)}, bf16[128,3072]{1,0:T(8,128)(2,1)S(1)}, u32[]{:S(2)}, u32[]{:S(2)}) collective-permute-start(bf16[128,3072]{1,0:T(8,128)(2,1)S(1)} %select_convert_fusion), channel_id=1, source_target_pairs={{0,1},{1,0},{2,3},{3,2},{4,5},{5,4},{6,7},{7,6},{8,9},{9,8},{10,11... | collective-permute-start | bytes 2359304 | tf_op jit(solution)/shard_map/ppermute | solution.py:116
  4.3 6.3 %copy-start.11 = (bf16[2048,1024]{1,0:T(8,128)(2,1)S(1)}, bf16[2048,1024]{1,0:T(8,128)(2,1)}, u32[]{:S(2)}) copy-start(bf16[2048,1024]{1,0:T(8,128)(2,1)} %param.14) | copy-start | bytes 12582916
  13.4 9.6 %collective-permute-start.1 = (bf16[272,256]{1,0:T(8,128)(2,1)S(1)}, bf16[272,256]{1,0:T(8,128)(2,1)S(1)}, u32[]{:S(2)}, u32[]{:S(2)}) collective-permute-start(bf16[272,256]{1,0:T(8,128)(2,1)S(1)} %pad_maximum_fusion), channel_id=1, source_target_pairs={{0,2},{2,0},{4,6},{6,4},{8,10},{10,8},{12,14},{14,12},{16,18},{18,... | collective-permute-start | bytes 417800 | tf_op jit(solution)/shard_map/ppermute | solution.py:37
  16.3 8.5 %collective-permute-start.2 = (bf16[272,256]{1,0:T(8,128)(2,1)S(1)}, bf16[272,256]{1,0:T(8,128)(2,1)S(1)}, u32[]{:S(2)}, u32[]{:S(2)}) collective-permute-start(bf16[272,256]{1,0:T(8,128)(2,1)S(1)} %pad_maximum_fusion.1), channel_id=1, source_target_pairs={{0,4},{2,6},{4,0},{6,2},{8,12},{10,14},{12,8},{14,10},{16,20},{18,... | collective-permute-start | bytes 417800 | tf_op jit(solution)/shard_map/ppermute | solution.py:37
  17.9 6.9 %collective-permute-start.3 = (bf16[272,256]{1,0:T(8,128)(2,1)S(1)}, bf16[272,256]{1,0:T(8,128)(2,1)S(1)}, u32[]{:S(2)}, u32[]{:S(2)}) collective-permute-start(bf16[272,256]{1,0:T(8,128)(2,1)S(1)} %pad_maximum_fusion.2), channel_id=1, source_target_pairs={{0,6},{2,4},{4,2},{6,0},{8,14},{10,12},{12,10},{14,8},{16,22},{18,... | collective-permute-start | bytes 417800 | tf_op jit(solution)/shard_map/ppermute | solution.py:37
  25.2 9.8 %collective-permute-start.4 = (bf16[272,64]{1,0:T(8,128)(2,1)S(1)}, bf16[272,64]{1,0:T(8,128)(2,1)S(1)}, u32[]{:S(2)}, u32[]{:S(2)}) collective-permute-start(bf16[272,64]{1,0:T(8,128)(2,1)S(1)} %pad_maximum_fusion.6), channel_id=1, source_target_pairs={{0,8},{2,10},{4,12},{6,14},{8,0},{10,2},{12,4},{14,6},{16,24},{18,... | collective-permute-start | bytes 104456 | tf_op jit(solution)/shard_map/ppermute | solution.py:37
  26.9 8.1 %collective-permute-start.5 = (bf16[272,64]{1,0:T(8,128)(2,1)S(1)}, bf16[272,64]{1,0:T(8,128)(2,1)S(1)}, u32[]{:S(2)}, u32[]{:S(2)}) collective-permute-start(bf16[272,64]{1,0:T(8,128)(2,1)S(1)} %pad_maximum_fusion.7), channel_id=1, source_target_pairs={{0,16},{2,18},{4,20},{6,22},{8,24},{10,26},{12,28},{14,30},{16,0},... | collective-permute-start | bytes 104456 | tf_op jit(solution)/shard_map/ppermute | solution.py:37
  29.6 6.2 %collective-permute-start.6 = (bf16[272,64]{1,0:T(8,128)(2,1)S(1)}, bf16[272,64]{1,0:T(8,128)(2,1)S(1)}, u32[]{:S(2)}, u32[]{:S(2)}) collective-permute-start(bf16[272,64]{1,0:T(8,128)(2,1)S(1)} %pad_maximum_fusion.8), channel_id=1, source_target_pairs={{0,24},{2,26},{4,28},{6,30},{8,16},{10,18},{12,20},{14,22},{16,8},... | collective-permute-start | bytes 104456 | tf_op jit(solution)/shard_map/ppermute | solution.py:37
  36.0 13.7 %collective-permute-start.7 = (bf16[272,64]{1,0:T(8,128)(2,1)S(1)}, bf16[272,64]{1,0:T(8,128)(2,1)S(1)}, u32[]{:S(2)}, u32[]{:S(2)}) collective-permute-start(bf16[272,64]{1,0:T(8,128)(2,1)S(1)} %pad_maximum_fusion.9), channel_id=1, source_target_pairs={{0,8},{2,10},{4,12},{6,14},{8,0},{10,2},{12,4},{14,6},{16,24},{18,... | collective-permute-start | bytes 104456 | tf_op jit(solution)/shard_map/ppermute | solution.py:51
  36.1 13.6 %collective-permute-start.8 = (bf16[272,64]{1,0:T(8,128)(2,1)S(1)}, bf16[272,64]{1,0:T(8,128)(2,1)S(1)}, u32[]{:S(2)}, u32[]{:S(2)}) collective-permute-start(bf16[272,64]{1,0:T(8,128)(2,1)S(1)} %pad_maximum_fusion.9), channel_id=1, source_target_pairs={{0,16},{2,18},{4,20},{6,22},{8,24},{10,26},{12,28},{14,30},{16,0},... | collective-permute-start | bytes 104456 | tf_op jit(solution)/shard_map/ppermute | solution.py:51
  39.6 10.2 %collective-permute-start.9 = (bf16[272,64]{1,0:T(8,128)(2,1)S(1)}, bf16[272,64]{1,0:T(8,128)(2,1)S(1)}, u32[]{:S(2)}, u32[]{:S(2)}) collective-permute-start(bf16[272,64]{1,0:T(8,128)(2,1)S(1)} %pad_maximum_fusion.9), channel_id=1, source_target_pairs={{0,24},{2,26},{4,28},{6,30},{8,16},{10,18},{12,20},{14,22},{16,8},... | collective-permute-start | bytes 104456 | tf_op jit(solution)/shard_map/ppermute | solution.py:51
  46.6 2.7 %copy-start.5 = (bf16[3072,1024]{1,0:T(8,128)(2,1)}, bf16[3072,1024]{1,0:T(8,128)(2,1)S(1)}, u32[]{:S(2)}) copy-start(bf16[3072,1024]{1,0:T(8,128)(2,1)S(1)} %constant_dynamic-update-slice_fusion.1) | copy-start | bytes 18874372
  51.2 6.8 %collective-permute-start.10 = (bf16[272,256]{1,0:T(8,128)(2,1)S(1)}, bf16[272,256]{1,0:T(8,128)(2,1)S(1)}, u32[]{:S(2)}, u32[]{:S(2)}) collective-permute-start(bf16[272,256]{1,0:T(8,128)(2,1)S(1)} %dynamic_update_slice.51), channel_id=1, source_target_pairs={{0,2},{2,0},{4,6},{6,4},{8,10},{10,8},{12,14},{14,12},{16,18},{18,... | collective-permute-start | bytes 417800 | tf_op jit(solution)/shard_map/ppermute | solution.py:51
  52.5 5.6 %collective-permute-start.11 = (bf16[272,256]{1,0:T(8,128)(2,1)S(1)}, bf16[272,256]{1,0:T(8,128)(2,1)S(1)}, u32[]{:S(2)}, u32[]{:S(2)}) collective-permute-start(bf16[272,256]{1,0:T(8,128)(2,1)S(1)} %dynamic_update_slice.51), channel_id=1, source_target_pairs={{0,4},{2,6},{4,0},{6,2},{8,12},{10,14},{12,8},{14,10},{16,20},{18,... | collective-permute-start | bytes 417800 | tf_op jit(solution)/shard_map/ppermute | solution.py:51
  53.4 6.0 %collective-permute-start.12 = (bf16[272,256]{1,0:T(8,128)(2,1)S(1)}, bf16[272,256]{1,0:T(8,128)(2,1)S(1)}, u32[]{:S(2)}, u32[]{:S(2)}) collective-permute-start(bf16[272,256]{1,0:T(8,128)(2,1)S(1)} %dynamic_update_slice.51), channel_id=1, source_target_pairs={{0,6},{2,4},{4,2},{6,0},{8,14},{10,12},{12,10},{14,8},{16,22},{18,... | collective-permute-start | bytes 417800 | tf_op jit(solution)/shard_map/ppermute | solution.py:51
  64.0 3.9 %copy-start.1 = (bf16[256,3072]{1,0:T(8,128)(2,1)}, bf16[256,3072]{1,0:T(8,128)(2,1)S(1)}, u32[]{:S(2)}) copy-start(bf16[256,3072]{1,0:T(8,128)(2,1)S(1)} %convolution_convert_fusion.1) | copy-start | bytes 4718596
  64.0 2.9 %collective-permute-start.14 = (bf16[128,3072]{1,0:T(8,128)(2,1)S(1)}, bf16[128,3072]{1,0:T(8,128)(2,1)S(1)}, u32[]{:S(2)}, u32[]{:S(2)}) collective-permute-start(bf16[128,3072]{1,0:T(8,128)(2,1)S(1)} %slice.446), channel_id=1, source_target_pairs={{0,1},{1,0},{2,3},{3,2},{4,5},{5,4},{6,7},{7,6},{8,9},{9,8},{10,11... | collective-permute-start | bytes 2359304 | tf_op jit(solution)/shard_map/ppermute | solution.py:148
  64.4 2.0 %collective-permute-start.13 = (f32[128]{0:T(128)S(1)}, f32[128]{0:T(128)S(1)}, u32[]{:S(2)}, u32[]{:S(2)}) collective-permute-start(f32[128]{0:T(128)S(1)} %slice.386), channel_id=1, source_target_pairs={{0,1},{1,0},{2,3},{3,2},{4,5},{5,4},{6,7},{7,6},{8,9},{9,8},{10,11... | collective-permute-start | bytes 1544 | tf_op jit(solution)/shard_map/ppermute | solution.py:147
  66.4 0.5 copy-start.9
  66.9 0.9 copy-start.3
  68.8 2.6 %collective-permute-start.15 = (bf16[128,3072]{1,0:T(8,128)(2,1)}, bf16[128,3072]{1,0:T(8,128)(2,1)}, u32[]{:S(2)}, u32[]{:S(2)}) collective-permute-start(bf16[128,3072]{1,0:T(8,128)(2,1)} %convert_element_type.364), channel_id=1, source_target_pairs={{0,1},{1,0},{2,3},{3,2},{4,5},{5,4},{6,7},{7,6},{8,9},{9,8},{10,11... | collective-permute-start | bytes 2359304 | tf_op jit(solution)/shard_map/ppermute | solution.py:116
  76.7 6.2 %collective-permute-start.16 = (bf16[272,256]{1,0:T(8,128)(2,1)S(1)}, bf16[272,256]{1,0:T(8,128)(2,1)S(1)}, u32[]{:S(2)}, u32[]{:S(2)}) collective-permute-start(bf16[272,256]{1,0:T(8,128)(2,1)S(1)} %pad_maximum_fusion.3), channel_id=1, source_target_pairs={{0,2},{2,0},{4,6},{6,4},{8,10},{10,8},{12,14},{14,12},{16,18},{18,... | collective-permute-start | bytes 417800 | tf_op jit(solution)/shard_map/ppermute | solution.py:37
  78.3 8.5 %collective-permute-start.17 = (bf16[272,256]{1,0:T(8,128)(2,1)S(1)}, bf16[272,256]{1,0:T(8,128)(2,1)S(1)}, u32[]{:S(2)}, u32[]{:S(2)}) collective-permute-start(bf16[272,256]{1,0:T(8,128)(2,1)S(1)} %pad_maximum_fusion.4), channel_id=1, source_target_pairs={{0,4},{2,6},{4,0},{6,2},{8,12},{10,14},{12,8},{14,10},{16,20},{18,... | collective-permute-start | bytes 417800 | tf_op jit(solution)/shard_map/ppermute | solution.py:37
  79.0 7.9 %collective-permute-start.18 = (bf16[272,256]{1,0:T(8,128)(2,1)S(1)}, bf16[272,256]{1,0:T(8,128)(2,1)S(1)}, u32[]{:S(2)}, u32[]{:S(2)}) collective-permute-start(bf16[272,256]{1,0:T(8,128)(2,1)S(1)} %pad_maximum_fusion.5), channel_id=1, source_target_pairs={{0,6},{2,4},{4,2},{6,0},{8,14},{10,12},{12,10},{14,8},{16,22},{18,... | collective-permute-start | bytes 417800 | tf_op jit(solution)/shard_map/ppermute | solution.py:37
  87.2 4.6 %collective-permute-start.19 = (bf16[272,64]{1,0:T(8,128)(2,1)S(1)}, bf16[272,64]{1,0:T(8,128)(2,1)S(1)}, u32[]{:S(2)}, u32[]{:S(2)}) collective-permute-start(bf16[272,64]{1,0:T(8,128)(2,1)S(1)} %pad_maximum_fusion.10), channel_id=1, source_target_pairs={{0,8},{2,10},{4,12},{6,14},{8,0},{10,2},{12,4},{14,6},{16,24},{18,... | collective-permute-start | bytes 104456 | tf_op jit(solution)/shard_map/ppermute | solution.py:37
  87.3 5.8 %collective-permute-start.20 = (bf16[272,64]{1,0:T(8,128)(2,1)S(1)}, bf16[272,64]{1,0:T(8,128)(2,1)S(1)}, u32[]{:S(2)}, u32[]{:S(2)}) collective-permute-start(bf16[272,64]{1,0:T(8,128)(2,1)S(1)} %pad_maximum_fusion.11), channel_id=1, source_target_pairs={{0,16},{2,18},{4,20},{6,22},{8,24},{10,26},{12,28},{14,30},{16,0},... | collective-permute-start | bytes 104456 | tf_op jit(solution)/shard_map/ppermute | solution.py:37
  90.9 6.5 %collective-permute-start.21 = (bf16[272,64]{1,0:T(8,128)(2,1)S(1)}, bf16[272,64]{1,0:T(8,128)(2,1)S(1)}, u32[]{:S(2)}, u32[]{:S(2)}) collective-permute-start(bf16[272,64]{1,0:T(8,128)(2,1)S(1)} %pad_maximum_fusion.12), channel_id=1, source_target_pairs={{0,24},{2,26},{4,28},{6,30},{8,16},{10,18},{12,20},{14,22},{16,8},... | collective-permute-start | bytes 104456 | tf_op jit(solution)/shard_map/ppermute | solution.py:37
  97.6 4.8 %collective-permute-start.22 = (bf16[272,64]{1,0:T(8,128)(2,1)S(1)}, bf16[272,64]{1,0:T(8,128)(2,1)}, u32[]{:S(2)}, u32[]{:S(2)}) collective-permute-start(bf16[272,64]{1,0:T(8,128)(2,1)S(1)} %pad_maximum_fusion.13), channel_id=1, source_target_pairs={{0,8},{2,10},{4,12},{6,14},{8,0},{10,2},{12,4},{14,6},{16,24},{18,... | collective-permute-start | bytes 104456 | tf_op jit(solution)/shard_map/ppermute | solution.py:51
  97.6 6.2 %collective-permute-start.23 = (bf16[272,64]{1,0:T(8,128)(2,1)S(1)}, bf16[272,64]{1,0:T(8,128)(2,1)S(1)}, u32[]{:S(2)}, u32[]{:S(2)}) collective-permute-start(bf16[272,64]{1,0:T(8,128)(2,1)S(1)} %pad_maximum_fusion.13), channel_id=1, source_target_pairs={{0,16},{2,18},{4,20},{6,22},{8,24},{10,26},{12,28},{14,30},{16,0},... | collective-permute-start | bytes 104456 | tf_op jit(solution)/shard_map/ppermute | solution.py:51
  98.8 6.3 %collective-permute-start.24 = (bf16[272,64]{1,0:T(8,128)(2,1)S(1)}, bf16[272,64]{1,0:T(8,128)(2,1)S(1)}, u32[]{:S(2)}, u32[]{:S(2)}) collective-permute-start(bf16[272,64]{1,0:T(8,128)(2,1)S(1)} %pad_maximum_fusion.13), channel_id=1, source_target_pairs={{0,24},{2,26},{4,28},{6,30},{8,16},{10,18},{12,20},{14,22},{16,8},... | collective-permute-start | bytes 104456 | tf_op jit(solution)/shard_map/ppermute | solution.py:51
  105.7 5.1 %collective-permute-start.25 = (bf16[272,256]{1,0:T(8,128)(2,1)S(1)}, bf16[272,256]{1,0:T(8,128)(2,1)S(1)}, u32[]{:S(2)}, u32[]{:S(2)}) collective-permute-start(bf16[272,256]{1,0:T(8,128)(2,1)S(1)} %dynamic_update_slice.59), channel_id=1, source_target_pairs={{0,2},{2,0},{4,6},{6,4},{8,10},{10,8},{12,14},{14,12},{16,18},{18,... | collective-permute-start | bytes 417800 | tf_op jit(solution)/shard_map/ppermute | solution.py:51
  106.1 5.1 %collective-permute-start.26 = (bf16[272,256]{1,0:T(8,128)(2,1)S(1)}, bf16[272,256]{1,0:T(8,128)(2,1)S(1)}, u32[]{:S(2)}, u32[]{:S(2)}) collective-permute-start(bf16[272,256]{1,0:T(8,128)(2,1)S(1)} %dynamic_update_slice.59), channel_id=1, source_target_pairs={{0,4},{2,6},{4,0},{6,2},{8,12},{10,14},{12,8},{14,10},{16,20},{18,... | collective-permute-start | bytes 417800 | tf_op jit(solution)/shard_map/ppermute | solution.py:51
  107.6 6.0 %collective-permute-start.27 = (bf16[272,256]{1,0:T(8,128)(2,1)S(1)}, bf16[272,256]{1,0:T(8,128)(2,1)S(1)}, u32[]{:S(2)}, u32[]{:S(2)}) collective-permute-start(bf16[272,256]{1,0:T(8,128)(2,1)S(1)} %dynamic_update_slice.59), channel_id=1, source_target_pairs={{0,6},{2,4},{4,2},{6,0},{8,14},{10,12},{12,10},{14,8},{16,22},{18,... | collective-permute-start | bytes 417800 | tf_op jit(solution)/shard_map/ppermute | solution.py:51
  113.6 7.2 %copy-start.4 = (bf16[128,3072]{1,0:T(8,128)(2,1)S(1)}, bf16[128,3072]{1,0:T(8,128)(2,1)}, u32[]{:S(2)}) copy-start(bf16[128,3072]{1,0:T(8,128)(2,1)} %copy-done.3) | copy-start | bytes 2359300
  118.3 2.4 %copy-start.10 = (f32[128]{0:T(128)S(1)}, f32[128]{0:T(128)}, u32[]{:S(2)}) copy-start(f32[128]{0:T(128)} %copy-done.9) | copy-start | bytes 1540
  118.3 2.5 %copy-start.2 = (bf16[256,3072]{1,0:T(8,128)(2,1)S(1)}, bf16[256,3072]{1,0:T(8,128)(2,1)}, u32[]{:S(2)}) copy-start(bf16[256,3072]{1,0:T(8,128)(2,1)} %copy-done.1) | copy-start | bytes 4718596
  118.3 2.4 %collective-permute-start.29 = (bf16[128,3072]{1,0:T(8,128)(2,1)S(1)}, bf16[128,3072]{1,0:T(8,128)(2,1)S(1)}, u32[]{:S(2)}, u32[]{:S(2)}) collective-permute-start(bf16[128,3072]{1,0:T(8,128)(2,1)S(1)} %slice.479), channel_id=1, source_target_pairs={{0,1},{1,0},{2,3},{3,2},{4,5},{5,4},{6,7},{7,6},{8,9},{9,8},{10,11... | collective-permute-start | bytes 2359304 | tf_op jit(solution)/shard_map/ppermute | solution.py:148
  118.6 2.0 %collective-permute-start.28 = (f32[128]{0:T(128)S(1)}, f32[128]{0:T(128)S(1)}, u32[]{:S(2)}, u32[]{:S(2)}) collective-permute-start(f32[128]{0:T(128)S(1)} %slice.427), channel_id=1, source_target_pairs={{0,1},{1,0},{2,3},{3,2},{4,5},{5,4},{6,7},{7,6},{8,9},{9,8},{10,11... | collective-permute-start | bytes 1544 | tf_op jit(solution)/shard_map/ppermute | solution.py:147

commit v2 on v1

--- a/solution.py
+++ b/solution.py
@@ -119,7 +119,10 @@
             if first:
                 coeff = coeff_from_table(rows)
             else:
-                coeff = jnp.dot(rows, built[0], preferred_element_type=jnp.float32)
+                coeff = sum(
+                    jnp.dot(rows[:, a:b], built[p], preferred_element_type=jnp.float32)
+                    for p, (a, b) in enumerate((p * span, (p + 1) * span) for p in range(pieces))
+                )
             sums = jnp.zeros((8, group), jnp.float32)
             sums = sums.at[0, :own].set(jnp.sum(vector * vector, axis=1))
             sums = sums.at[1, :own].set(jnp.sum(noise_var[None, :] * vector * vector, axis=1))
@@ -132,17 +135,22 @@
                 [piece(p) for p in range(pieces)] if first else (),
             )
             if first:
-                built.append(jnp.concatenate(side, 0))
-            features = built[0]
+                built.extend(side)
             weights = gathered[:samples]
             sums = gathered[samples : samples + 8].astype(jnp.float32) + gathered[
                 samples + 8 : samples + 16
             ].astype(jnp.float32)
             wide = weights.astype(jnp.float32)
             energy = jnp.sum(wide * wide / spectrum[None, :], axis=1)
-            partials = lax.dot_general(
-                weights, features, (((1,), (1,)), ((), ())), preferred_element_type=jnp.float32
-            ).astype(jnp.bfloat16)
+            partials = jnp.concatenate(
+                [
+                    lax.dot_general(
+                        weights, built[p], (((1,), (1,)), ((), ())), preferred_element_type=jnp.float32
+                    ).astype(jnp.bfloat16)
+                    for p in range(pieces)
+                ],
+                1,
+            )
             if pair:
                 energy = energy[:own] + lax.ppermute(energy[own:], "eig", swap)
                 image = partials[:own].astype(jnp.float32) + lax.ppermute(

time: 124 us -> 124 us (level)
  local copies, waits for them, and re-layouts: 12.5 us -> 7.46 us
  waiting for transfers between devices: 26.9 us -> 30.4 us
  matrix products: 37.8 us -> 39.5 us
    ppermute x12, waiting for transfers between devices: 6.46 us -> 11.6 us  [vert_sum(): lax.ppermute(cur, 'vert', [(i, i ^ masks[t]) for i in range(n_vert)])]
    concatenate x1 -> x0, local copies, waits for them, and re-layouts: 3.14 us -> none  [operate(): built.append(jnp.concatenate(side, 0))]
    dot_general x3, matrix products: 16 us -> 17.9 us  [work(): jnp.dot(rows, eig_table, preferred_element_type=jnp.float32)]
    unnamed x26 -> x34, local copies, waits for them, and re-layouts: 3.57 us -> 1.74 us
    ppermute x12, waiting for transfers between devices: 14.3 us -> 12.5 us  [vert_sum(): lax.ppermute(send, 'vert', [(i, i ^ masks[t + 1]) for i in range(n_vert)])]
    dot_general x3 -> x9, matrix products: 14.4 us -> 14.1 us  [the longest x6 7.94 us: operate(): lax.dot_general(weights, built[p], (((1,), (1,)), ((), ())), preferred_el...]
  transfers between devices with their start and end apart: 30 -> 30, of which waited for: 15 -> 19; matrix products, arithmetic and copies ran while one was open for 19% -> 18% of each run, Pallas kernels for 0% -> 0%
where the time goes in v2:
time: 124 us
  matrix products  39.5 us (32%)
  starting transfers between devices  35.2 us (28%)
  waiting for transfers between devices  30.4 us (25%)
  other arithmetic  8.96 us (7%)
  local copies, waits for them, and re-layouts  7.46 us (6%)
  between operations  2.41 us (2%)
    dot_general x3, matrix products, work(): jnp.dot(rows, eig_table, preferred_element_type=jnp.float32)  17.9 us
    ppermute x12, starting transfers between devices, vert_sum(): lax.ppermute(send, 'vert', [(i, i ^ masks[t + 1]) for i in range(n_vert)])  17.2 us
    ppermute x12, starting transfers between devices, vert_sum(): lax.ppermute(cur, 'vert', [(i, i ^ masks[t]) for i in range(n_vert)])  16 us
    ppermute x12, waiting for transfers between devices, vert_sum(): lax.ppermute(send, 'vert', [(i, i ^ masks[t + 1]) for i in range(n_vert)])  12.5 us
    ppermute x12, waiting for transfers between devices, vert_sum(): lax.ppermute(cur, 'vert', [(i, i ^ masks[t]) for i in range(n_vert)])  11.6 us
    dot_general x6, matrix products, operate(): lax.dot_general(weights, built[p], (((1,), (1,)), ((), ())), preferred_el...  7.94 us
    dot_general x3, matrix products, operate(): jnp.dot(rows[:, a:b], built[p], preferred_element_type=jnp.float32)  6.14 us
    dot_general x1, matrix products, coeff_from_table(): summed = jnp.dot(rows, picker, preferred_element_type=jnp.float32)  5.08 us
  transfers between devices with their start and end apart: 30, of which 19 were waited for; matrix products, arithmetic and copies ran while one was open for 18% of the time, Pallas kernels for 0%

profile of v2, /device:TPU:0, one launch (start us, length us, event | category | flops | bytes accessed | tf_op | source)
XLA Modules:
  0.0 123.9 jit_solution(9006905212863156074)
XLA Ops:
  1.5 1.5 %select_convert_fusion = bf16[128,3072]{1,0:T(8,128)(2,1)S(1)} fusion(f32[128,3072]{1,0:T(8,128)} %param.19, pred[3072]{0:T(1024)(128)(4,1)S(1)} %iota_compare_fusion.14), kind=kLoop, calls=%fused_computation.59 | loop fusion | flops 393216 | bytes 2362368 | tf_op jit(solution)/shard_map/convert_element_type | solution.py:114
  3.0 0.6 collective-permute-start
  4.3 1.2 collective-permute-done
  5.5 5.1 %subtract_convert_fusion = (bf16[256,2048]{1,0:T(8,128)(2,1)S(1)}, bf16[256,2048]{1,0:T(8,128)(2,1)S(1)}) fusion(s32[3072]{0:T(1024)S(1)} %copy-done.12, bf16[128,3072]{1,0:T(8,128)(2,1)S(1)} %collective-permute-done, bf16[128,3072]{1,0:T(8,128)(2,1)S(1)} %select_convert_fusion), kind=kOutput, calls=%fused_computation.28 | convolution fusion | flops 3232759808 | bytes 3682304 | tf_op jit(solution)/shard_map/dot_general | solution.py:86
  10.6 2.4 %fusion.8 = f32[512,1024]{1,0:T(8,128)S(1)} fusion(bf16[2048,1024]{1,0:T(8,128)(2,1)S(1)} %copy-done.16, bf16[256,2048]{1,0:T(8,128)(2,1)S(1)} %get-tuple-element.115, bf16[256,2048]{1,0:T(8,128)(2,1)S(1)} %get-tuple-element.116), kind=kOutput, calls=%fused_computation.24 | convolution fusion | flops 2151677952 | bytes 8388608 | tf_op jit(solution)/shard_map/dot_general | solution.py:89
  13.4 2.9 %collective-permute-start.1 = (bf16[272,256]{1,0:T(8,128)(2,1)S(1)}, bf16[272,256]{1,0:T(8,128)(2,1)S(1)}, u32[]{:S(2)}, u32[]{:S(2)}) collective-permute-start(bf16[272,256]{1,0:T(8,128)(2,1)S(1)} %pad_maximum_fusion.4), channel_id=1, source_target_pairs={{0,2},{2,0},{4,6},{6,4},{8,10},{10,8},{12,14},{14,12},{16,18},{18,... | collective-permute-start | bytes 417800 | tf_op jit(solution)/shard_map/ppermute | solution.py:37
  16.3 1.6 %collective-permute-start.3 = (bf16[272,256]{1,0:T(8,128)(2,1)S(1)}, bf16[272,256]{1,0:T(8,128)(2,1)S(1)}, u32[]{:S(2)}, u32[]{:S(2)}) collective-permute-start(bf16[272,256]{1,0:T(8,128)(2,1)S(1)} %pad_maximum_fusion.6), channel_id=1, source_target_pairs={{0,6},{2,4},{4,2},{6,0},{8,14},{10,12},{12,10},{14,8},{16,22},{18,... | collective-permute-start | bytes 417800 | tf_op jit(solution)/shard_map/ppermute | solution.py:37
  18.0 6.0 %fusion.14 = bf16[1024,1024]{1,0:T(8,128)(2,1)} fusion(bf16[2048,1024]{1,0:T(8,128)(2,1)S(1)} %copy-done.16, s32[1024]{0:T(1024)S(1)} %get-tuple-element.65), kind=kOutput, calls=%fused_computation.31 | convolution fusion | flops 4298113024 | bytes 6295552 | tf_op jit(solution)/shard_map/dot_general | solution.py:79
  24.0 0.6 collective-permute-done.3
  24.6 1.5 %collective-permute-done.2 = bf16[272,256]{1,0:T(8,128)(2,1)S(1)} collective-permute-done((bf16[272,256]{1,0:T(8,128)(2,1)S(1)}, bf16[272,256]{1,0:T(8,128)(2,1)S(1)}, u32[]{:S(2)}, u32[]{:S(2)}) %collective-permute-start.2) | collective-permute-done | bytes 139296 | tf_op jit(solution)/shard_map/ppermute | solution.py:37
  26.5 1.7 %collective-permute-start.4 = (bf16[272,64]{1,0:T(8,128)(2,1)S(1)}, bf16[272,64]{1,0:T(8,128)(2,1)S(1)}, u32[]{:S(2)}, u32[]{:S(2)}) collective-permute-start(bf16[272,64]{1,0:T(8,128)(2,1)S(1)} %pad_maximum_fusion.10), channel_id=1, source_target_pairs={{0,8},{2,10},{4,12},{6,14},{8,0},{10,2},{12,4},{14,6},{16,24},{18,... | collective-permute-start | bytes 104456 | tf_op jit(solution)/shard_map/ppermute | solution.py:37
  28.2 2.5 %collective-permute-start.6 = (bf16[272,64]{1,0:T(8,128)(2,1)S(1)}, bf16[272,64]{1,0:T(8,128)(2,1)S(1)}, u32[]{:S(2)}, u32[]{:S(2)}) collective-permute-start(bf16[272,64]{1,0:T(8,128)(2,1)S(1)} %pad_maximum_fusion.12), channel_id=1, source_target_pairs={{0,24},{2,26},{4,28},{6,30},{8,16},{10,18},{12,20},{14,22},{16,8},... | collective-permute-start | bytes 104456 | tf_op jit(solution)/shard_map/ppermute | solution.py:37
  31.0 6.0 %fusion.13 = bf16[1024,1024]{1,0:T(8,128)(2,1)} fusion(bf16[2048,1024]{1,0:T(8,128)(2,1)S(1)} %copy-done.16, s32[1024]{0:T(1024)S(1)} %get-tuple-element.69), kind=kOutput, calls=%fused_computation.30 | convolution fusion | flops 4298113024 | bytes 6295552 | tf_op jit(solution)/shard_map/dot_general | solution.py:79
  37.3 1.8 %collective-permute-start.7 = (bf16[272,64]{1,0:T(8,128)(2,1)S(1)}, bf16[272,64]{1,0:T(8,128)(2,1)S(1)}, u32[]{:S(2)}, u32[]{:S(2)}) collective-permute-start(bf16[272,64]{1,0:T(8,128)(2,1)S(1)} %pad_maximum_fusion.13), channel_id=1, source_target_pairs={{0,8},{2,10},{4,12},{6,14},{8,0},{10,2},{12,4},{14,6},{16,24},{18,... | collective-permute-start | bytes 104456 | tf_op jit(solution)/shard_map/ppermute | solution.py:51
  39.0 1.7 %collective-permute-start.8 = (bf16[272,64]{1,0:T(8,128)(2,1)S(1)}, bf16[272,64]{1,0:T(8,128)(2,1)S(1)}, u32[]{:S(2)}, u32[]{:S(2)}) collective-permute-start(bf16[272,64]{1,0:T(8,128)(2,1)S(1)} %pad_maximum_fusion.13), channel_id=1, source_target_pairs={{0,16},{2,18},{4,20},{6,22},{8,24},{10,26},{12,28},{14,30},{16,0},... | collective-permute-start | bytes 104456 | tf_op jit(solution)/shard_map/ppermute | solution.py:51
  40.7 1.0 collective-permute-start.9
  41.7 6.0 %fusion.12 = bf16[1024,1024]{1,0:T(8,128)(2,1)} fusion(bf16[2048,1024]{1,0:T(8,128)(2,1)S(1)} %copy-done.16, s32[1024]{0:T(1024)S(1)} %get-tuple-element.73), kind=kOutput, calls=%fused_computation.29 | convolution fusion | flops 4298113024 | bytes 6295552 | tf_op jit(solution)/shard_map/dot_general | solution.py:79
  48.1 0.6 dynamic_update_slice.49
  49.0 0.6 dynamic_update_slice.51
  49.6 1.6 %collective-permute-start.10 = (bf16[272,256]{1,0:T(8,128)(2,1)S(1)}, bf16[272,256]{1,0:T(8,128)(2,1)S(1)}, u32[]{:S(2)}, u32[]{:S(2)}) collective-permute-start(bf16[272,256]{1,0:T(8,128)(2,1)S(1)} %dynamic_update_slice.51), channel_id=1, source_target_pairs={{0,2},{2,0},{4,6},{6,4},{8,10},{10,8},{12,14},{14,12},{16,18},{18,... | collective-permute-start | bytes 417800 | tf_op jit(solution)/shard_map/ppermute | solution.py:51
  51.7 1.5 %collective-permute-start.12 = (bf16[272,256]{1,0:T(8,128)(2,1)S(1)}, bf16[272,256]{1,0:T(8,128)(2,1)S(1)}, u32[]{:S(2)}, u32[]{:S(2)}) collective-permute-start(bf16[272,256]{1,0:T(8,128)(2,1)S(1)} %dynamic_update_slice.51), channel_id=1, source_target_pairs={{0,6},{2,4},{4,2},{6,0},{8,14},{10,12},{12,10},{14,8},{16,22},{18,... | collective-permute-start | bytes 417800 | tf_op jit(solution)/shard_map/ppermute | solution.py:51
  53.2 2.2 %collective-permute-done.10 = bf16[272,256]{1,0:T(8,128)(2,1)S(1)} collective-permute-done((bf16[272,256]{1,0:T(8,128)(2,1)S(1)}, bf16[272,256]{1,0:T(8,128)(2,1)S(1)}, u32[]{:S(2)}, u32[]{:S(2)}) %collective-permute-start.10) | collective-permute-done | bytes 139296 | tf_op jit(solution)/shard_map/ppermute | solution.py:51
  55.4 0.8 collective-permute-done.11
  56.2 1.5 %collective-permute-done.12 = bf16[272,256]{1,0:T(8,128)(2,1)S(1)} collective-permute-done((bf16[272,256]{1,0:T(8,128)(2,1)S(1)}, bf16[272,256]{1,0:T(8,128)(2,1)S(1)}, u32[]{:S(2)}, u32[]{:S(2)}) %collective-permute-start.12) | collective-permute-done | bytes 139296 | tf_op jit(solution)/shard_map/ppermute | solution.py:51
  57.7 2.5 %convolution_convert_fusion.5 = bf16[256,1024]{1,0:T(8,128)(2,1)S(1)} fusion(bf16[1024,1024]{1,0:T(8,128)(2,1)} %fusion.14, bf16[272,1024]{1,0:T(8,128)(2,1)S(1)} %constant_dynamic-update-slice_fusion.4), kind=kOutput, calls=%fused_computation.58 | convolution fusion | flops 537133056 | bytes 3145728 | tf_op jit(solution)/shard_map/dot_general | solution.py:147
  60.2 0.7 convolution_convert_fusion.4
  61.0 0.8 copy-done.8
  61.8 0.7 convolution_convert_fusion.3
  63.1 0.6 collective-permute-start.13
  63.6 1.5 %collective-permute-done.13 = f32[128]{0:T(128)S(1)} collective-permute-done((f32[128]{0:T(128)S(1)}, f32[128]{0:T(128)S(1)}, u32[]{:S(2)}, u32[]{:S(2)}) %collective-permute-start.13) | collective-permute-done | bytes 544 | tf_op jit(solution)/shard_map/ppermute | solution.py:155
  65.1 0.9 fusion.16
  66.1 1.0 convert_element_type.378
  67.6 2.1 %collective-permute-done.15 = bf16[128,3072]{1,0:T(8,128)(2,1)} collective-permute-done((bf16[128,3072]{1,0:T(8,128)(2,1)}, bf16[128,3072]{1,0:T(8,128)(2,1)}, u32[]{:S(2)}, u32[]{:S(2)}) %collective-permute-start.15) | collective-permute-done | bytes 786464 | tf_op jit(solution)/shard_map/ppermute | solution.py:116
  69.7 2.5 %fusion.29 = f32[256,1024]{1,0:T(8,128)S(1)} fusion(bf16[1024,1024]{1,0:T(8,128)(2,1)} %fusion.13, bf16[128,3072]{1,0:T(8,128)(2,1)} %convert_element_type.378, bf16[128,3072]{1,0:T(8,128)(2,1)} %collective-permute-done.15), kind=kOutput, calls=%fused_computation.75 | convolution fusion | flops 537919488 | bytes 4718592 | tf_op jit(solution)/shard_map/dot_general | solution.py:123
  72.2 1.9 %fusion.33 = f32[256,1024]{1,0:T(8,128)S(1)} fusion(bf16[1024,1024]{1,0:T(8,128)(2,1)S(1)} %copy-done.9, bf16[128,3072]{1,0:T(8,128)(2,1)} %collective-permute-done.15, bf16[128,3072]{1,0:T(8,128)(2,1)} %convert_element_type.378), kind=kOutput, calls=%fused_computation.78 | convolution fusion | flops 537919488 | bytes 4718592 | tf_op jit(solution)/shard_map/dot_general | solution.py:123
  74.1 1.8 %fusion.24 = f32[256,1024]{1,0:T(8,128)S(1)} fusion(f32[256,1024]{1,0:T(8,128)S(1)} %fusion.33, f32[256,1024]{1,0:T(8,128)S(1)} %fusion.29, bf16[1024,1024]{1,0:T(8,128)(2,1)S(1)} %copy-done.5, bf16[128,3072]{1,0:T(8,128)(2,1)} %convert_element_type.378, bf16[128,3072]{1,0:T(8,128)(2,1)} %collective-permute-done.15, f32[1024]{0:T(1024)S(1)} %power_multiply_fusion), kind=kOutput, calls=%fused_computation.52 | convolution fusion | flops 538705920 | bytes 6819840 | tf_op jit(solution)/shard_map/dot_general | solution.py:123
  76.1 1.5 %collective-permute-start.18 = (bf16[272,256]{1,0:T(8,128)(2,1)S(1)}, bf16[272,256]{1,0:T(8,128)(2,1)S(1)}, u32[]{:S(2)}, u32[]{:S(2)}) collective-permute-start(bf16[272,256]{1,0:T(8,128)(2,1)S(1)} %pad_maximum_fusion.9), channel_id=1, source_target_pairs={{0,6},{2,4},{4,2},{6,0},{8,14},{10,12},{12,10},{14,8},{16,22},{18,... | collective-permute-start | bytes 417800 | tf_op jit(solution)/shard_map/ppermute | solution.py:37
  77.6 0.7 collective-permute-start.17
  78.3 1.6 %collective-permute-start.16 = (bf16[272,256]{1,0:T(8,128)(2,1)S(1)}, bf16[272,256]{1,0:T(8,128)(2,1)S(1)}, u32[]{:S(2)}, u32[]{:S(2)}) collective-permute-start(bf16[272,256]{1,0:T(8,128)(2,1)S(1)} %pad_maximum_fusion.7), channel_id=1, source_target_pairs={{0,2},{2,0},{4,6},{6,4},{8,10},{10,8},{12,14},{14,12},{16,18},{18,... | collective-permute-start | bytes 417800 | tf_op jit(solution)/shard_map/ppermute | solution.py:37
  79.8 3.8 %collective-permute-done.18 = bf16[272,256]{1,0:T(8,128)(2,1)S(1)} collective-permute-done((bf16[272,256]{1,0:T(8,128)(2,1)S(1)}, bf16[272,256]{1,0:T(8,128)(2,1)S(1)}, u32[]{:S(2)}, u32[]{:S(2)}) %collective-permute-start.18) | collective-permute-done | bytes 139296 | tf_op jit(solution)/shard_map/ppermute | solution.py:37
  83.7 2.1 %collective-permute-done.17 = bf16[272,256]{1,0:T(8,128)(2,1)S(1)} collective-permute-done((bf16[272,256]{1,0:T(8,128)(2,1)S(1)}, bf16[272,256]{1,0:T(8,128)(2,1)S(1)}, u32[]{:S(2)}, u32[]{:S(2)}) %collective-permute-start.17) | collective-permute-done | bytes 139296 | tf_op jit(solution)/shard_map/ppermute | solution.py:37
  86.2 2.9 %collective-permute-start.21 = (bf16[272,64]{1,0:T(8,128)(2,1)S(1)}, bf16[272,64]{1,0:T(8,128)(2,1)S(1)}, u32[]{:S(2)}, u32[]{:S(2)}) collective-permute-start(bf16[272,64]{1,0:T(8,128)(2,1)S(1)} %pad_maximum_fusion.16), channel_id=1, source_target_pairs={{0,24},{2,26},{4,28},{6,30},{8,16},{10,18},{12,20},{14,22},{16,8},... | collective-permute-start | bytes 104456 | tf_op jit(solution)/shard_map/ppermute | solution.py:37
  89.2 1.6 %collective-permute-start.19 = (bf16[272,64]{1,0:T(8,128)(2,1)S(1)}, bf16[272,64]{1,0:T(8,128)(2,1)S(1)}, u32[]{:S(2)}, u32[]{:S(2)}) collective-permute-start(bf16[272,64]{1,0:T(8,128)(2,1)S(1)} %pad_maximum_fusion.14), channel_id=1, source_target_pairs={{0,8},{2,10},{4,12},{6,14},{8,0},{10,2},{12,4},{14,6},{16,24},{18,... | collective-permute-start | bytes 104456 | tf_op jit(solution)/shard_map/ppermute | solution.py:37
  90.8 2.3 %collective-permute-done.21 = bf16[272,64]{1,0:T(8,128)(2,1)S(1)} collective-permute-done((bf16[272,64]{1,0:T(8,128)(2,1)S(1)}, bf16[272,64]{1,0:T(8,128)(2,1)S(1)}, u32[]{:S(2)}, u32[]{:S(2)}) %collective-permute-start.21) | collective-permute-done | bytes 34848 | tf_op jit(solution)/shard_map/ppermute | solution.py:37
  93.1 2.2 %collective-permute-done.20 = bf16[272,64]{1,0:T(8,128)(2,1)S(1)} collective-permute-done((bf16[272,64]{1,0:T(8,128)(2,1)S(1)}, bf16[272,64]{1,0:T(8,128)(2,1)S(1)}, u32[]{:S(2)}, u32[]{:S(2)}) %collective-permute-start.20) | collective-permute-done | bytes 34848 | tf_op jit(solution)/shard_map/ppermute | solution.py:37
  95.6 0.9 collective-permute-start.22
  96.5 2.3 %collective-permute-start.23 = (bf16[272,64]{1,0:T(8,128)(2,1)S(1)}, bf16[272,64]{1,0:T(8,128)(2,1)S(1)}, u32[]{:S(2)}, u32[]{:S(2)}) collective-permute-start(bf16[272,64]{1,0:T(8,128)(2,1)S(1)} %pad_maximum_fusion.17), channel_id=1, source_target_pairs={{0,16},{2,18},{4,20},{6,22},{8,24},{10,26},{12,28},{14,30},{16,0},... | collective-permute-start | bytes 104456 | tf_op jit(solution)/shard_map/ppermute | solution.py:51
  98.7 1.3 %collective-permute-start.24 = (bf16[272,64]{1,0:T(8,128)(2,1)S(1)}, bf16[272,64]{1,0:T(8,128)(2,1)S(1)}, u32[]{:S(2)}, u32[]{:S(2)}) collective-permute-start(bf16[272,64]{1,0:T(8,128)(2,1)S(1)} %pad_maximum_fusion.17), channel_id=1, source_target_pairs={{0,24},{2,26},{4,28},{6,30},{8,16},{10,18},{12,20},{14,22},{16,8},... | collective-permute-start | bytes 104456 | tf_op jit(solution)/shard_map/ppermute | solution.py:51
  100.8 1.4 %dynamic_update_slice.57 = bf16[272,256]{1,0:T(8,128)(2,1)S(1)} dynamic-update-slice(bf16[272,256]{1,0:T(8,128)(2,1)S(1)} %dynamic_update_slice.56, bf16[272,64]{1,0:T(8,128)(2,1)} %collective-permute-done.22, s32[]{:T(128)} %constant.112.clone.1, s32[]{:T(128)S(6)} %select_n.32) | dynamic-update-slice | bytes 69636 | tf_op jit(solution)/shard_map/dynamic_update_slice | solution.py:55
  102.2 2.0 %collective-permute-done.23 = bf16[272,64]{1,0:T(8,128)(2,1)S(1)} collective-permute-done((bf16[272,64]{1,0:T(8,128)(2,1)S(1)}, bf16[272,64]{1,0:T(8,128)(2,1)S(1)}, u32[]{:S(2)}, u32[]{:S(2)}) %collective-permute-start.23) | collective-permute-done | bytes 34848 | tf_op jit(solution)/shard_map/ppermute | solution.py:51
  104.9 0.5 dynamic_update_slice.59
  105.5 0.6 collective-permute-start.25
  106.1 1.4 %collective-permute-start.26 = (bf16[272,256]{1,0:T(8,128)(2,1)S(1)}, bf16[272,256]{1,0:T(8,128)(2,1)S(1)}, u32[]{:S(2)}, u32[]{:S(2)}) collective-permute-start(bf16[272,256]{1,0:T(8,128)(2,1)S(1)} %dynamic_update_slice.59), channel_id=1, source_target_pairs={{0,4},{2,6},{4,0},{6,2},{8,12},{10,14},{12,8},{14,10},{16,20},{18,... | collective-permute-start | bytes 417800 | tf_op jit(solution)/shard_map/ppermute | solution.py:51
  107.5 1.5 %collective-permute-start.27 = (bf16[272,256]{1,0:T(8,128)(2,1)S(1)}, bf16[272,256]{1,0:T(8,128)(2,1)S(1)}, u32[]{:S(2)}, u32[]{:S(2)}) collective-permute-start(bf16[272,256]{1,0:T(8,128)(2,1)S(1)} %dynamic_update_slice.59), channel_id=1, source_target_pairs={{0,6},{2,4},{4,2},{6,0},{8,14},{10,12},{12,10},{14,8},{16,22},{18,... | collective-permute-start | bytes 417800 | tf_op jit(solution)/shard_map/ppermute | solution.py:51
  109.1 1.6 %collective-permute-done.25 = bf16[272,256]{1,0:T(8,128)(2,1)S(1)} collective-permute-done((bf16[272,256]{1,0:T(8,128)(2,1)S(1)}, bf16[272,256]{1,0:T(8,128)(2,1)S(1)}, u32[]{:S(2)}, u32[]{:S(2)}) %collective-permute-start.25) | collective-permute-done | bytes 139296 | tf_op jit(solution)/shard_map/ppermute | solution.py:51
  110.8 0.9 collective-permute-done.26
  111.7 1.8 %collective-permute-done.27 = bf16[272,256]{1,0:T(8,128)(2,1)S(1)} collective-permute-done((bf16[272,256]{1,0:T(8,128)(2,1)S(1)}, bf16[272,256]{1,0:T(8,128)(2,1)S(1)}, u32[]{:S(2)}, u32[]{:S(2)}) %collective-permute-start.27) | collective-permute-done | bytes 139296 | tf_op jit(solution)/shard_map/ppermute | solution.py:51
  113.5 2.5 %convolution_convert_fusion.2 = bf16[256,1024]{1,0:T(8,128)(2,1)S(1)} fusion(bf16[1024,1024]{1,0:T(8,128)(2,1)} %fusion.14, bf16[272,1024]{1,0:T(8,128)(2,1)S(1)} %constant_dynamic-update-slice_fusion), kind=kOutput, calls=%fused_computation.55 | convolution fusion | flops 537133056 | bytes 3145728 | tf_op jit(solution)/shard_map/dot_general | solution.py:147
  116.0 0.7 convolution_convert_fusion.1
  116.8 0.8 copy-done.10
  117.6 0.7 convolution_convert_fusion
  118.9 0.6 collective-permute-start.28
  119.4 1.5 %collective-permute-done.28 = f32[128]{0:T(128)S(1)} collective-permute-done((f32[128]{0:T(128)S(1)}, f32[128]{0:T(128)S(1)}, u32[]{:S(2)}, u32[]{:S(2)}) %collective-permute-start.28) | collective-permute-done | bytes 544 | tf_op jit(solution)/shard_map/ppermute | solution.py:155
  121.0 2.9 %fusion.19 = (f32[128,3072]{1,0:T(8,128)}, f32[128,3072]{1,0:T(8,128)}) fusion(f32[128,3072]{1,0:T(8,128)S(1)} %get-tuple-element.100, bf16[128,3072]{1,0:T(8,128)(2,1)S(1)} %collective-permute-done.29, bf16[128,3072]{1,0:T(8,128)(2,1)S(1)} %copy-done.4, f32[128,3072]{1,0:T(8,128)S(1)} %copy-done, bf16[256,3072]{1,0:T(8,128)(2,1)S(1)} %pad_maximum_fusion.1, ...), kind=kLoop, calls=%fused_computation.40 | loop fusion | flops 8650752 | bytes 9454080 | tf_op jit(solution)/shard_map/sub | solution.py:176
  (151 shorter events, 7.4 us)
Async XLA Ops:
  0.6 2.9 %copy-start = (f32[128,3072]{1,0:T(8,128)S(1)}, f32[128,3072]{1,0:T(8,128)}, u32[]{:S(2)}) copy-start(f32[128,3072]{1,0:T(8,128)} %param.19) | copy-start | bytes 4718596
  0.6 2.9 %copy-start.11 = (f32[3072]{0:T(1024)S(1)}, f32[3072]{0:T(1024)}, u32[]{:S(2)}) copy-start(f32[3072]{0:T(1024)} %param.17) | copy-start | bytes 36868
  1.4 2.8 %copy-start.13 = (f32[1024]{0:T(1024)S(1)}, f32[1024]{0:T(1024)}, u32[]{:S(2)}) copy-start(f32[1024]{0:T(1024)} %param.18) | copy-start | bytes 12292
  1.4 2.8 %copy-start.12 = (s32[3072]{0:T(1024)S(1)}, s32[3072]{0:T(1024)}, u32[]{:S(2)}) copy-start(s32[3072]{0:T(1024)} %param.15) | copy-start | bytes 36868
  3.0 2.5 %collective-permute-start = (bf16[128,3072]{1,0:T(8,128)(2,1)S(1)}, bf16[128,3072]{1,0:T(8,128)(2,1)S(1)}, u32[]{:S(2)}, u32[]{:S(2)}) collective-permute-start(bf16[128,3072]{1,0:T(8,128)(2,1)S(1)} %select_convert_fusion), channel_id=1, source_target_pairs={{0,1},{1,0},{2,3},{3,2},{4,5},{5,4},{6,7},{7,6},{8,9},{9,8},{10,11... | collective-permute-start | bytes 2359304 | tf_op jit(solution)/shard_map/ppermute | solution.py:116
  4.3 6.3 %copy-start.16 = (bf16[2048,1024]{1,0:T(8,128)(2,1)S(1)}, bf16[2048,1024]{1,0:T(8,128)(2,1)}, u32[]{:S(2)}) copy-start(bf16[2048,1024]{1,0:T(8,128)(2,1)} %param.14) | copy-start | bytes 12582916
  13.4 12.7 %collective-permute-start.1 = (bf16[272,256]{1,0:T(8,128)(2,1)S(1)}, bf16[272,256]{1,0:T(8,128)(2,1)S(1)}, u32[]{:S(2)}, u32[]{:S(2)}) collective-permute-start(bf16[272,256]{1,0:T(8,128)(2,1)S(1)} %pad_maximum_fusion.4), channel_id=1, source_target_pairs={{0,2},{2,0},{4,6},{6,4},{8,10},{10,8},{12,14},{14,12},{16,18},{18,... | collective-permute-start | bytes 417800 | tf_op jit(solution)/shard_map/ppermute | solution.py:37
  16.3 8.2 %collective-permute-start.3 = (bf16[272,256]{1,0:T(8,128)(2,1)S(1)}, bf16[272,256]{1,0:T(8,128)(2,1)S(1)}, u32[]{:S(2)}, u32[]{:S(2)}) collective-permute-start(bf16[272,256]{1,0:T(8,128)(2,1)S(1)} %pad_maximum_fusion.6), channel_id=1, source_target_pairs={{0,6},{2,4},{4,2},{6,0},{8,14},{10,12},{12,10},{14,8},{16,22},{18,... | collective-permute-start | bytes 417800 | tf_op jit(solution)/shard_map/ppermute | solution.py:37
  17.9 8.2 %collective-permute-start.2 = (bf16[272,256]{1,0:T(8,128)(2,1)S(1)}, bf16[272,256]{1,0:T(8,128)(2,1)S(1)}, u32[]{:S(2)}, u32[]{:S(2)}) collective-permute-start(bf16[272,256]{1,0:T(8,128)(2,1)S(1)} %pad_maximum_fusion.5), channel_id=1, source_target_pairs={{0,4},{2,6},{4,0},{6,2},{8,12},{10,14},{12,8},{14,10},{16,20},{18,... | collective-permute-start | bytes 417800 | tf_op jit(solution)/shard_map/ppermute | solution.py:37
  26.5 10.5 %collective-permute-start.4 = (bf16[272,64]{1,0:T(8,128)(2,1)S(1)}, bf16[272,64]{1,0:T(8,128)(2,1)S(1)}, u32[]{:S(2)}, u32[]{:S(2)}) collective-permute-start(bf16[272,64]{1,0:T(8,128)(2,1)S(1)} %pad_maximum_fusion.10), channel_id=1, source_target_pairs={{0,8},{2,10},{4,12},{6,14},{8,0},{10,2},{12,4},{14,6},{16,24},{18,... | collective-permute-start | bytes 104456 | tf_op jit(solution)/shard_map/ppermute | solution.py:37
  28.2 8.8 %collective-permute-start.6 = (bf16[272,64]{1,0:T(8,128)(2,1)S(1)}, bf16[272,64]{1,0:T(8,128)(2,1)S(1)}, u32[]{:S(2)}, u32[]{:S(2)}) collective-permute-start(bf16[272,64]{1,0:T(8,128)(2,1)S(1)} %pad_maximum_fusion.12), channel_id=1, source_target_pairs={{0,24},{2,26},{4,28},{6,30},{8,16},{10,18},{12,20},{14,22},{16,8},... | collective-permute-start | bytes 104456 | tf_op jit(solution)/shard_map/ppermute | solution.py:37
  30.8 6.2 %collective-permute-start.5 = (bf16[272,64]{1,0:T(8,128)(2,1)S(1)}, bf16[272,64]{1,0:T(8,128)(2,1)S(1)}, u32[]{:S(2)}, u32[]{:S(2)}) collective-permute-start(bf16[272,64]{1,0:T(8,128)(2,1)S(1)} %pad_maximum_fusion.11), channel_id=1, source_target_pairs={{0,16},{2,18},{4,20},{6,22},{8,24},{10,26},{12,28},{14,30},{16,0},... | collective-permute-start | bytes 104456 | tf_op jit(solution)/shard_map/ppermute | solution.py:37
  37.3 10.8 %collective-permute-start.7 = (bf16[272,64]{1,0:T(8,128)(2,1)S(1)}, bf16[272,64]{1,0:T(8,128)(2,1)S(1)}, u32[]{:S(2)}, u32[]{:S(2)}) collective-permute-start(bf16[272,64]{1,0:T(8,128)(2,1)S(1)} %pad_maximum_fusion.13), channel_id=1, source_target_pairs={{0,8},{2,10},{4,12},{6,14},{8,0},{10,2},{12,4},{14,6},{16,24},{18,... | collective-permute-start | bytes 104456 | tf_op jit(solution)/shard_map/ppermute | solution.py:51
  39.0 9.0 %collective-permute-start.8 = (bf16[272,64]{1,0:T(8,128)(2,1)S(1)}, bf16[272,64]{1,0:T(8,128)(2,1)S(1)}, u32[]{:S(2)}, u32[]{:S(2)}) collective-permute-start(bf16[272,64]{1,0:T(8,128)(2,1)S(1)} %pad_maximum_fusion.13), channel_id=1, source_target_pairs={{0,16},{2,18},{4,20},{6,22},{8,24},{10,26},{12,28},{14,30},{16,0},... | collective-permute-start | bytes 104456 | tf_op jit(solution)/shard_map/ppermute | solution.py:51
  40.7 7.3 %collective-permute-start.9 = (bf16[272,64]{1,0:T(8,128)(2,1)S(1)}, bf16[272,64]{1,0:T(8,128)(2,1)S(1)}, u32[]{:S(2)}, u32[]{:S(2)}) collective-permute-start(bf16[272,64]{1,0:T(8,128)(2,1)S(1)} %pad_maximum_fusion.13), channel_id=1, source_target_pairs={{0,24},{2,26},{4,28},{6,30},{8,16},{10,18},{12,20},{14,22},{16,8},... | collective-permute-start | bytes 104456 | tf_op jit(solution)/shard_map/ppermute | solution.py:51
  49.6 5.8 %collective-permute-start.10 = (bf16[272,256]{1,0:T(8,128)(2,1)S(1)}, bf16[272,256]{1,0:T(8,128)(2,1)S(1)}, u32[]{:S(2)}, u32[]{:S(2)}) collective-permute-start(bf16[272,256]{1,0:T(8,128)(2,1)S(1)} %dynamic_update_slice.51), channel_id=1, source_target_pairs={{0,2},{2,0},{4,6},{6,4},{8,10},{10,8},{12,14},{14,12},{16,18},{18,... | collective-permute-start | bytes 417800 | tf_op jit(solution)/shard_map/ppermute | solution.py:51
  51.2 5.1 %collective-permute-start.11 = (bf16[272,256]{1,0:T(8,128)(2,1)S(1)}, bf16[272,256]{1,0:T(8,128)(2,1)S(1)}, u32[]{:S(2)}, u32[]{:S(2)}) collective-permute-start(bf16[272,256]{1,0:T(8,128)(2,1)S(1)} %dynamic_update_slice.51), channel_id=1, source_target_pairs={{0,4},{2,6},{4,0},{6,2},{8,12},{10,14},{12,8},{14,10},{16,20},{18,... | collective-permute-start | bytes 417800 | tf_op jit(solution)/shard_map/ppermute | solution.py:51
  51.7 6.0 %collective-permute-start.12 = (bf16[272,256]{1,0:T(8,128)(2,1)S(1)}, bf16[272,256]{1,0:T(8,128)(2,1)S(1)}, u32[]{:S(2)}, u32[]{:S(2)}) collective-permute-start(bf16[272,256]{1,0:T(8,128)(2,1)S(1)} %dynamic_update_slice.51), channel_id=1, source_target_pairs={{0,6},{2,4},{4,2},{6,0},{8,14},{10,12},{12,10},{14,8},{16,22},{18,... | collective-permute-start | bytes 417800 | tf_op jit(solution)/shard_map/ppermute | solution.py:51
  57.7 2.5 %copy-start.6 = (bf16[1024,1024]{1,0:T(8,128)(2,1)S(1)}, bf16[1024,1024]{1,0:T(8,128)(2,1)}, u32[]{:S(2)}) copy-start(bf16[1024,1024]{1,0:T(8,128)(2,1)} %fusion.13) | copy-start | bytes 6291460
  60.2 1.6 %copy-start.8 = (bf16[1024,1024]{1,0:T(8,128)(2,1)S(1)}, bf16[1024,1024]{1,0:T(8,128)(2,1)}, u32[]{:S(2)}) copy-start(bf16[1024,1024]{1,0:T(8,128)(2,1)} %fusion.12) | copy-start | bytes 6291460
  62.7 3.4 %copy-start.1 = (bf16[256,3072]{1,0:T(8,128)(2,1)}, bf16[256,3072]{1,0:T(8,128)(2,1)S(1)}, u32[]{:S(2)}) copy-start(bf16[256,3072]{1,0:T(8,128)(2,1)S(1)} %pad_maximum_fusion) | copy-start | bytes 4718596
  62.8 2.4 %collective-permute-start.14 = (bf16[128,3072]{1,0:T(8,128)(2,1)S(1)}, bf16[128,3072]{1,0:T(8,128)(2,1)S(1)}, u32[]{:S(2)}, u32[]{:S(2)}) collective-permute-start(bf16[128,3072]{1,0:T(8,128)(2,1)S(1)} %slice.458), channel_id=1, source_target_pairs={{0,1},{1,0},{2,3},{3,2},{4,5},{5,4},{6,7},{7,6},{8,9},{9,8},{10,11... | collective-permute-start | bytes 2359304 | tf_op jit(solution)/shard_map/ppermute | solution.py:156
  63.1 2.0 %collective-permute-start.13 = (f32[128]{0:T(128)S(1)}, f32[128]{0:T(128)S(1)}, u32[]{:S(2)}, u32[]{:S(2)}) collective-permute-start(f32[128]{0:T(128)S(1)} %slice.395), channel_id=1, source_target_pairs={{0,1},{1,0},{2,3},{3,2},{4,5},{5,4},{6,7},{7,6},{8,9},{9,8},{10,11... | collective-permute-start | bytes 1544 | tf_op jit(solution)/shard_map/ppermute | solution.py:155
  65.1 1.0 copy-start.14
  65.1 1.0 copy-start.3
  67.1 2.6 %collective-permute-start.15 = (bf16[128,3072]{1,0:T(8,128)(2,1)}, bf16[128,3072]{1,0:T(8,128)(2,1)}, u32[]{:S(2)}, u32[]{:S(2)}) collective-permute-start(bf16[128,3072]{1,0:T(8,128)(2,1)} %convert_element_type.378), channel_id=1, source_target_pairs={{0,1},{1,0},{2,3},{3,2},{4,5},{5,4},{6,7},{7,6},{8,9},{9,8},{10,11... | collective-permute-start | bytes 2359304 | tf_op jit(solution)/shard_map/ppermute | solution.py:116
  67.6 4.6 %copy-start.9 = (bf16[1024,1024]{1,0:T(8,128)(2,1)S(1)}, bf16[1024,1024]{1,0:T(8,128)(2,1)}, u32[]{:S(2)}) copy-start(bf16[1024,1024]{1,0:T(8,128)(2,1)} %fusion.12) | copy-start | bytes 6291460
  72.2 1.9 %copy-start.5 = (bf16[1024,1024]{1,0:T(8,128)(2,1)S(1)}, bf16[1024,1024]{1,0:T(8,128)(2,1)}, u32[]{:S(2)}) copy-start(bf16[1024,1024]{1,0:T(8,128)(2,1)} %fusion.14) | copy-start | bytes 6291460
  76.1 7.5 %collective-permute-start.18 = (bf16[272,256]{1,0:T(8,128)(2,1)S(1)}, bf16[272,256]{1,0:T(8,128)(2,1)S(1)}, u32[]{:S(2)}, u32[]{:S(2)}) collective-permute-start(bf16[272,256]{1,0:T(8,128)(2,1)S(1)} %pad_maximum_fusion.9), channel_id=1, source_target_pairs={{0,6},{2,4},{4,2},{6,0},{8,14},{10,12},{12,10},{14,8},{16,22},{18,... | collective-permute-start | bytes 417800 | tf_op jit(solution)/shard_map/ppermute | solution.py:37
  77.6 8.2 %collective-permute-start.17 = (bf16[272,256]{1,0:T(8,128)(2,1)S(1)}, bf16[272,256]{1,0:T(8,128)(2,1)S(1)}, u32[]{:S(2)}, u32[]{:S(2)}) collective-permute-start(bf16[272,256]{1,0:T(8,128)(2,1)S(1)} %pad_maximum_fusion.8), channel_id=1, source_target_pairs={{0,4},{2,6},{4,0},{6,2},{8,12},{10,14},{12,8},{14,10},{16,20},{18,... | collective-permute-start | bytes 417800 | tf_op jit(solution)/shard_map/ppermute | solution.py:37
  78.3 7.5 %collective-permute-start.16 = (bf16[272,256]{1,0:T(8,128)(2,1)S(1)}, bf16[272,256]{1,0:T(8,128)(2,1)S(1)}, u32[]{:S(2)}, u32[]{:S(2)}) collective-permute-start(bf16[272,256]{1,0:T(8,128)(2,1)S(1)} %pad_maximum_fusion.7), channel_id=1, source_target_pairs={{0,2},{2,0},{4,6},{6,4},{8,10},{10,8},{12,14},{14,12},{16,18},{18,... | collective-permute-start | bytes 417800 | tf_op jit(solution)/shard_map/ppermute | solution.py:37
  86.2 6.9 %collective-permute-start.21 = (bf16[272,64]{1,0:T(8,128)(2,1)S(1)}, bf16[272,64]{1,0:T(8,128)(2,1)S(1)}, u32[]{:S(2)}, u32[]{:S(2)}) collective-permute-start(bf16[272,64]{1,0:T(8,128)(2,1)S(1)} %pad_maximum_fusion.16), channel_id=1, source_target_pairs={{0,24},{2,26},{4,28},{6,30},{8,16},{10,18},{12,20},{14,22},{16,8},... | collective-permute-start | bytes 104456 | tf_op jit(solution)/shard_map/ppermute | solution.py:37
  89.1 6.2 %collective-permute-start.20 = (bf16[272,64]{1,0:T(8,128)(2,1)S(1)}, bf16[272,64]{1,0:T(8,128)(2,1)S(1)}, u32[]{:S(2)}, u32[]{:S(2)}) collective-permute-start(bf16[272,64]{1,0:T(8,128)(2,1)S(1)} %pad_maximum_fusion.15), channel_id=1, source_target_pairs={{0,16},{2,18},{4,20},{6,22},{8,24},{10,26},{12,28},{14,30},{16,0},... | collective-permute-start | bytes 104456 | tf_op jit(solution)/shard_map/ppermute | solution.py:37
  89.2 6.2 %collective-permute-start.19 = (bf16[272,64]{1,0:T(8,128)(2,1)S(1)}, bf16[272,64]{1,0:T(8,128)(2,1)S(1)}, u32[]{:S(2)}, u32[]{:S(2)}) collective-permute-start(bf16[272,64]{1,0:T(8,128)(2,1)S(1)} %pad_maximum_fusion.14), channel_id=1, source_target_pairs={{0,8},{2,10},{4,12},{6,14},{8,0},{10,2},{12,4},{14,6},{16,24},{18,... | collective-permute-start | bytes 104456 | tf_op jit(solution)/shard_map/ppermute | solution.py:37
  95.6 5.2 %collective-permute-start.22 = (bf16[272,64]{1,0:T(8,128)(2,1)S(1)}, bf16[272,64]{1,0:T(8,128)(2,1)}, u32[]{:S(2)}, u32[]{:S(2)}) collective-permute-start(bf16[272,64]{1,0:T(8,128)(2,1)S(1)} %pad_maximum_fusion.17), channel_id=1, source_target_pairs={{0,8},{2,10},{4,12},{6,14},{8,0},{10,2},{12,4},{14,6},{16,24},{18,... | collective-permute-start | bytes 104456 | tf_op jit(solution)/shard_map/ppermute | solution.py:51
  96.5 7.7 %collective-permute-start.23 = (bf16[272,64]{1,0:T(8,128)(2,1)S(1)}, bf16[272,64]{1,0:T(8,128)(2,1)S(1)}, u32[]{:S(2)}, u32[]{:S(2)}) collective-permute-start(bf16[272,64]{1,0:T(8,128)(2,1)S(1)} %pad_maximum_fusion.17), channel_id=1, source_target_pairs={{0,16},{2,18},{4,20},{6,22},{8,24},{10,26},{12,28},{14,30},{16,0},... | collective-permute-start | bytes 104456 | tf_op jit(solution)/shard_map/ppermute | solution.py:51
  98.7 6.2 %collective-permute-start.24 = (bf16[272,64]{1,0:T(8,128)(2,1)S(1)}, bf16[272,64]{1,0:T(8,128)(2,1)S(1)}, u32[]{:S(2)}, u32[]{:S(2)}) collective-permute-start(bf16[272,64]{1,0:T(8,128)(2,1)S(1)} %pad_maximum_fusion.17), channel_id=1, source_target_pairs={{0,24},{2,26},{4,28},{6,30},{8,16},{10,18},{12,20},{14,22},{16,8},... | collective-permute-start | bytes 104456 | tf_op jit(solution)/shard_map/ppermute | solution.py:51
  105.5 5.3 %collective-permute-start.25 = (bf16[272,256]{1,0:T(8,128)(2,1)S(1)}, bf16[272,256]{1,0:T(8,128)(2,1)S(1)}, u32[]{:S(2)}, u32[]{:S(2)}) collective-permute-start(bf16[272,256]{1,0:T(8,128)(2,1)S(1)} %dynamic_update_slice.59), channel_id=1, source_target_pairs={{0,2},{2,0},{4,6},{6,4},{8,10},{10,8},{12,14},{14,12},{16,18},{18,... | collective-permute-start | bytes 417800 | tf_op jit(solution)/shard_map/ppermute | solution.py:51
  106.1 5.6 %collective-permute-start.26 = (bf16[272,256]{1,0:T(8,128)(2,1)S(1)}, bf16[272,256]{1,0:T(8,128)(2,1)S(1)}, u32[]{:S(2)}, u32[]{:S(2)}) collective-permute-start(bf16[272,256]{1,0:T(8,128)(2,1)S(1)} %dynamic_update_slice.59), channel_id=1, source_target_pairs={{0,4},{2,6},{4,0},{6,2},{8,12},{10,14},{12,8},{14,10},{16,20},{18,... | collective-permute-start | bytes 417800 | tf_op jit(solution)/shard_map/ppermute | solution.py:51
  107.5 6.0 %collective-permute-start.27 = (bf16[272,256]{1,0:T(8,128)(2,1)S(1)}, bf16[272,256]{1,0:T(8,128)(2,1)S(1)}, u32[]{:S(2)}, u32[]{:S(2)}) collective-permute-start(bf16[272,256]{1,0:T(8,128)(2,1)S(1)} %dynamic_update_slice.59), channel_id=1, source_target_pairs={{0,6},{2,4},{4,2},{6,0},{8,14},{10,12},{12,10},{14,8},{16,22},{18,... | collective-permute-start | bytes 417800 | tf_op jit(solution)/shard_map/ppermute | solution.py:51
  113.5 2.5 %copy-start.7 = (bf16[1024,1024]{1,0:T(8,128)(2,1)S(1)}, bf16[1024,1024]{1,0:T(8,128)(2,1)}, u32[]{:S(2)}) copy-start(bf16[1024,1024]{1,0:T(8,128)(2,1)} %fusion.13) | copy-start | bytes 6291460
  116.0 1.6 %copy-start.10 = (bf16[1024,1024]{1,0:T(8,128)(2,1)S(1)}, bf16[1024,1024]{1,0:T(8,128)(2,1)}, u32[]{:S(2)}) copy-start(bf16[1024,1024]{1,0:T(8,128)(2,1)} %fusion.12) | copy-start | bytes 6291460
  118.4 2.6 %copy-start.4 = (bf16[128,3072]{1,0:T(8,128)(2,1)S(1)}, bf16[128,3072]{1,0:T(8,128)(2,1)}, u32[]{:S(2)}) copy-start(bf16[128,3072]{1,0:T(8,128)(2,1)} %copy-done.3) | copy-start | bytes 2359300
  118.5 2.4 %copy-start.15 = (f32[128]{0:T(128)S(1)}, f32[128]{0:T(128)}, u32[]{:S(2)}) copy-start(f32[128]{0:T(128)} %copy-done.14) | copy-start | bytes 1540
  118.5 2.5 %copy-start.2 = (bf16[256,3072]{1,0:T(8,128)(2,1)S(1)}, bf16[256,3072]{1,0:T(8,128)(2,1)}, u32[]{:S(2)}) copy-start(bf16[256,3072]{1,0:T(8,128)(2,1)} %copy-done.1) | copy-start | bytes 4718596
  118.6 2.4 %collective-permute-start.29 = (bf16[128,3072]{1,0:T(8,128)(2,1)S(1)}, bf16[128,3072]{1,0:T(8,128)(2,1)S(1)}, u32[]{:S(2)}, u32[]{:S(2)}) collective-permute-start(bf16[128,3072]{1,0:T(8,128)(2,1)S(1)} %slice.495), channel_id=1, source_target_pairs={{0,1},{1,0},{2,3},{3,2},{4,5},{5,4},{6,7},{7,6},{8,9},{9,8},{10,11... | collective-permute-start | bytes 2359304 | tf_op jit(solution)/shard_map/ppermute | solution.py:156
  118.9 2.0 %collective-permute-start.28 = (f32[128]{0:T(128)S(1)}, f32[128]{0:T(128)S(1)}, u32[]{:S(2)}, u32[]{:S(2)}) collective-permute-start(f32[128]{0:T(128)S(1)} %slice.439), channel_id=1, source_target_pairs={{0,1},{1,0},{2,3},{3,2},{4,5},{5,4},{6,7},{7,6},{8,9},{9,8},{10,11... | collective-permute-start | bytes 1544 | tf_op jit(solution)/shard_map/ppermute | solution.py:155

commit v3 on v1

--- a/solution.py
+++ b/solution.py
@@ -112,14 +112,17 @@
 
         def operate(vector, first=False):
             lowered = vector.astype(jnp.bfloat16)
-            if pair:
-                rows = jnp.concatenate([lowered, lax.ppermute(lowered, "eig", swap)], 0)
+            project = coeff_from_table if first else (
+                lambda rows: jnp.dot(rows, built[0], preferred_element_type=jnp.float32)
+            )
+            if pair and not first:
+                coeff = jnp.concatenate(
+                    [project(lowered), project(lax.ppermute(lowered, "eig", swap))], 0
+                )
+            elif pair:
+                coeff = project(jnp.concatenate([lowered, lax.ppermute(lowered, "eig", swap)], 0))
             else:
-                rows = lax.all_gather(lowered, "eig", axis=0, tiled=True)
-            if first:
-                coeff = coeff_from_table(rows)
-            else:
-                coeff = jnp.dot(rows, built[0], preferred_element_type=jnp.float32)
+                coeff = project(lax.all_gather(lowered, "eig", axis=0, tiled=True))
             sums = jnp.zeros((8, group), jnp.float32)
             sums = sums.at[0, :own].set(jnp.sum(vector * vector, axis=1))
             sums = sums.at[1, :own].set(jnp.sum(noise_var[None, :] * vector * vector, axis=1))
@@ -140,15 +143,17 @@
             ].astype(jnp.float32)
             wide = weights.astype(jnp.float32)
             energy = jnp.sum(wide * wide / spectrum[None, :], axis=1)
-            partials = lax.dot_general(
-                weights, features, (((1,), (1,)), ((), ())), preferred_element_type=jnp.float32
-            ).astype(jnp.bfloat16)
+            def image_of(rows):
+                return lax.dot_general(
+                    rows, features, (((1,), (1,)), ((), ())), preferred_element_type=jnp.float32
+                ).astype(jnp.bfloat16)
+
             if pair:
                 energy = energy[:own] + lax.ppermute(energy[own:], "eig", swap)
-                image = partials[:own].astype(jnp.float32) + lax.ppermute(
-                    partials[own:], "eig", swap
-                ).astype(jnp.float32)
+                theirs = lax.ppermute(image_of(weights[own:]), "eig", swap)
+                image = image_of(weights[:own]).astype(jnp.float32) + theirs.astype(jnp.float32)
             else:
+                partials = image_of(weights)
                 energy = lax.psum_scatter(energy, "eig", scatter_dimension=0, tiled=True)
                 image = lax.psum_scatter(
                     partials, "eig", scatter_dimension=0, tiled=True

time: 124 us -> 141 us (1.14)
  matrix products: 37.8 us -> 54.4 us
  waiting for transfers between devices: 26.9 us -> 29.9 us
  other arithmetic: 8.79 us -> 6.62 us
    dot_general x3 -> x6, matrix products: 14.4 us -> 31 us  [the longest x4 22.9 us: image_of(): lax.dot_general(rows, features, (((1,), (1,)), ((), ())), preferred_eleme...]
    ppermute x12, waiting for transfers between devices: 14.3 us -> 18 us  [vert_sum(): lax.ppermute(send, 'vert', [(i, i ^ masks[t + 1]) for i in range(n_vert)])]
    sub x1 -> x0, other arithmetic: 2.94 us -> none  [shards(): residual = residual - step_size[:, None] * along]
    ppermute x12, waiting for transfers between devices: 6.46 us -> 8.7 us  [vert_sum(): lax.ppermute(cur, 'vert', [(i, i ^ masks[t]) for i in range(n_vert)])]
    ppermute x4, waiting for transfers between devices: 3.26 us -> 1.17 us  [the longest x2 1.16 us: operate(): lax.ppermute(lowered, 'eig', swap)]
    add x0 -> x1, other arithmetic: none -> 1.57 us  [shards(): solution = solution + step_size[:, None] * direction]
    unnamed x26 -> x18, local copies, waits for them, and re-layouts: 3.57 us -> 3.59 us
  transfers between devices with their start and end apart: 30 -> 30, of which waited for: 15 -> 18; matrix products, arithmetic and copies ran while one was open for 19% -> 22% of each run, Pallas kernels for 0% -> 0%
where the time goes in v3:
time: 141 us
  matrix products  54.4 us (39%)
  starting transfers between devices  35.1 us (25%)
  waiting for transfers between devices  29.9 us (21%)
  local copies, waits for them, and re-layouts  12.6 us (9%)
  other arithmetic  6.62 us (5%)
  between operations  2.25 us (2%)
    dot_general x4, matrix products, image_of(): lax.dot_general(rows, features, (((1,), (1,)), ((), ())), preferred_eleme...  22.9 us
    ppermute x12, waiting for transfers between devices, vert_sum(): lax.ppermute(send, 'vert', [(i, i ^ masks[t + 1]) for i in range(n_vert)])  18 us
    ppermute x12, starting transfers between devices, vert_sum(): lax.ppermute(send, 'vert', [(i, i ^ masks[t + 1]) for i in range(n_vert)])  17.2 us
    ppermute x12, starting transfers between devices, vert_sum(): lax.ppermute(cur, 'vert', [(i, i ^ masks[t]) for i in range(n_vert)])  16 us
    dot_general x3, matrix products, work(): jnp.dot(rows, eig_table, preferred_element_type=jnp.float32)  16 us
    ppermute x12, waiting for transfers between devices, vert_sum(): lax.ppermute(cur, 'vert', [(i, i ^ masks[t]) for i in range(n_vert)])  8.7 us
    dot_general x2, matrix products, operate(): jnp.dot(rows, built[0], preferred_element_type=jnp.float32)  8.05 us
    dot_general x1, matrix products, coeff_from_table(): summed = jnp.dot(rows, picker, preferred_element_type=jnp.float32)  5.09 us
  transfers between devices with their start and end apart: 30, of which 18 were waited for; matrix products, arithmetic and copies ran while one was open for 22% of the time, Pallas kernels for 0%

profile of v3, /device:TPU:0, one launch (start us, length us, event | category | flops | bytes accessed | tf_op | source)
XLA Modules:
  0.0 141.0 jit_solution(11316312774581570942)
XLA Ops:
  1.4 1.5 %select_convert_fusion = bf16[128,3072]{1,0:T(8,128)(2,1)S(1)} fusion(f32[128,3072]{1,0:T(8,128)} %param.19, pred[3072]{0:T(1024)(128)(4,1)S(1)} %iota_compare_fusion.14), kind=kLoop, calls=%fused_computation.54 | loop fusion | flops 393216 | bytes 2362368 | tf_op jit(solution)/shard_map/convert_element_type | solution.py:114
  3.0 0.6 collective-permute-start
  3.5 0.4 fusion.26
  4.3 1.2 collective-permute-done
  5.5 5.1 %subtract_convert_fusion = (bf16[256,2048]{1,0:T(8,128)(2,1)S(1)}, bf16[256,2048]{1,0:T(8,128)(2,1)S(1)}) fusion(s32[3072]{0:T(1024)S(1)} %copy-done.3, bf16[128,3072]{1,0:T(8,128)(2,1)S(1)} %collective-permute-done, bf16[128,3072]{1,0:T(8,128)(2,1)S(1)} %select_convert_fusion), kind=kOutput, calls=%fused_computation.41 | convolution fusion | flops 3232759808 | bytes 3682304 | tf_op jit(solution)/shard_map/dot_general | solution.py:86
  10.6 2.4 %fusion.19 = f32[512,1024]{1,0:T(8,128)S(1)} fusion(bf16[2048,1024]{1,0:T(8,128)(2,1)S(1)} %copy-done.7, bf16[256,2048]{1,0:T(8,128)(2,1)S(1)} %get-tuple-element.115, bf16[256,2048]{1,0:T(8,128)(2,1)S(1)} %get-tuple-element.116), kind=kOutput, calls=%fused_computation.37 | convolution fusion | flops 2151677952 | bytes 8388608 | tf_op jit(solution)/shard_map/dot_general | solution.py:89
  13.4 2.9 %collective-permute-start.1 = (bf16[272,256]{1,0:T(8,128)(2,1)S(1)}, bf16[272,256]{1,0:T(8,128)(2,1)S(1)}, u32[]{:S(2)}, u32[]{:S(2)}) collective-permute-start(bf16[272,256]{1,0:T(8,128)(2,1)S(1)} %pad_maximum_fusion), channel_id=1, source_target_pairs={{0,2},{2,0},{4,6},{6,4},{8,10},{10,8},{12,14},{14,12},{16,18},{18,... | collective-permute-start | bytes 417800 | tf_op jit(solution)/shard_map/ppermute | solution.py:37
  16.3 1.6 %collective-permute-start.3 = (bf16[272,256]{1,0:T(8,128)(2,1)S(1)}, bf16[272,256]{1,0:T(8,128)(2,1)S(1)}, u32[]{:S(2)}, u32[]{:S(2)}) collective-permute-start(bf16[272,256]{1,0:T(8,128)(2,1)S(1)} %pad_maximum_fusion.2), channel_id=1, source_target_pairs={{0,6},{2,4},{4,2},{6,0},{8,14},{10,12},{12,10},{14,8},{16,22},{18,... | collective-permute-start | bytes 417800 | tf_op jit(solution)/shard_map/ppermute | solution.py:37
  18.0 5.0 %fusion.25 = bf16[1024,1024]{1,0:T(8,128)(2,1)S(1)} fusion(bf16[2048,1024]{1,0:T(8,128)(2,1)S(1)} %copy-done.7, s32[1024]{0:T(1024)S(1)} %get-tuple-element.65), kind=kOutput, calls=%fused_computation.44 | convolution fusion | flops 4298113024 | bytes 6295552 | tf_op jit(solution)/shard_map/dot_general | solution.py:79
  23.0 1.6 %collective-permute-done.3 = bf16[272,256]{1,0:T(8,128)(2,1)S(1)} collective-permute-done((bf16[272,256]{1,0:T(8,128)(2,1)S(1)}, bf16[272,256]{1,0:T(8,128)(2,1)S(1)}, u32[]{:S(2)}, u32[]{:S(2)}) %collective-permute-start.3) | collective-permute-done | bytes 139296 | tf_op jit(solution)/shard_map/ppermute | solution.py:37
  24.6 1.5 %collective-permute-done.2 = bf16[272,256]{1,0:T(8,128)(2,1)S(1)} collective-permute-done((bf16[272,256]{1,0:T(8,128)(2,1)S(1)}, bf16[272,256]{1,0:T(8,128)(2,1)S(1)}, u32[]{:S(2)}, u32[]{:S(2)}) %collective-permute-start.2) | collective-permute-done | bytes 139296 | tf_op jit(solution)/shard_map/ppermute | solution.py:37
  26.5 1.6 %collective-permute-start.4 = (bf16[272,64]{1,0:T(8,128)(2,1)S(1)}, bf16[272,64]{1,0:T(8,128)(2,1)S(1)}, u32[]{:S(2)}, u32[]{:S(2)}) collective-permute-start(bf16[272,64]{1,0:T(8,128)(2,1)S(1)} %pad_maximum_fusion.6), channel_id=1, source_target_pairs={{0,8},{2,10},{4,12},{6,14},{8,0},{10,2},{12,4},{14,6},{16,24},{18,... | collective-permute-start | bytes 104456 | tf_op jit(solution)/shard_map/ppermute | solution.py:37
  28.2 5.0 %fusion.24 = bf16[1024,1024]{1,0:T(8,128)(2,1)S(1)} fusion(bf16[2048,1024]{1,0:T(8,128)(2,1)S(1)} %copy-done.7, s32[1024]{0:T(1024)S(1)} %get-tuple-element.69), kind=kOutput, calls=%fused_computation.43 | convolution fusion | flops 4298113024 | bytes 6295552 | tf_op jit(solution)/shard_map/dot_general | solution.py:79
  33.2 2.5 %collective-permute-start.6 = (bf16[272,64]{1,0:T(8,128)(2,1)S(1)}, bf16[272,64]{1,0:T(8,128)(2,1)S(1)}, u32[]{:S(2)}, u32[]{:S(2)}) collective-permute-start(bf16[272,64]{1,0:T(8,128)(2,1)S(1)} %pad_maximum_fusion.8), channel_id=1, source_target_pairs={{0,24},{2,26},{4,28},{6,30},{8,16},{10,18},{12,20},{14,22},{16,8},... | collective-permute-start | bytes 104456 | tf_op jit(solution)/shard_map/ppermute | solution.py:37
  35.9 1.5 %constant_dynamic-update-slice_fusion.2 = bf16[3072,1024]{1,0:T(8,128)(2,1)} fusion(bf16[1024,1024]{1,0:T(8,128)(2,1)S(1)} %fusion.25), kind=kLoop, calls=%fused_computation.139 | loop fusion | bytes 4194304
  37.4 2.1 %collective-permute-done.6 = bf16[272,64]{1,0:T(8,128)(2,1)S(1)} collective-permute-done((bf16[272,64]{1,0:T(8,128)(2,1)S(1)}, bf16[272,64]{1,0:T(8,128)(2,1)S(1)}, u32[]{:S(2)}, u32[]{:S(2)}) %collective-permute-start.6) | collective-permute-done | bytes 34848 | tf_op jit(solution)/shard_map/ppermute | solution.py:37
  39.6 2.3 %collective-permute-done.5 = bf16[272,64]{1,0:T(8,128)(2,1)S(1)} collective-permute-done((bf16[272,64]{1,0:T(8,128)(2,1)S(1)}, bf16[272,64]{1,0:T(8,128)(2,1)S(1)}, u32[]{:S(2)}, u32[]{:S(2)}) %collective-permute-start.5) | collective-permute-done | bytes 34848 | tf_op jit(solution)/shard_map/ppermute | solution.py:37
  42.2 2.9 %collective-permute-start.8 = (bf16[272,64]{1,0:T(8,128)(2,1)S(1)}, bf16[272,64]{1,0:T(8,128)(2,1)S(1)}, u32[]{:S(2)}, u32[]{:S(2)}) collective-permute-start(bf16[272,64]{1,0:T(8,128)(2,1)S(1)} %pad_maximum_fusion.9), channel_id=1, source_target_pairs={{0,16},{2,18},{4,20},{6,22},{8,24},{10,26},{12,28},{14,30},{16,0},... | collective-permute-start | bytes 104456 | tf_op jit(solution)/shard_map/ppermute | solution.py:51
  45.1 1.4 %collective-permute-start.9 = (bf16[272,64]{1,0:T(8,128)(2,1)S(1)}, bf16[272,64]{1,0:T(8,128)(2,1)S(1)}, u32[]{:S(2)}, u32[]{:S(2)}) collective-permute-start(bf16[272,64]{1,0:T(8,128)(2,1)S(1)} %pad_maximum_fusion.9), channel_id=1, source_target_pairs={{0,24},{2,26},{4,28},{6,30},{8,16},{10,18},{12,20},{14,22},{16,8},... | collective-permute-start | bytes 104456 | tf_op jit(solution)/shard_map/ppermute | solution.py:51
  46.6 6.1 %fusion.23 = bf16[1024,1024]{1,0:T(8,128)(2,1)} fusion(bf16[2048,1024]{1,0:T(8,128)(2,1)S(1)} %copy-done.7, s32[1024]{0:T(1024)S(1)} %get-tuple-element.73), kind=kOutput, calls=%fused_computation.42 | convolution fusion | flops 4298113024 | bytes 6295552 | tf_op jit(solution)/shard_map/dot_general | solution.py:79
  52.6 1.5 %constant_dynamic-update-slice_fusion.1 = bf16[3072,1024]{1,0:T(8,128)(2,1)} fusion(bf16[3072,1024]{1,0:T(8,128)(2,1)} %constant_dynamic-update-slice_fusion.2, bf16[1024,1024]{1,0:T(8,128)(2,1)S(1)} %fusion.24), kind=kLoop, calls=%fused_computation.138 | loop fusion | bytes 4194304
  54.5 0.6 dynamic_update_slice.49
  55.5 0.8 dynamic_update_slice.51
  56.3 1.6 %collective-permute-start.10 = (bf16[272,256]{1,0:T(8,128)(2,1)S(1)}, bf16[272,256]{1,0:T(8,128)(2,1)S(1)}, u32[]{:S(2)}, u32[]{:S(2)}) collective-permute-start(bf16[272,256]{1,0:T(8,128)(2,1)S(1)} %dynamic_update_slice.51), channel_id=1, source_target_pairs={{0,2},{2,0},{4,6},{6,4},{8,10},{10,8},{12,14},{14,12},{16,18},{18,... | collective-permute-start | bytes 417800 | tf_op jit(solution)/shard_map/ppermute | solution.py:51
  57.8 0.5 collective-permute-start.11
  58.3 1.5 %collective-permute-start.12 = (bf16[272,256]{1,0:T(8,128)(2,1)S(1)}, bf16[272,256]{1,0:T(8,128)(2,1)S(1)}, u32[]{:S(2)}, u32[]{:S(2)}) collective-permute-start(bf16[272,256]{1,0:T(8,128)(2,1)S(1)} %dynamic_update_slice.51), channel_id=1, source_target_pairs={{0,6},{2,4},{4,2},{6,0},{8,14},{10,12},{12,10},{14,8},{16,22},{18,... | collective-permute-start | bytes 417800 | tf_op jit(solution)/shard_map/ppermute | solution.py:51
  59.8 3.1 %constant_dynamic-update-slice_fusion = bf16[3072,1024]{1,0:T(8,128)(2,1)} fusion(bf16[3072,1024]{1,0:T(8,128)(2,1)} %constant_dynamic-update-slice_fusion.1, bf16[1024,1024]{1,0:T(8,128)(2,1)} %fusion.23), kind=kLoop, calls=%fused_computation.137 | loop fusion | bytes 4194304 | tf_op jit(solution)/shard_map/concatenate | solution.py:138
  63.1 1.3 collective-permute-done.11
  64.5 5.0 %convolution_convert_fusion.2 = bf16[128,3072]{1,0:T(8,128)(2,1)S(1)} fusion(bf16[3072,1024]{1,0:T(8,128)(2,1)} %constant_dynamic-update-slice_fusion, bf16[272,1024]{1,0:T(8,128)(2,1)S(1)} %constant_dynamic-update-slice_fusion.7), kind=kOutput, calls=%fused_computation.21 | convolution fusion | flops 805699584 | bytes 7340032 | tf_op jit(solution)/shard_map/dot_general | solution.py:147
  69.7 0.6 collective-permute-start.13
  70.3 1.5 %collective-permute-done.13 = f32[128]{0:T(128)S(1)} collective-permute-done((f32[128]{0:T(128)S(1)}, f32[128]{0:T(128)S(1)}, u32[]{:S(2)}, u32[]{:S(2)}) %collective-permute-start.13) | collective-permute-done | bytes 544 | tf_op jit(solution)/shard_map/ppermute | solution.py:152
  71.8 0.5 copy-done.5
  72.3 6.5 %fusion.27 = (f32[128]{0:T(128)S(1)}, f32[128]{0:T(128)S(1)}, f32[128,3072]{1,0:T(8,128)S(1)}, f32[128,3072]{1,0:T(8,128)}) fusion(f32[3072]{0:T(1024)S(1)} %copy-done.2, f32[128]{0:T(128)S(1)} %fusion.61, f32[128,3072]{1,0:T(8,128)S(1)} %copy-done, pred[3072]{0:T(1024)(128)(4,1)S(1)} %iota_compare_fusion.14, ...), kind=kOutput, calls=%fused_computation.46 | convolution fusion | flops 811204352 | bytes 12075520 | tf_op jit(solution)/shard_map/dot_general | solution.py:147
  78.9 1.0 convert_element_type.371
  80.1 4.0 %fusion.66 = f32[128,1024]{1,0:T(8,128)S(1)} fusion(bf16[128,3072]{1,0:T(8,128)(2,1)} %convert_element_type.371, bf16[3072,1024]{1,0:T(8,128)(2,1)} %constant_dynamic-update-slice_fusion), kind=kOutput, calls=%fused_computation.202 | convolution fusion | flops 805306368 | bytes 7602176 | tf_op jit(solution)/shard_map/dot_general | solution.py:116
  84.2 4.0 %fusion.67 = f32[128,1024]{1,0:T(8,128)S(1)} fusion(bf16[128,3072]{1,0:T(8,128)(2,1)} %collective-permute-done.15, bf16[3072,1024]{1,0:T(8,128)(2,1)} %constant_dynamic-update-slice_fusion), kind=kOutput, calls=%fused_computation.203 | convolution fusion | flops 805306368 | bytes 7602176 | tf_op jit(solution)/shard_map/dot_general | solution.py:116
  88.6 1.4 collective-permute-start.18
  90.0 0.7 collective-permute-start.17
  90.7 1.6 %collective-permute-start.16 = (bf16[272,256]{1,0:T(8,128)(2,1)S(1)}, bf16[272,256]{1,0:T(8,128)(2,1)S(1)}, u32[]{:S(2)}, u32[]{:S(2)}) collective-permute-start(bf16[272,256]{1,0:T(8,128)(2,1)S(1)} %pad_maximum_fusion.3), channel_id=1, source_target_pairs={{0,2},{2,0},{4,6},{6,4},{8,10},{10,8},{12,14},{14,12},{16,18},{18,... | collective-permute-start | bytes 417800 | tf_op jit(solution)/shard_map/ppermute | solution.py:37
  92.3 3.8 %collective-permute-done.18 = bf16[272,256]{1,0:T(8,128)(2,1)S(1)} collective-permute-done((bf16[272,256]{1,0:T(8,128)(2,1)S(1)}, bf16[272,256]{1,0:T(8,128)(2,1)S(1)}, u32[]{:S(2)}, u32[]{:S(2)}) %collective-permute-start.18) | collective-permute-done | bytes 139296 | tf_op jit(solution)/shard_map/ppermute | solution.py:37
  96.2 2.3 %collective-permute-done.17 = bf16[272,256]{1,0:T(8,128)(2,1)S(1)} collective-permute-done((bf16[272,256]{1,0:T(8,128)(2,1)S(1)}, bf16[272,256]{1,0:T(8,128)(2,1)S(1)}, u32[]{:S(2)}, u32[]{:S(2)}) %collective-permute-start.17) | collective-permute-done | bytes 139296 | tf_op jit(solution)/shard_map/ppermute | solution.py:37
  98.9 2.7 %collective-permute-start.21 = (bf16[272,64]{1,0:T(8,128)(2,1)S(1)}, bf16[272,64]{1,0:T(8,128)(2,1)S(1)}, u32[]{:S(2)}, u32[]{:S(2)}) collective-permute-start(bf16[272,64]{1,0:T(8,128)(2,1)S(1)} %pad_maximum_fusion.12), channel_id=1, source_target_pairs={{0,24},{2,26},{4,28},{6,30},{8,16},{10,18},{12,20},{14,22},{16,8},... | collective-permute-start | bytes 104456 | tf_op jit(solution)/shard_map/ppermute | solution.py:37
  101.7 1.8 %collective-permute-start.19 = (bf16[272,64]{1,0:T(8,128)(2,1)S(1)}, bf16[272,64]{1,0:T(8,128)(2,1)S(1)}, u32[]{:S(2)}, u32[]{:S(2)}) collective-permute-start(bf16[272,64]{1,0:T(8,128)(2,1)S(1)} %pad_maximum_fusion.10), channel_id=1, source_target_pairs={{0,8},{2,10},{4,12},{6,14},{8,0},{10,2},{12,4},{14,6},{16,24},{18,... | collective-permute-start | bytes 104456 | tf_op jit(solution)/shard_map/ppermute | solution.py:37
  103.5 2.2 %collective-permute-done.21 = bf16[272,64]{1,0:T(8,128)(2,1)S(1)} collective-permute-done((bf16[272,64]{1,0:T(8,128)(2,1)S(1)}, bf16[272,64]{1,0:T(8,128)(2,1)S(1)}, u32[]{:S(2)}, u32[]{:S(2)}) %collective-permute-start.21) | collective-permute-done | bytes 34848 | tf_op jit(solution)/shard_map/ppermute | solution.py:37
  105.7 2.1 %collective-permute-done.20 = bf16[272,64]{1,0:T(8,128)(2,1)S(1)} collective-permute-done((bf16[272,64]{1,0:T(8,128)(2,1)S(1)}, bf16[272,64]{1,0:T(8,128)(2,1)S(1)}, u32[]{:S(2)}, u32[]{:S(2)}) %collective-permute-start.20) | collective-permute-done | bytes 34848 | tf_op jit(solution)/shard_map/ppermute | solution.py:37
  108.1 0.9 collective-permute-start.22
  109.0 2.4 %collective-permute-start.23 = (bf16[272,64]{1,0:T(8,128)(2,1)S(1)}, bf16[272,64]{1,0:T(8,128)(2,1)S(1)}, u32[]{:S(2)}, u32[]{:S(2)}) collective-permute-start(bf16[272,64]{1,0:T(8,128)(2,1)S(1)} %pad_maximum_fusion.13), channel_id=1, source_target_pairs={{0,16},{2,18},{4,20},{6,22},{8,24},{10,26},{12,28},{14,30},{16,0},... | collective-permute-start | bytes 104456 | tf_op jit(solution)/shard_map/ppermute | solution.py:51
  111.3 1.2 collective-permute-start.24
  112.9 0.4 collective-permute-done.22
  113.3 1.4 dynamic_update_slice.57
  114.7 2.0 %collective-permute-done.23 = bf16[272,64]{1,0:T(8,128)(2,1)S(1)} collective-permute-done((bf16[272,64]{1,0:T(8,128)(2,1)S(1)}, bf16[272,64]{1,0:T(8,128)(2,1)S(1)}, u32[]{:S(2)}, u32[]{:S(2)}) %collective-permute-start.23) | collective-permute-done | bytes 34848 | tf_op jit(solution)/shard_map/ppermute | solution.py:51
  117.0 0.5 collective-permute-done.24
  117.6 0.8 dynamic_update_slice.59
  118.4 0.7 collective-permute-start.25
  119.1 1.4 %collective-permute-start.26 = (bf16[272,256]{1,0:T(8,128)(2,1)S(1)}, bf16[272,256]{1,0:T(8,128)(2,1)S(1)}, u32[]{:S(2)}, u32[]{:S(2)}) collective-permute-start(bf16[272,256]{1,0:T(8,128)(2,1)S(1)} %dynamic_update_slice.59), channel_id=1, source_target_pairs={{0,4},{2,6},{4,0},{6,2},{8,12},{10,14},{12,8},{14,10},{16,20},{18,... | collective-permute-start | bytes 417800 | tf_op jit(solution)/shard_map/ppermute | solution.py:51
  120.5 1.4 %collective-permute-start.27 = (bf16[272,256]{1,0:T(8,128)(2,1)S(1)}, bf16[272,256]{1,0:T(8,128)(2,1)S(1)}, u32[]{:S(2)}, u32[]{:S(2)}) collective-permute-start(bf16[272,256]{1,0:T(8,128)(2,1)S(1)} %dynamic_update_slice.59), channel_id=1, source_target_pairs={{0,6},{2,4},{4,2},{6,0},{8,14},{10,12},{12,10},{14,8},{16,22},{18,... | collective-permute-start | bytes 417800 | tf_op jit(solution)/shard_map/ppermute | solution.py:51
  122.0 1.7 %collective-permute-done.25 = bf16[272,256]{1,0:T(8,128)(2,1)S(1)} collective-permute-done((bf16[272,256]{1,0:T(8,128)(2,1)S(1)}, bf16[272,256]{1,0:T(8,128)(2,1)S(1)}, u32[]{:S(2)}, u32[]{:S(2)}) %collective-permute-start.25) | collective-permute-done | bytes 139296 | tf_op jit(solution)/shard_map/ppermute | solution.py:51
  123.7 1.0 collective-permute-done.26
  124.8 1.7 %collective-permute-done.27 = bf16[272,256]{1,0:T(8,128)(2,1)S(1)} collective-permute-done((bf16[272,256]{1,0:T(8,128)(2,1)S(1)}, bf16[272,256]{1,0:T(8,128)(2,1)S(1)}, u32[]{:S(2)}, u32[]{:S(2)}) %collective-permute-start.27) | collective-permute-done | bytes 139296 | tf_op jit(solution)/shard_map/ppermute | solution.py:51
  126.5 5.0 %convolution_convert_fusion = bf16[128,3072]{1,0:T(8,128)(2,1)S(1)} fusion(bf16[3072,1024]{1,0:T(8,128)(2,1)} %constant_dynamic-update-slice_fusion, bf16[272,1024]{1,0:T(8,128)(2,1)S(1)} %constant_dynamic-update-slice_fusion.3), kind=kOutput, calls=%fused_computation.12 | convolution fusion | flops 805699584 | bytes 7340032 | tf_op jit(solution)/shard_map/dot_general | solution.py:147
  131.8 0.5 collective-permute-start.29
  132.2 0.6 collective-permute-done.28
  132.9 1.6 %multiply_add_fusion = f32[128,3072]{1,0:T(8,128)} fusion(f32[128,3072]{1,0:T(8,128)S(1)} %get-tuple-element.100, f32[128,3072]{1,0:T(8,128)S(1)} %copy-done, f32[128]{0:T(128)S(1)} %get-tuple-element.85, f32[128]{0:T(128)S(1)} %get-tuple-element.84, f32[128]{0:T(128)S(1)} %fusion.61, pred[3072]{0:T(1024)(128)(4,1)S(1)} %iota_compare_fusion.14), kind=kLoop, calls=%fused_computation.50 | loop fusion | flops 2359296 | bytes 4723200 | tf_op jit(solution)/shard_map/add | solution.py:172
  134.5 6.5 %fusion.14 = f32[128,3072]{1,0:T(8,128)} fusion(f32[128,3072]{1,0:T(8,128)S(1)} %get-tuple-element.100, bf16[3072,1024]{1,0:T(8,128)(2,1)} %constant_dynamic-update-slice_fusion, f32[128,3072]{1,0:T(8,128)S(1)} %copy-done.1, bf16[128,3072]{1,0:T(8,128)(2,1)S(1)} %collective-permute-done.29, f32[128]{0:T(128)S(1)} %get-tuple-element.85, ...), kind=kOutput, calls=%fused_computation.20 | convolution fusion | flops 809631744 | bytes 12075008 | tf_op jit(solution)/shard_map/dot_general | solution.py:147
  (129 shorter events, 5.2 us)
Async XLA Ops:
  0.6 2.9 %copy-start = (f32[128,3072]{1,0:T(8,128)S(1)}, f32[128,3072]{1,0:T(8,128)}, u32[]{:S(2)}) copy-start(f32[128,3072]{1,0:T(8,128)} %param.19) | copy-start | bytes 4718596
  0.6 2.9 %copy-start.2 = (f32[3072]{0:T(1024)S(1)}, f32[3072]{0:T(1024)}, u32[]{:S(2)}) copy-start(f32[3072]{0:T(1024)} %param.17) | copy-start | bytes 36868
  0.7 3.6 %copy-start.4 = (f32[1024]{0:T(1024)S(1)}, f32[1024]{0:T(1024)}, u32[]{:S(2)}) copy-start(f32[1024]{0:T(1024)} %param.18) | copy-start | bytes 12292
  0.7 3.6 %copy-start.3 = (s32[3072]{0:T(1024)S(1)}, s32[3072]{0:T(1024)}, u32[]{:S(2)}) copy-start(s32[3072]{0:T(1024)} %param.15) | copy-start | bytes 36868
  3.0 2.5 %collective-permute-start = (bf16[128,3072]{1,0:T(8,128)(2,1)S(1)}, bf16[128,3072]{1,0:T(8,128)(2,1)S(1)}, u32[]{:S(2)}, u32[]{:S(2)}) collective-permute-start(bf16[128,3072]{1,0:T(8,128)(2,1)S(1)} %select_convert_fusion), channel_id=1, source_target_pairs={{0,1},{1,0},{2,3},{3,2},{4,5},{5,4},{6,7},{7,6},{8,9},{9,8},{10,11... | collective-permute-start | bytes 2359304 | tf_op jit(solution)/shard_map/ppermute | solution.py:123
  4.3 6.3 %copy-start.7 = (bf16[2048,1024]{1,0:T(8,128)(2,1)S(1)}, bf16[2048,1024]{1,0:T(8,128)(2,1)}, u32[]{:S(2)}) copy-start(bf16[2048,1024]{1,0:T(8,128)(2,1)} %param.14) | copy-start | bytes 12582916
  13.4 12.7 %collective-permute-start.1 = (bf16[272,256]{1,0:T(8,128)(2,1)S(1)}, bf16[272,256]{1,0:T(8,128)(2,1)S(1)}, u32[]{:S(2)}, u32[]{:S(2)}) collective-permute-start(bf16[272,256]{1,0:T(8,128)(2,1)S(1)} %pad_maximum_fusion), channel_id=1, source_target_pairs={{0,2},{2,0},{4,6},{6,4},{8,10},{10,8},{12,14},{14,12},{16,18},{18,... | collective-permute-start | bytes 417800 | tf_op jit(solution)/shard_map/ppermute | solution.py:37
  16.3 8.3 %collective-permute-start.3 = (bf16[272,256]{1,0:T(8,128)(2,1)S(1)}, bf16[272,256]{1,0:T(8,128)(2,1)S(1)}, u32[]{:S(2)}, u32[]{:S(2)}) collective-permute-start(bf16[272,256]{1,0:T(8,128)(2,1)S(1)} %pad_maximum_fusion.2), channel_id=1, source_target_pairs={{0,6},{2,4},{4,2},{6,0},{8,14},{10,12},{12,10},{14,8},{16,22},{18,... | collective-permute-start | bytes 417800 | tf_op jit(solution)/shard_map/ppermute | solution.py:37
  17.9 8.2 %collective-permute-start.2 = (bf16[272,256]{1,0:T(8,128)(2,1)S(1)}, bf16[272,256]{1,0:T(8,128)(2,1)S(1)}, u32[]{:S(2)}, u32[]{:S(2)}) collective-permute-start(bf16[272,256]{1,0:T(8,128)(2,1)S(1)} %pad_maximum_fusion.1), channel_id=1, source_target_pairs={{0,4},{2,6},{4,0},{6,2},{8,12},{10,14},{12,8},{14,10},{16,20},{18,... | collective-permute-start | bytes 417800 | tf_op jit(solution)/shard_map/ppermute | solution.py:37
  26.5 15.3 %collective-permute-start.4 = (bf16[272,64]{1,0:T(8,128)(2,1)S(1)}, bf16[272,64]{1,0:T(8,128)(2,1)S(1)}, u32[]{:S(2)}, u32[]{:S(2)}) collective-permute-start(bf16[272,64]{1,0:T(8,128)(2,1)S(1)} %pad_maximum_fusion.6), channel_id=1, source_target_pairs={{0,8},{2,10},{4,12},{6,14},{8,0},{10,2},{12,4},{14,6},{16,24},{18,... | collective-permute-start | bytes 104456 | tf_op jit(solution)/shard_map/ppermute | solution.py:37
  33.2 6.4 %collective-permute-start.6 = (bf16[272,64]{1,0:T(8,128)(2,1)S(1)}, bf16[272,64]{1,0:T(8,128)(2,1)S(1)}, u32[]{:S(2)}, u32[]{:S(2)}) collective-permute-start(bf16[272,64]{1,0:T(8,128)(2,1)S(1)} %pad_maximum_fusion.8), channel_id=1, source_target_pairs={{0,24},{2,26},{4,28},{6,30},{8,16},{10,18},{12,20},{14,22},{16,8},... | collective-permute-start | bytes 104456 | tf_op jit(solution)/shard_map/ppermute | solution.py:37
  35.7 6.1 %collective-permute-start.5 = (bf16[272,64]{1,0:T(8,128)(2,1)S(1)}, bf16[272,64]{1,0:T(8,128)(2,1)S(1)}, u32[]{:S(2)}, u32[]{:S(2)}) collective-permute-start(bf16[272,64]{1,0:T(8,128)(2,1)S(1)} %pad_maximum_fusion.7), channel_id=1, source_target_pairs={{0,16},{2,18},{4,20},{6,22},{8,24},{10,26},{12,28},{14,30},{16,0},... | collective-permute-start | bytes 104456 | tf_op jit(solution)/shard_map/ppermute | solution.py:37
  42.1 12.4 %collective-permute-start.7 = (bf16[272,64]{1,0:T(8,128)(2,1)S(1)}, bf16[272,64]{1,0:T(8,128)(2,1)S(1)}, u32[]{:S(2)}, u32[]{:S(2)}) collective-permute-start(bf16[272,64]{1,0:T(8,128)(2,1)S(1)} %pad_maximum_fusion.9), channel_id=1, source_target_pairs={{0,8},{2,10},{4,12},{6,14},{8,0},{10,2},{12,4},{14,6},{16,24},{18,... | collective-permute-start | bytes 104456 | tf_op jit(solution)/shard_map/ppermute | solution.py:51
  42.2 12.3 %collective-permute-start.8 = (bf16[272,64]{1,0:T(8,128)(2,1)S(1)}, bf16[272,64]{1,0:T(8,128)(2,1)S(1)}, u32[]{:S(2)}, u32[]{:S(2)}) collective-permute-start(bf16[272,64]{1,0:T(8,128)(2,1)S(1)} %pad_maximum_fusion.9), channel_id=1, source_target_pairs={{0,16},{2,18},{4,20},{6,22},{8,24},{10,26},{12,28},{14,30},{16,0},... | collective-permute-start | bytes 104456 | tf_op jit(solution)/shard_map/ppermute | solution.py:51
  45.1 9.4 %collective-permute-start.9 = (bf16[272,64]{1,0:T(8,128)(2,1)S(1)}, bf16[272,64]{1,0:T(8,128)(2,1)S(1)}, u32[]{:S(2)}, u32[]{:S(2)}) collective-permute-start(bf16[272,64]{1,0:T(8,128)(2,1)S(1)} %pad_maximum_fusion.9), channel_id=1, source_target_pairs={{0,24},{2,26},{4,28},{6,30},{8,16},{10,18},{12,20},{14,22},{16,8},... | collective-permute-start | bytes 104456 | tf_op jit(solution)/shard_map/ppermute | solution.py:51
  56.3 6.8 %collective-permute-start.10 = (bf16[272,256]{1,0:T(8,128)(2,1)S(1)}, bf16[272,256]{1,0:T(8,128)(2,1)S(1)}, u32[]{:S(2)}, u32[]{:S(2)}) collective-permute-start(bf16[272,256]{1,0:T(8,128)(2,1)S(1)} %dynamic_update_slice.51), channel_id=1, source_target_pairs={{0,2},{2,0},{4,6},{6,4},{8,10},{10,8},{12,14},{14,12},{16,18},{18,... | collective-permute-start | bytes 417800 | tf_op jit(solution)/shard_map/ppermute | solution.py:51
  57.8 6.6 %collective-permute-start.11 = (bf16[272,256]{1,0:T(8,128)(2,1)S(1)}, bf16[272,256]{1,0:T(8,128)(2,1)S(1)}, u32[]{:S(2)}, u32[]{:S(2)}) collective-permute-start(bf16[272,256]{1,0:T(8,128)(2,1)S(1)} %dynamic_update_slice.51), channel_id=1, source_target_pairs={{0,4},{2,6},{4,0},{6,2},{8,12},{10,14},{12,8},{14,10},{16,20},{18,... | collective-permute-start | bytes 417800 | tf_op jit(solution)/shard_map/ppermute | solution.py:51
  58.3 6.1 %collective-permute-start.12 = (bf16[272,256]{1,0:T(8,128)(2,1)S(1)}, bf16[272,256]{1,0:T(8,128)(2,1)S(1)}, u32[]{:S(2)}, u32[]{:S(2)}) collective-permute-start(bf16[272,256]{1,0:T(8,128)(2,1)S(1)} %dynamic_update_slice.51), channel_id=1, source_target_pairs={{0,6},{2,4},{4,2},{6,0},{8,14},{10,12},{12,10},{14,8},{16,22},{18,... | collective-permute-start | bytes 417800 | tf_op jit(solution)/shard_map/ppermute | solution.py:51
  69.4 2.9 %collective-permute-start.14 = (bf16[128,3072]{1,0:T(8,128)(2,1)S(1)}, bf16[128,3072]{1,0:T(8,128)(2,1)S(1)}, u32[]{:S(2)}, u32[]{:S(2)}) collective-permute-start(bf16[128,3072]{1,0:T(8,128)(2,1)S(1)} %convolution_convert_fusion.2), channel_id=1, source_target_pairs={{0,1},{1,0},{2,3},{3,2},{4,5},{5,4},{6,7},{7,6},{8,9},{9,8},{10,11... | collective-permute-start | bytes 2359304 | tf_op jit(solution)/shard_map/ppermute | solution.py:153
  69.7 2.0 %collective-permute-start.13 = (f32[128]{0:T(128)S(1)}, f32[128]{0:T(128)S(1)}, u32[]{:S(2)}, u32[]{:S(2)}) collective-permute-start(f32[128]{0:T(128)S(1)} %slice.390), channel_id=1, source_target_pairs={{0,1},{1,0},{2,3},{3,2},{4,5},{5,4},{6,7},{7,6},{8,9},{9,8},{10,11... | collective-permute-start | bytes 1544 | tf_op jit(solution)/shard_map/ppermute | solution.py:152
  71.8 0.5 copy-start.5
  79.8 4.3 %collective-permute-start.15 = (bf16[128,3072]{1,0:T(8,128)(2,1)}, bf16[128,3072]{1,0:T(8,128)(2,1)}, u32[]{:S(2)}, u32[]{:S(2)}) collective-permute-start(bf16[128,3072]{1,0:T(8,128)(2,1)} %convert_element_type.371), channel_id=1, source_target_pairs={{0,1},{1,0},{2,3},{3,2},{4,5},{5,4},{6,7},{7,6},{8,9},{9,8},{10,11... | collective-permute-start | bytes 2359304 | tf_op jit(solution)/shard_map/ppermute | solution.py:120
  88.6 7.6 %collective-permute-start.18 = (bf16[272,256]{1,0:T(8,128)(2,1)S(1)}, bf16[272,256]{1,0:T(8,128)(2,1)S(1)}, u32[]{:S(2)}, u32[]{:S(2)}) collective-permute-start(bf16[272,256]{1,0:T(8,128)(2,1)S(1)} %pad_maximum_fusion.5), channel_id=1, source_target_pairs={{0,6},{2,4},{4,2},{6,0},{8,14},{10,12},{12,10},{14,8},{16,22},{18,... | collective-permute-start | bytes 417800 | tf_op jit(solution)/shard_map/ppermute | solution.py:37
  90.0 8.5 %collective-permute-start.17 = (bf16[272,256]{1,0:T(8,128)(2,1)S(1)}, bf16[272,256]{1,0:T(8,128)(2,1)S(1)}, u32[]{:S(2)}, u32[]{:S(2)}) collective-permute-start(bf16[272,256]{1,0:T(8,128)(2,1)S(1)} %pad_maximum_fusion.4), channel_id=1, source_target_pairs={{0,4},{2,6},{4,0},{6,2},{8,12},{10,14},{12,8},{14,10},{16,20},{18,... | collective-permute-start | bytes 417800 | tf_op jit(solution)/shard_map/ppermute | solution.py:37
  90.7 7.8 %collective-permute-start.16 = (bf16[272,256]{1,0:T(8,128)(2,1)S(1)}, bf16[272,256]{1,0:T(8,128)(2,1)S(1)}, u32[]{:S(2)}, u32[]{:S(2)}) collective-permute-start(bf16[272,256]{1,0:T(8,128)(2,1)S(1)} %pad_maximum_fusion.3), channel_id=1, source_target_pairs={{0,2},{2,0},{4,6},{6,4},{8,10},{10,8},{12,14},{14,12},{16,18},{18,... | collective-permute-start | bytes 417800 | tf_op jit(solution)/shard_map/ppermute | solution.py:37
  98.9 6.8 %collective-permute-start.21 = (bf16[272,64]{1,0:T(8,128)(2,1)S(1)}, bf16[272,64]{1,0:T(8,128)(2,1)S(1)}, u32[]{:S(2)}, u32[]{:S(2)}) collective-permute-start(bf16[272,64]{1,0:T(8,128)(2,1)S(1)} %pad_maximum_fusion.12), channel_id=1, source_target_pairs={{0,24},{2,26},{4,28},{6,30},{8,16},{10,18},{12,20},{14,22},{16,8},... | collective-permute-start | bytes 104456 | tf_op jit(solution)/shard_map/ppermute | solution.py:37
  101.6 6.2 %collective-permute-start.20 = (bf16[272,64]{1,0:T(8,128)(2,1)S(1)}, bf16[272,64]{1,0:T(8,128)(2,1)S(1)}, u32[]{:S(2)}, u32[]{:S(2)}) collective-permute-start(bf16[272,64]{1,0:T(8,128)(2,1)S(1)} %pad_maximum_fusion.11), channel_id=1, source_target_pairs={{0,16},{2,18},{4,20},{6,22},{8,24},{10,26},{12,28},{14,30},{16,0},... | collective-permute-start | bytes 104456 | tf_op jit(solution)/shard_map/ppermute | solution.py:37
  101.7 6.2 %collective-permute-start.19 = (bf16[272,64]{1,0:T(8,128)(2,1)S(1)}, bf16[272,64]{1,0:T(8,128)(2,1)S(1)}, u32[]{:S(2)}, u32[]{:S(2)}) collective-permute-start(bf16[272,64]{1,0:T(8,128)(2,1)S(1)} %pad_maximum_fusion.10), channel_id=1, source_target_pairs={{0,8},{2,10},{4,12},{6,14},{8,0},{10,2},{12,4},{14,6},{16,24},{18,... | collective-permute-start | bytes 104456 | tf_op jit(solution)/shard_map/ppermute | solution.py:37
  108.1 5.2 %collective-permute-start.22 = (bf16[272,64]{1,0:T(8,128)(2,1)S(1)}, bf16[272,64]{1,0:T(8,128)(2,1)}, u32[]{:S(2)}, u32[]{:S(2)}) collective-permute-start(bf16[272,64]{1,0:T(8,128)(2,1)S(1)} %pad_maximum_fusion.13), channel_id=1, source_target_pairs={{0,8},{2,10},{4,12},{6,14},{8,0},{10,2},{12,4},{14,6},{16,24},{18,... | collective-permute-start | bytes 104456 | tf_op jit(solution)/shard_map/ppermute | solution.py:51
  109.0 7.8 %collective-permute-start.23 = (bf16[272,64]{1,0:T(8,128)(2,1)S(1)}, bf16[272,64]{1,0:T(8,128)(2,1)S(1)}, u32[]{:S(2)}, u32[]{:S(2)}) collective-permute-start(bf16[272,64]{1,0:T(8,128)(2,1)S(1)} %pad_maximum_fusion.13), channel_id=1, source_target_pairs={{0,16},{2,18},{4,20},{6,22},{8,24},{10,26},{12,28},{14,30},{16,0},... | collective-permute-start | bytes 104456 | tf_op jit(solution)/shard_map/ppermute | solution.py:51
  111.3 6.2 %collective-permute-start.24 = (bf16[272,64]{1,0:T(8,128)(2,1)S(1)}, bf16[272,64]{1,0:T(8,128)(2,1)S(1)}, u32[]{:S(2)}, u32[]{:S(2)}) collective-permute-start(bf16[272,64]{1,0:T(8,128)(2,1)S(1)} %pad_maximum_fusion.13), channel_id=1, source_target_pairs={{0,24},{2,26},{4,28},{6,30},{8,16},{10,18},{12,20},{14,22},{16,8},... | collective-permute-start | bytes 104456 | tf_op jit(solution)/shard_map/ppermute | solution.py:51
  118.4 5.3 %collective-permute-start.25 = (bf16[272,256]{1,0:T(8,128)(2,1)S(1)}, bf16[272,256]{1,0:T(8,128)(2,1)S(1)}, u32[]{:S(2)}, u32[]{:S(2)}) collective-permute-start(bf16[272,256]{1,0:T(8,128)(2,1)S(1)} %dynamic_update_slice.59), channel_id=1, source_target_pairs={{0,2},{2,0},{4,6},{6,4},{8,10},{10,8},{12,14},{14,12},{16,18},{18,... | collective-permute-start | bytes 417800 | tf_op jit(solution)/shard_map/ppermute | solution.py:51
  119.1 5.7 %collective-permute-start.26 = (bf16[272,256]{1,0:T(8,128)(2,1)S(1)}, bf16[272,256]{1,0:T(8,128)(2,1)S(1)}, u32[]{:S(2)}, u32[]{:S(2)}) collective-permute-start(bf16[272,256]{1,0:T(8,128)(2,1)S(1)} %dynamic_update_slice.59), channel_id=1, source_target_pairs={{0,4},{2,6},{4,0},{6,2},{8,12},{10,14},{12,8},{14,10},{16,20},{18,... | collective-permute-start | bytes 417800 | tf_op jit(solution)/shard_map/ppermute | solution.py:51
  120.5 6.0 %collective-permute-start.27 = (bf16[272,256]{1,0:T(8,128)(2,1)S(1)}, bf16[272,256]{1,0:T(8,128)(2,1)S(1)}, u32[]{:S(2)}, u32[]{:S(2)}) collective-permute-start(bf16[272,256]{1,0:T(8,128)(2,1)S(1)} %dynamic_update_slice.59), channel_id=1, source_target_pairs={{0,6},{2,4},{4,2},{6,0},{8,14},{10,12},{12,10},{14,8},{16,22},{18,... | collective-permute-start | bytes 417800 | tf_op jit(solution)/shard_map/ppermute | solution.py:51
  126.5 6.4 %copy-start.6 = (f32[128]{0:T(128)S(1)}, f32[128]{0:T(128)}, u32[]{:S(2)}) copy-start(f32[128]{0:T(128)} %copy-done.5) | copy-start | bytes 1540
  131.7 1.2 collective-permute-start.28
  131.8 2.7 %collective-permute-start.29 = (bf16[128,3072]{1,0:T(8,128)(2,1)S(1)}, bf16[128,3072]{1,0:T(8,128)(2,1)S(1)}, u32[]{:S(2)}, u32[]{:S(2)}) collective-permute-start(bf16[128,3072]{1,0:T(8,128)(2,1)S(1)} %convolution_convert_fusion), channel_id=1, source_target_pairs={{0,1},{1,0},{2,3},{3,2},{4,5},{5,4},{6,7},{7,6},{8,9},{9,8},{10,11... | collective-permute-start | bytes 2359304 | tf_op jit(solution)/shard_map/ppermute | solution.py:153
  132.9 1.6 %copy-start.1 = (f32[128,3072]{1,0:T(8,128)S(1)}, f32[128,3072]{1,0:T(8,128)}, u32[]{:S(2)}) copy-start(f32[128,3072]{1,0:T(8,128)} %get-tuple-element.140) | copy-start | bytes 4718596

commit v4 on v1

--- a/solution.py
+++ b/solution.py
@@ -19,7 +19,7 @@
         return received
 
     bits = n_vert.bit_length() - 1
-    rounds = [list(range(b, min(b + 2, bits))) for b in range(0, bits, 2)]
+    rounds = [list(range(b, min(b + 3, bits))) for b in range(0, bits, 3)]
     me = lax.axis_index("vert")
     cur = x
     plan = []

time: 124 us -> 134 us (1.081)
  starting transfers between devices: 35.4 us -> 50.6 us
  local copies, waits for them, and re-layouts: 12.5 us -> 9.39 us
  waiting for transfers between devices: 26.9 us -> 24.4 us
    ppermute x12 -> x16, starting transfers between devices: 17.4 us -> 26 us  [vert_sum(): lax.ppermute(send, 'vert', [(i, i ^ masks[t + 1]) for i in range(n_vert)])]
    ppermute x12 -> x16, waiting for transfers between devices: 14.3 us -> 5.87 us  [vert_sum(): lax.ppermute(send, 'vert', [(i, i ^ masks[t + 1]) for i in range(n_vert)])]
    ppermute x12 -> x16, starting transfers between devices: 16 us -> 22.6 us  [vert_sum(): lax.ppermute(cur, 'vert', [(i, i ^ masks[t]) for i in range(n_vert)])]
    ppermute x12 -> x16, waiting for transfers between devices: 6.46 us -> 12.3 us  [vert_sum(): lax.ppermute(cur, 'vert', [(i, i ^ masks[t]) for i in range(n_vert)])]
    dynamic_update_slice x12 -> x16, local copies, waits for them, and re-layouts: 3.83 us -> 1.41 us  [vert_sum(): out = lax.dynamic_update_slice_in_dim(out, got, (digit ^ t) * width, axis=1)]
    unnamed x26 -> x22, local copies, waits for them, and re-layouts: 3.57 us -> 3.05 us
  transfers between devices with their start and end apart: 30 -> 38, of which waited for: 15 -> 14; matrix products, arithmetic and copies ran while one was open for 19% -> 17% of each run, Pallas kernels for 0% -> 0%
where the time goes in v4:
time: 134 us
  starting transfers between devices  50.6 us (38%)
  matrix products  37.8 us (28%)
  waiting for transfers between devices  24.4 us (18%)
  local copies, waits for them, and re-layouts  9.39 us (7%)
  other arithmetic  8.82 us (7%)
  between operations  2.56 us (2%)
    ppermute x16, starting transfers between devices, vert_sum(): lax.ppermute(send, 'vert', [(i, i ^ masks[t + 1]) for i in range(n_vert)])  26 us
    ppermute x16, starting transfers between devices, vert_sum(): lax.ppermute(cur, 'vert', [(i, i ^ masks[t]) for i in range(n_vert)])  22.6 us
    dot_general x3, matrix products, work(): jnp.dot(rows, eig_table, preferred_element_type=jnp.float32)  16 us
    ppermute x16, waiting for transfers between devices, vert_sum(): lax.ppermute(cur, 'vert', [(i, i ^ masks[t]) for i in range(n_vert)])  12.3 us
    dot_general x2, matrix products, operate(): lax.dot_general(weights, features, (((1,), (1,)), ((), ())), preferred_el...  9.3 us
    ppermute x16, waiting for transfers between devices, vert_sum(): lax.ppermute(send, 'vert', [(i, i ^ masks[t + 1]) for i in range(n_vert)])  5.87 us
    dot_general x1, matrix products, coeff_from_table(): summed = jnp.dot(rows, picker, preferred_element_type=jnp.float32)  5.09 us
    dot_general x1, matrix products, operate(): coeff = jnp.dot(rows, built[0], preferred_element_type=jnp.float32)  5.07 us
  transfers between devices with their start and end apart: 38, of which 14 were waited for; matrix products, arithmetic and copies ran while one was open for 17% of the time, Pallas kernels for 0%

profile of v4, /device:TPU:0, one launch (start us, length us, event | category | flops | bytes accessed | tf_op | source)
XLA Modules:
  0.0 133.5 jit_solution(12119395598488159633)
XLA Ops:
  1.5 1.5 %select_convert_fusion = bf16[128,3072]{1,0:T(8,128)(2,1)S(1)} fusion(f32[128,3072]{1,0:T(8,128)} %param.19, pred[3072]{0:T(1024)(128)(4,1)S(1)} %iota_compare_fusion.14), kind=kLoop, calls=%fused_computation.59 | loop fusion | flops 393216 | bytes 2362368 | tf_op jit(solution)/shard_map/convert_element_type | solution.py:114
  3.0 0.6 collective-permute-start
  3.6 0.4 fusion.15
  4.3 1.1 collective-permute-done
  5.5 5.1 %subtract_convert_fusion = (bf16[256,2048]{1,0:T(8,128)(2,1)S(1)}, bf16[256,2048]{1,0:T(8,128)(2,1)S(1)}) fusion(s32[3072]{0:T(1024)S(1)} %copy-done.7, bf16[128,3072]{1,0:T(8,128)(2,1)S(1)} %collective-permute-done, bf16[128,3072]{1,0:T(8,128)(2,1)S(1)} %select_convert_fusion), kind=kOutput, calls=%fused_computation.38 | convolution fusion | flops 3232759808 | bytes 3682304 | tf_op jit(solution)/shard_map/dot_general | solution.py:86
  10.6 2.4 %fusion.8 = f32[512,1024]{1,0:T(8,128)S(1)} fusion(bf16[2048,1024]{1,0:T(8,128)(2,1)S(1)} %copy-done.9, bf16[256,2048]{1,0:T(8,128)(2,1)S(1)} %get-tuple-element.123, bf16[256,2048]{1,0:T(8,128)(2,1)S(1)} %get-tuple-element.124), kind=kOutput, calls=%fused_computation.34 | convolution fusion | flops 2151677952 | bytes 8388608 | tf_op jit(solution)/shard_map/dot_general | solution.py:89
  13.6 2.9 %collective-permute-start.1 = (bf16[272,128]{1,0:T(8,128)(2,1)S(1)}, bf16[272,128]{1,0:T(8,128)(2,1)S(1)}, u32[]{:S(2)}, u32[]{:S(2)}) collective-permute-start(bf16[272,128]{1,0:T(8,128)(2,1)S(1)} %pad_maximum_fusion), channel_id=1, source_target_pairs={{0,2},{2,0},{4,6},{6,4},{8,10},{10,8},{12,14},{14,12},{16,18},{18,... | collective-permute-start | bytes 208904 | tf_op jit(solution)/shard_map/ppermute | solution.py:37
  16.5 1.5 %collective-permute-start.2 = (bf16[272,128]{1,0:T(8,128)(2,1)S(1)}, bf16[272,128]{1,0:T(8,128)(2,1)S(1)}, u32[]{:S(2)}, u32[]{:S(2)}) collective-permute-start(bf16[272,128]{1,0:T(8,128)(2,1)S(1)} %pad_maximum_fusion.1), channel_id=1, source_target_pairs={{0,4},{2,6},{4,0},{6,2},{8,12},{10,14},{12,8},{14,10},{16,20},{18,... | collective-permute-start | bytes 208904 | tf_op jit(solution)/shard_map/ppermute | solution.py:37
  18.1 2.0 %collective-permute-start.4 = (bf16[272,128]{1,0:T(8,128)(2,1)S(1)}, bf16[272,128]{1,0:T(8,128)(2,1)S(1)}, u32[]{:S(2)}, u32[]{:S(2)}) collective-permute-start(bf16[272,128]{1,0:T(8,128)(2,1)S(1)} %pad_maximum_fusion.3), channel_id=1, source_target_pairs={{0,8},{2,10},{4,12},{6,14},{8,0},{10,2},{12,4},{14,6},{16,24},{18,... | collective-permute-start | bytes 208904 | tf_op jit(solution)/shard_map/ppermute | solution.py:37
  20.1 1.4 %collective-permute-start.5 = (bf16[272,128]{1,0:T(8,128)(2,1)S(1)}, bf16[272,128]{1,0:T(8,128)(2,1)S(1)}, u32[]{:S(2)}, u32[]{:S(2)}) collective-permute-start(bf16[272,128]{1,0:T(8,128)(2,1)S(1)} %pad_maximum_fusion.4), channel_id=1, source_target_pairs={{0,10},{2,8},{4,14},{6,12},{8,2},{10,0},{12,6},{14,4},{16,26},{18,... | collective-permute-start | bytes 208904 | tf_op jit(solution)/shard_map/ppermute | solution.py:37
  21.5 2.6 %collective-permute-start.6 = (bf16[272,128]{1,0:T(8,128)(2,1)S(1)}, bf16[272,128]{1,0:T(8,128)(2,1)S(1)}, u32[]{:S(2)}, u32[]{:S(2)}) collective-permute-start(bf16[272,128]{1,0:T(8,128)(2,1)S(1)} %pad_maximum_fusion.5), channel_id=1, source_target_pairs={{0,12},{2,14},{4,8},{6,10},{8,4},{10,6},{12,0},{14,2},{16,28},{18,... | collective-permute-start | bytes 208904 | tf_op jit(solution)/shard_map/ppermute | solution.py:37
  24.1 0.7 collective-permute-start.7
  24.8 5.0 %fusion.14 = bf16[1024,1024]{1,0:T(8,128)(2,1)S(1)} fusion(bf16[2048,1024]{1,0:T(8,128)(2,1)S(1)} %copy-done.9, s32[1024]{0:T(1024)S(1)} %get-tuple-element.65), kind=kOutput, calls=%fused_computation.41 | convolution fusion | flops 4298113024 | bytes 6295552 | tf_op jit(solution)/shard_map/dot_general | solution.py:79
  29.8 0.4 collective-permute-done.7
  30.6 2.7 %collective-permute-start.8 = (bf16[272,64]{1,0:T(8,128)(2,1)S(1)}, bf16[272,64]{1,0:T(8,128)(2,1)S(1)}, u32[]{:S(2)}, u32[]{:S(2)}) collective-permute-start(bf16[272,64]{1,0:T(8,128)(2,1)S(1)} %pad_maximum_fusion.7), channel_id=1, source_target_pairs={{0,16},{2,18},{4,20},{6,22},{8,24},{10,26},{12,28},{14,30},{16,0},... | collective-permute-start | bytes 104456 | tf_op jit(solution)/shard_map/ppermute | solution.py:37
  33.3 5.0 %fusion.13 = bf16[1024,1024]{1,0:T(8,128)(2,1)S(1)} fusion(bf16[2048,1024]{1,0:T(8,128)(2,1)S(1)} %copy-done.9, s32[1024]{0:T(1024)S(1)} %get-tuple-element.73), kind=kOutput, calls=%fused_computation.40 | convolution fusion | flops 4298113024 | bytes 6295552 | tf_op jit(solution)/shard_map/dot_general | solution.py:79
  38.6 0.4 collective-permute-start.9
  39.0 6.0 %fusion.12 = bf16[1024,1024]{1,0:T(8,128)(2,1)} fusion(bf16[2048,1024]{1,0:T(8,128)(2,1)S(1)} %copy-done.9, s32[1024]{0:T(1024)S(1)} %get-tuple-element.75), kind=kOutput, calls=%fused_computation.39 | convolution fusion | flops 4298113024 | bytes 6295552 | tf_op jit(solution)/shard_map/dot_general | solution.py:79
  45.2 2.7 %copy-done.5 = bf16[3072,1024]{1,0:T(8,128)(2,1)} copy-done((bf16[3072,1024]{1,0:T(8,128)(2,1)}, bf16[3072,1024]{1,0:T(8,128)(2,1)S(1)}, u32[]{:S(2)}) %copy-start.5) | copy-done | bytes 6291480
  48.2 0.6 dynamic_update_slice.61
  48.8 0.9 collective-permute-start.10
  49.7 1.5 %collective-permute-start.11 = (bf16[272,128]{1,0:T(8,128)(2,1)S(1)}, bf16[272,128]{1,0:T(8,128)(2,1)S(1)}, u32[]{:S(2)}, u32[]{:S(2)}) collective-permute-start(bf16[272,128]{1,0:T(8,128)(2,1)S(1)} %dynamic_update_slice.61), channel_id=1, source_target_pairs={{0,4},{2,6},{4,0},{6,2},{8,12},{10,14},{12,8},{14,10},{16,20},{18,... | collective-permute-start | bytes 208904 | tf_op jit(solution)/shard_map/ppermute | solution.py:51
  51.2 1.2 collective-permute-start.12
  52.4 1.3 collective-permute-start.13
  53.7 0.9 collective-permute-start.14
  54.6 3.1 %constant_dynamic-update-slice_fusion.16 = bf16[3072,1024]{1,0:T(8,128)(2,1)} fusion(bf16[3072,1024]{1,0:T(8,128)(2,1)} %copy-done.5, bf16[1024,1024]{1,0:T(8,128)(2,1)} %fusion.12), kind=kLoop, calls=%fused_computation.187 | loop fusion | bytes 4194304 | tf_op jit(solution)/shard_map/concatenate | solution.py:135
  57.8 2.9 %collective-permute-start.15 = (bf16[272,128]{1,0:T(8,128)(2,1)S(1)}, bf16[272,128]{1,0:T(8,128)(2,1)S(1)}, u32[]{:S(2)}, u32[]{:S(2)}) collective-permute-start(bf16[272,128]{1,0:T(8,128)(2,1)S(1)} %dynamic_update_slice.61), channel_id=1, source_target_pairs={{0,12},{2,14},{4,8},{6,10},{8,4},{10,6},{12,0},{14,2},{16,28},{18,... | collective-permute-start | bytes 208904 | tf_op jit(solution)/shard_map/ppermute | solution.py:51
  60.8 0.8 collective-permute-start.16
  61.7 1.4 %collective-permute-done.15 = bf16[272,128]{1,0:T(8,128)(2,1)S(1)} collective-permute-done((bf16[272,128]{1,0:T(8,128)(2,1)S(1)}, bf16[272,128]{1,0:T(8,128)(2,1)S(1)}, u32[]{:S(2)}, u32[]{:S(2)}) %collective-permute-start.15) | collective-permute-done | bytes 69664 | tf_op jit(solution)/shard_map/ppermute | solution.py:51
  63.1 3.8 %collective-permute-done.16 = bf16[272,128]{1,0:T(8,128)(2,1)S(1)} collective-permute-done((bf16[272,128]{1,0:T(8,128)(2,1)S(1)}, bf16[272,128]{1,0:T(8,128)(2,1)S(1)}, u32[]{:S(2)}, u32[]{:S(2)}) %collective-permute-start.16) | collective-permute-done | bytes 69664 | tf_op jit(solution)/shard_map/ppermute | solution.py:51
  67.0 4.6 %convolution_convert_fusion.1 = bf16[256,3072]{1,0:T(8,128)(2,1)S(1)} fusion(bf16[3072,1024]{1,0:T(8,128)(2,1)} %constant_dynamic-update-slice_fusion.16, bf16[272,1024]{1,0:T(8,128)(2,1)S(1)} %constant_dynamic-update-slice_fusion.8), kind=kOutput, calls=%fused_computation.29 | convolution fusion | flops 1611399168 | bytes 8388608 | tf_op jit(solution)/shard_map/dot_general | solution.py:143
  72.0 0.6 collective-permute-start.17
  72.6 1.5 %collective-permute-done.17 = f32[128]{0:T(128)S(1)} collective-permute-done((f32[128]{0:T(128)S(1)}, f32[128]{0:T(128)S(1)}, u32[]{:S(2)}, u32[]{:S(2)}) %collective-permute-start.17) | collective-permute-done | bytes 544 | tf_op jit(solution)/shard_map/ppermute | solution.py:147
  74.1 0.9 fusion.16
  75.0 1.0 convert_element_type.452
  76.5 2.1 %collective-permute-done.19 = bf16[128,3072]{1,0:T(8,128)(2,1)} collective-permute-done((bf16[128,3072]{1,0:T(8,128)(2,1)}, bf16[128,3072]{1,0:T(8,128)(2,1)}, u32[]{:S(2)}, u32[]{:S(2)}) %collective-permute-start.19) | collective-permute-done | bytes 786464 | tf_op jit(solution)/shard_map/ppermute | solution.py:116
  78.6 5.1 %fusion.27 = f32[256,1024]{1,0:T(8,128)S(1)} fusion(bf16[3072,1024]{1,0:T(8,128)(2,1)} %constant_dynamic-update-slice_fusion.16, bf16[128,3072]{1,0:T(8,128)(2,1)} %collective-permute-done.19, bf16[128,3072]{1,0:T(8,128)(2,1)} %convert_element_type.452, f32[1024]{0:T(1024)S(1)} %power_multiply_fusion), kind=kOutput, calls=%fused_computation.58 | convolution fusion | flops 1614020608 | bytes 8916992 | tf_op jit(solution)/shard_map/dot_general | solution.py:122
  84.1 0.6 collective-permute-start.20
  84.7 0.6 collective-permute-start.21
  85.3 2.3 %collective-permute-start.22 = (bf16[272,128]{1,0:T(8,128)(2,1)S(1)}, bf16[272,128]{1,0:T(8,128)(2,1)S(1)}, u32[]{:S(2)}, u32[]{:S(2)}) collective-permute-start(bf16[272,128]{1,0:T(8,128)(2,1)S(1)} %pad_maximum_fusion.11), channel_id=1, source_target_pairs={{0,6},{2,4},{4,2},{6,0},{8,14},{10,12},{12,10},{14,8},{16,22},{18,... | collective-permute-start | bytes 208904 | tf_op jit(solution)/shard_map/ppermute | solution.py:37
  87.8 1.9 %collective-permute-start.24 = (bf16[272,128]{1,0:T(8,128)(2,1)S(1)}, bf16[272,128]{1,0:T(8,128)(2,1)S(1)}, u32[]{:S(2)}, u32[]{:S(2)}) collective-permute-start(bf16[272,128]{1,0:T(8,128)(2,1)S(1)} %pad_maximum_fusion.13), channel_id=1, source_target_pairs={{0,10},{2,8},{4,14},{6,12},{8,2},{10,0},{12,6},{14,4},{16,26},{18,... | collective-permute-start | bytes 208904 | tf_op jit(solution)/shard_map/ppermute | solution.py:37
  89.7 0.8 collective-permute-start.25
  90.5 3.2 %collective-permute-start.26 = (bf16[272,128]{1,0:T(8,128)(2,1)S(1)}, bf16[272,128]{1,0:T(8,128)(2,1)S(1)}, u32[]{:S(2)}, u32[]{:S(2)}) collective-permute-start(bf16[272,128]{1,0:T(8,128)(2,1)S(1)} %pad_maximum_fusion.15), channel_id=1, source_target_pairs={{0,14},{2,12},{4,10},{6,8},{8,6},{10,4},{12,2},{14,0},{16,30},{18,... | collective-permute-start | bytes 208904 | tf_op jit(solution)/shard_map/ppermute | solution.py:37
  93.8 1.3 collective-permute-done.25
  95.2 1.5 %collective-permute-done.26 = bf16[272,128]{1,0:T(8,128)(2,1)S(1)} collective-permute-done((bf16[272,128]{1,0:T(8,128)(2,1)S(1)}, bf16[272,128]{1,0:T(8,128)(2,1)S(1)}, u32[]{:S(2)}, u32[]{:S(2)}) %collective-permute-start.26) | collective-permute-done | bytes 69664 | tf_op jit(solution)/shard_map/ppermute | solution.py:37
  97.0 2.7 %collective-permute-start.27 = (bf16[272,64]{1,0:T(8,128)(2,1)S(1)}, bf16[272,64]{1,0:T(8,128)(2,1)S(1)}, u32[]{:S(2)}, u32[]{:S(2)}) collective-permute-start(bf16[272,64]{1,0:T(8,128)(2,1)S(1)} %pad_maximum_fusion.16), channel_id=1, source_target_pairs={{0,16},{2,18},{4,20},{6,22},{8,24},{10,26},{12,28},{14,30},{16,0},... | collective-permute-start | bytes 104456 | tf_op jit(solution)/shard_map/ppermute | solution.py:37
  99.7 2.6 %collective-permute-done.27 = bf16[272,64]{1,0:T(8,128)(2,1)S(1)} collective-permute-done((bf16[272,64]{1,0:T(8,128)(2,1)S(1)}, bf16[272,64]{1,0:T(8,128)(2,1)S(1)}, u32[]{:S(2)}, u32[]{:S(2)}) %collective-permute-start.27) | collective-permute-done | bytes 34848 | tf_op jit(solution)/shard_map/ppermute | solution.py:37
  102.5 2.8 %collective-permute-start.28 = (bf16[272,64]{1,0:T(8,128)(2,1)S(1)}, bf16[272,64]{1,0:T(8,128)(2,1)S(1)}, u32[]{:S(2)}, u32[]{:S(2)}) collective-permute-start(bf16[272,64]{1,0:T(8,128)(2,1)S(1)} %pad_maximum_fusion.17), channel_id=1, source_target_pairs={{0,16},{2,18},{4,20},{6,22},{8,24},{10,26},{12,28},{14,30},{16,0},... | collective-permute-start | bytes 104456 | tf_op jit(solution)/shard_map/ppermute | solution.py:51
  105.5 2.2 %collective-permute-done.28 = bf16[272,64]{1,0:T(8,128)(2,1)S(1)} collective-permute-done((bf16[272,64]{1,0:T(8,128)(2,1)S(1)}, bf16[272,64]{1,0:T(8,128)(2,1)S(1)}, u32[]{:S(2)}, u32[]{:S(2)}) %collective-permute-start.28) | collective-permute-done | bytes 34848 | tf_op jit(solution)/shard_map/ppermute | solution.py:51
  107.8 0.5 dynamic_update_slice.71
  108.3 0.8 collective-permute-start.29
  109.2 1.5 %collective-permute-start.30 = (bf16[272,128]{1,0:T(8,128)(2,1)S(1)}, bf16[272,128]{1,0:T(8,128)(2,1)S(1)}, u32[]{:S(2)}, u32[]{:S(2)}) collective-permute-start(bf16[272,128]{1,0:T(8,128)(2,1)S(1)} %dynamic_update_slice.71), channel_id=1, source_target_pairs={{0,4},{2,6},{4,0},{6,2},{8,12},{10,14},{12,8},{14,10},{16,20},{18,... | collective-permute-start | bytes 208904 | tf_op jit(solution)/shard_map/ppermute | solution.py:51
  110.7 1.2 collective-permute-start.31
  111.9 1.9 %collective-permute-start.32 = (bf16[272,128]{1,0:T(8,128)(2,1)S(1)}, bf16[272,128]{1,0:T(8,128)(2,1)S(1)}, u32[]{:S(2)}, u32[]{:S(2)}) collective-permute-start(bf16[272,128]{1,0:T(8,128)(2,1)S(1)} %dynamic_update_slice.71), channel_id=1, source_target_pairs={{0,8},{2,10},{4,12},{6,14},{8,0},{10,2},{12,4},{14,6},{16,24},{18,... | collective-permute-start | bytes 208904 | tf_op jit(solution)/shard_map/ppermute | solution.py:51
  113.8 1.4 %collective-permute-start.33 = (bf16[272,128]{1,0:T(8,128)(2,1)S(1)}, bf16[272,128]{1,0:T(8,128)(2,1)S(1)}, u32[]{:S(2)}, u32[]{:S(2)}) collective-permute-start(bf16[272,128]{1,0:T(8,128)(2,1)S(1)} %dynamic_update_slice.71), channel_id=1, source_target_pairs={{0,10},{2,8},{4,14},{6,12},{8,2},{10,0},{12,6},{14,4},{16,26},{18,... | collective-permute-start | bytes 208904 | tf_op jit(solution)/shard_map/ppermute | solution.py:51
  115.3 1.9 %collective-permute-start.34 = (bf16[272,128]{1,0:T(8,128)(2,1)S(1)}, bf16[272,128]{1,0:T(8,128)(2,1)S(1)}, u32[]{:S(2)}, u32[]{:S(2)}) collective-permute-start(bf16[272,128]{1,0:T(8,128)(2,1)S(1)} %dynamic_update_slice.71), channel_id=1, source_target_pairs={{0,12},{2,14},{4,8},{6,10},{8,4},{10,6},{12,0},{14,2},{16,28},{18,... | collective-permute-start | bytes 208904 | tf_op jit(solution)/shard_map/ppermute | solution.py:51
  117.2 1.2 collective-permute-start.35
  118.5 0.5 collective-permute-done.33
  119.0 1.5 %collective-permute-done.34 = bf16[272,128]{1,0:T(8,128)(2,1)S(1)} collective-permute-done((bf16[272,128]{1,0:T(8,128)(2,1)S(1)}, bf16[272,128]{1,0:T(8,128)(2,1)S(1)}, u32[]{:S(2)}, u32[]{:S(2)}) %collective-permute-start.34) | collective-permute-done | bytes 69664 | tf_op jit(solution)/shard_map/ppermute | solution.py:51
  120.6 2.8 %collective-permute-done.35 = bf16[272,128]{1,0:T(8,128)(2,1)S(1)} collective-permute-done((bf16[272,128]{1,0:T(8,128)(2,1)S(1)}, bf16[272,128]{1,0:T(8,128)(2,1)S(1)}, u32[]{:S(2)}, u32[]{:S(2)}) %collective-permute-start.35) | collective-permute-done | bytes 69664 | tf_op jit(solution)/shard_map/ppermute | solution.py:51
  123.4 4.7 %convolution_convert_fusion = bf16[256,3072]{1,0:T(8,128)(2,1)S(1)} fusion(bf16[3072,1024]{1,0:T(8,128)(2,1)} %constant_dynamic-update-slice_fusion.16, bf16[272,1024]{1,0:T(8,128)(2,1)S(1)} %constant_dynamic-update-slice_fusion), kind=kOutput, calls=%fused_computation.28 | convolution fusion | flops 1611399168 | bytes 8388608 | tf_op jit(solution)/shard_map/dot_general | solution.py:143
  128.5 0.6 collective-permute-start.36
  129.1 1.5 %collective-permute-done.36 = f32[128]{0:T(128)S(1)} collective-permute-done((f32[128]{0:T(128)S(1)}, f32[128]{0:T(128)S(1)}, u32[]{:S(2)}, u32[]{:S(2)}) %collective-permute-start.36) | collective-permute-done | bytes 544 | tf_op jit(solution)/shard_map/ppermute | solution.py:147
  130.6 2.9 %fusion.19 = (f32[128,3072]{1,0:T(8,128)}, f32[128,3072]{1,0:T(8,128)}) fusion(f32[128,3072]{1,0:T(8,128)S(1)} %get-tuple-element.104, bf16[128,3072]{1,0:T(8,128)(2,1)S(1)} %collective-permute-done.37, bf16[128,3072]{1,0:T(8,128)(2,1)S(1)} %copy-done.4, f32[128,3072]{1,0:T(8,128)S(1)} %copy-done, bf16[256,3072]{1,0:T(8,128)(2,1)S(1)} %convolution_convert_fusion, ...), kind=kLoop, calls=%fused_computation.46 | loop fusion | flops 8650752 | bytes 9454080 | tf_op jit(solution)/shard_map/sub | solution.py:168
  (178 shorter events, 5.0 us)
Async XLA Ops:
  0.6 2.9 %copy-start = (f32[128,3072]{1,0:T(8,128)S(1)}, f32[128,3072]{1,0:T(8,128)}, u32[]{:S(2)}) copy-start(f32[128,3072]{1,0:T(8,128)} %param.19) | copy-start | bytes 4718596
  0.6 2.9 %copy-start.6 = (f32[3072]{0:T(1024)S(1)}, f32[3072]{0:T(1024)}, u32[]{:S(2)}) copy-start(f32[3072]{0:T(1024)} %param.17) | copy-start | bytes 36868
  1.4 2.8 %copy-start.8 = (f32[1024]{0:T(1024)S(1)}, f32[1024]{0:T(1024)}, u32[]{:S(2)}) copy-start(f32[1024]{0:T(1024)} %param.18) | copy-start | bytes 12292
  1.4 2.9 %copy-start.7 = (s32[3072]{0:T(1024)S(1)}, s32[3072]{0:T(1024)}, u32[]{:S(2)}) copy-start(s32[3072]{0:T(1024)} %param.15) | copy-start | bytes 36868
  3.0 2.5 %collective-permute-start = (bf16[128,3072]{1,0:T(8,128)(2,1)S(1)}, bf16[128,3072]{1,0:T(8,128)(2,1)S(1)}, u32[]{:S(2)}, u32[]{:S(2)}) collective-permute-start(bf16[128,3072]{1,0:T(8,128)(2,1)S(1)} %select_convert_fusion), channel_id=1, source_target_pairs={{0,1},{1,0},{2,3},{3,2},{4,5},{5,4},{6,7},{7,6},{8,9},{9,8},{10,11... | collective-permute-start | bytes 2359304 | tf_op jit(solution)/shard_map/ppermute | solution.py:116
  4.3 6.2 %copy-start.9 = (bf16[2048,1024]{1,0:T(8,128)(2,1)S(1)}, bf16[2048,1024]{1,0:T(8,128)(2,1)}, u32[]{:S(2)}) copy-start(bf16[2048,1024]{1,0:T(8,128)(2,1)} %param.14) | copy-start | bytes 12582916
  13.6 7.9 %collective-permute-start.1 = (bf16[272,128]{1,0:T(8,128)(2,1)S(1)}, bf16[272,128]{1,0:T(8,128)(2,1)S(1)}, u32[]{:S(2)}, u32[]{:S(2)}) collective-permute-start(bf16[272,128]{1,0:T(8,128)(2,1)S(1)} %pad_maximum_fusion), channel_id=1, source_target_pairs={{0,2},{2,0},{4,6},{6,4},{8,10},{10,8},{12,14},{14,12},{16,18},{18,... | collective-permute-start | bytes 208904 | tf_op jit(solution)/shard_map/ppermute | solution.py:37
  16.5 7.6 %collective-permute-start.2 = (bf16[272,128]{1,0:T(8,128)(2,1)S(1)}, bf16[272,128]{1,0:T(8,128)(2,1)S(1)}, u32[]{:S(2)}, u32[]{:S(2)}) collective-permute-start(bf16[272,128]{1,0:T(8,128)(2,1)S(1)} %pad_maximum_fusion.1), channel_id=1, source_target_pairs={{0,4},{2,6},{4,0},{6,2},{8,12},{10,14},{12,8},{14,10},{16,20},{18,... | collective-permute-start | bytes 208904 | tf_op jit(solution)/shard_map/ppermute | solution.py:37
  18.0 11.8 %collective-permute-start.3 = (bf16[272,128]{1,0:T(8,128)(2,1)S(1)}, bf16[272,128]{1,0:T(8,128)(2,1)S(1)}, u32[]{:S(2)}, u32[]{:S(2)}) collective-permute-start(bf16[272,128]{1,0:T(8,128)(2,1)S(1)} %pad_maximum_fusion.2), channel_id=1, source_target_pairs={{0,6},{2,4},{4,2},{6,0},{8,14},{10,12},{12,10},{14,8},{16,22},{18,... | collective-permute-start | bytes 208904 | tf_op jit(solution)/shard_map/ppermute | solution.py:37
  18.1 11.7 %collective-permute-start.4 = (bf16[272,128]{1,0:T(8,128)(2,1)S(1)}, bf16[272,128]{1,0:T(8,128)(2,1)S(1)}, u32[]{:S(2)}, u32[]{:S(2)}) collective-permute-start(bf16[272,128]{1,0:T(8,128)(2,1)S(1)} %pad_maximum_fusion.3), channel_id=1, source_target_pairs={{0,8},{2,10},{4,12},{6,14},{8,0},{10,2},{12,4},{14,6},{16,24},{18,... | collective-permute-start | bytes 208904 | tf_op jit(solution)/shard_map/ppermute | solution.py:37
  20.1 9.7 %collective-permute-start.5 = (bf16[272,128]{1,0:T(8,128)(2,1)S(1)}, bf16[272,128]{1,0:T(8,128)(2,1)S(1)}, u32[]{:S(2)}, u32[]{:S(2)}) collective-permute-start(bf16[272,128]{1,0:T(8,128)(2,1)S(1)} %pad_maximum_fusion.4), channel_id=1, source_target_pairs={{0,10},{2,8},{4,14},{6,12},{8,2},{10,0},{12,6},{14,4},{16,26},{18,... | collective-permute-start | bytes 208904 | tf_op jit(solution)/shard_map/ppermute | solution.py:37
  21.5 8.3 %collective-permute-start.6 = (bf16[272,128]{1,0:T(8,128)(2,1)S(1)}, bf16[272,128]{1,0:T(8,128)(2,1)S(1)}, u32[]{:S(2)}, u32[]{:S(2)}) collective-permute-start(bf16[272,128]{1,0:T(8,128)(2,1)S(1)} %pad_maximum_fusion.5), channel_id=1, source_target_pairs={{0,12},{2,14},{4,8},{6,10},{8,4},{10,6},{12,0},{14,2},{16,28},{18,... | collective-permute-start | bytes 208904 | tf_op jit(solution)/shard_map/ppermute | solution.py:37
  24.1 6.1 %collective-permute-start.7 = (bf16[272,128]{1,0:T(8,128)(2,1)S(1)}, bf16[272,128]{1,0:T(8,128)(2,1)S(1)}, u32[]{:S(2)}, u32[]{:S(2)}) collective-permute-start(bf16[272,128]{1,0:T(8,128)(2,1)S(1)} %pad_maximum_fusion.6), channel_id=1, source_target_pairs={{0,14},{2,12},{4,10},{6,8},{8,6},{10,4},{12,2},{14,0},{16,30},{18,... | collective-permute-start | bytes 208904 | tf_op jit(solution)/shard_map/ppermute | solution.py:37
  30.6 7.8 %collective-permute-start.8 = (bf16[272,64]{1,0:T(8,128)(2,1)S(1)}, bf16[272,64]{1,0:T(8,128)(2,1)S(1)}, u32[]{:S(2)}, u32[]{:S(2)}) collective-permute-start(bf16[272,64]{1,0:T(8,128)(2,1)S(1)} %pad_maximum_fusion.7), channel_id=1, source_target_pairs={{0,16},{2,18},{4,20},{6,22},{8,24},{10,26},{12,28},{14,30},{16,0},... | collective-permute-start | bytes 104456 | tf_op jit(solution)/shard_map/ppermute | solution.py:37
  38.6 9.6 %collective-permute-start.9 = (bf16[272,64]{1,0:T(8,128)(2,1)S(1)}, bf16[272,64]{1,0:T(8,128)(2,1)S(1)}, u32[]{:S(2)}, u32[]{:S(2)}) collective-permute-start(bf16[272,64]{1,0:T(8,128)(2,1)S(1)} %pad_maximum_fusion.8), channel_id=1, source_target_pairs={{0,16},{2,18},{4,20},{6,22},{8,24},{10,26},{12,28},{14,30},{16,0},... | collective-permute-start | bytes 104456 | tf_op jit(solution)/shard_map/ppermute | solution.py:51
  45.2 2.7 %copy-start.5 = (bf16[3072,1024]{1,0:T(8,128)(2,1)}, bf16[3072,1024]{1,0:T(8,128)(2,1)S(1)}, u32[]{:S(2)}) copy-start(bf16[3072,1024]{1,0:T(8,128)(2,1)S(1)} %constant_dynamic-update-slice_fusion.17) | copy-start | bytes 18874372
  48.8 9.0 %collective-permute-start.10 = (bf16[272,128]{1,0:T(8,128)(2,1)S(1)}, bf16[272,128]{1,0:T(8,128)(2,1)S(1)}, u32[]{:S(2)}, u32[]{:S(2)}) collective-permute-start(bf16[272,128]{1,0:T(8,128)(2,1)S(1)} %dynamic_update_slice.61), channel_id=1, source_target_pairs={{0,2},{2,0},{4,6},{6,4},{8,10},{10,8},{12,14},{14,12},{16,18},{18,... | collective-permute-start | bytes 208904 | tf_op jit(solution)/shard_map/ppermute | solution.py:51
  49.7 11.1 %collective-permute-start.11 = (bf16[272,128]{1,0:T(8,128)(2,1)S(1)}, bf16[272,128]{1,0:T(8,128)(2,1)S(1)}, u32[]{:S(2)}, u32[]{:S(2)}) collective-permute-start(bf16[272,128]{1,0:T(8,128)(2,1)S(1)} %dynamic_update_slice.61), channel_id=1, source_target_pairs={{0,4},{2,6},{4,0},{6,2},{8,12},{10,14},{12,8},{14,10},{16,20},{18,... | collective-permute-start | bytes 208904 | tf_op jit(solution)/shard_map/ppermute | solution.py:51
  51.2 10.4 %collective-permute-start.12 = (bf16[272,128]{1,0:T(8,128)(2,1)S(1)}, bf16[272,128]{1,0:T(8,128)(2,1)S(1)}, u32[]{:S(2)}, u32[]{:S(2)}) collective-permute-start(bf16[272,128]{1,0:T(8,128)(2,1)S(1)} %dynamic_update_slice.61), channel_id=1, source_target_pairs={{0,6},{2,4},{4,2},{6,0},{8,14},{10,12},{12,10},{14,8},{16,22},{18,... | collective-permute-start | bytes 208904 | tf_op jit(solution)/shard_map/ppermute | solution.py:51
  52.4 9.3 %collective-permute-start.13 = (bf16[272,128]{1,0:T(8,128)(2,1)S(1)}, bf16[272,128]{1,0:T(8,128)(2,1)S(1)}, u32[]{:S(2)}, u32[]{:S(2)}) collective-permute-start(bf16[272,128]{1,0:T(8,128)(2,1)S(1)} %dynamic_update_slice.61), channel_id=1, source_target_pairs={{0,8},{2,10},{4,12},{6,14},{8,0},{10,2},{12,4},{14,6},{16,24},{18,... | collective-permute-start | bytes 208904 | tf_op jit(solution)/shard_map/ppermute | solution.py:51
  53.7 8.0 %collective-permute-start.14 = (bf16[272,128]{1,0:T(8,128)(2,1)S(1)}, bf16[272,128]{1,0:T(8,128)(2,1)S(1)}, u32[]{:S(2)}, u32[]{:S(2)}) collective-permute-start(bf16[272,128]{1,0:T(8,128)(2,1)S(1)} %dynamic_update_slice.61), channel_id=1, source_target_pairs={{0,10},{2,8},{4,14},{6,12},{8,2},{10,0},{12,6},{14,4},{16,26},{18,... | collective-permute-start | bytes 208904 | tf_op jit(solution)/shard_map/ppermute | solution.py:51
  57.8 5.3 %collective-permute-start.15 = (bf16[272,128]{1,0:T(8,128)(2,1)S(1)}, bf16[272,128]{1,0:T(8,128)(2,1)S(1)}, u32[]{:S(2)}, u32[]{:S(2)}) collective-permute-start(bf16[272,128]{1,0:T(8,128)(2,1)S(1)} %dynamic_update_slice.61), channel_id=1, source_target_pairs={{0,12},{2,14},{4,8},{6,10},{8,4},{10,6},{12,0},{14,2},{16,28},{18,... | collective-permute-start | bytes 208904 | tf_op jit(solution)/shard_map/ppermute | solution.py:51
  60.8 6.2 %collective-permute-start.16 = (bf16[272,128]{1,0:T(8,128)(2,1)S(1)}, bf16[272,128]{1,0:T(8,128)(2,1)S(1)}, u32[]{:S(2)}, u32[]{:S(2)}) collective-permute-start(bf16[272,128]{1,0:T(8,128)(2,1)S(1)} %dynamic_update_slice.61), channel_id=1, source_target_pairs={{0,14},{2,12},{4,10},{6,8},{8,6},{10,4},{12,2},{14,0},{16,30},{18,... | collective-permute-start | bytes 208904 | tf_op jit(solution)/shard_map/ppermute | solution.py:51
  71.6 3.4 %copy-start.1 = (bf16[256,3072]{1,0:T(8,128)(2,1)}, bf16[256,3072]{1,0:T(8,128)(2,1)S(1)}, u32[]{:S(2)}) copy-start(bf16[256,3072]{1,0:T(8,128)(2,1)S(1)} %convolution_convert_fusion.1) | copy-start | bytes 4718596
  71.7 2.4 %collective-permute-start.18 = (bf16[128,3072]{1,0:T(8,128)(2,1)S(1)}, bf16[128,3072]{1,0:T(8,128)(2,1)S(1)}, u32[]{:S(2)}, u32[]{:S(2)}) collective-permute-start(bf16[128,3072]{1,0:T(8,128)(2,1)S(1)} %slice.538), channel_id=1, source_target_pairs={{0,1},{1,0},{2,3},{3,2},{4,5},{5,4},{6,7},{7,6},{8,9},{9,8},{10,11... | collective-permute-start | bytes 2359304 | tf_op jit(solution)/shard_map/ppermute | solution.py:148
  72.0 2.0 %collective-permute-start.17 = (f32[128]{0:T(128)S(1)}, f32[128]{0:T(128)S(1)}, u32[]{:S(2)}, u32[]{:S(2)}) collective-permute-start(f32[128]{0:T(128)S(1)} %slice.460), channel_id=1, source_target_pairs={{0,1},{1,0},{2,3},{3,2},{4,5},{5,4},{6,7},{7,6},{8,9},{9,8},{10,11... | collective-permute-start | bytes 1544 | tf_op jit(solution)/shard_map/ppermute | solution.py:147
  74.0 0.9 copy-start.3
  76.0 2.6 %collective-permute-start.19 = (bf16[128,3072]{1,0:T(8,128)(2,1)}, bf16[128,3072]{1,0:T(8,128)(2,1)}, u32[]{:S(2)}, u32[]{:S(2)}) collective-permute-start(bf16[128,3072]{1,0:T(8,128)(2,1)} %convert_element_type.452), channel_id=1, source_target_pairs={{0,1},{1,0},{2,3},{3,2},{4,5},{5,4},{6,7},{7,6},{8,9},{9,8},{10,11... | collective-permute-start | bytes 2359304 | tf_op jit(solution)/shard_map/ppermute | solution.py:116
  84.1 5.6 %collective-permute-start.20 = (bf16[272,128]{1,0:T(8,128)(2,1)S(1)}, bf16[272,128]{1,0:T(8,128)(2,1)S(1)}, u32[]{:S(2)}, u32[]{:S(2)}) collective-permute-start(bf16[272,128]{1,0:T(8,128)(2,1)S(1)} %pad_maximum_fusion.9), channel_id=1, source_target_pairs={{0,2},{2,0},{4,6},{6,4},{8,10},{10,8},{12,14},{14,12},{16,18},{18,... | collective-permute-start | bytes 208904 | tf_op jit(solution)/shard_map/ppermute | solution.py:37
  84.7 5.9 %collective-permute-start.21 = (bf16[272,128]{1,0:T(8,128)(2,1)S(1)}, bf16[272,128]{1,0:T(8,128)(2,1)S(1)}, u32[]{:S(2)}, u32[]{:S(2)}) collective-permute-start(bf16[272,128]{1,0:T(8,128)(2,1)S(1)} %pad_maximum_fusion.10), channel_id=1, source_target_pairs={{0,4},{2,6},{4,0},{6,2},{8,12},{10,14},{12,8},{14,10},{16,20},{18,... | collective-permute-start | bytes 208904 | tf_op jit(solution)/shard_map/ppermute | solution.py:37
  85.3 8.4 %collective-permute-start.22 = (bf16[272,128]{1,0:T(8,128)(2,1)S(1)}, bf16[272,128]{1,0:T(8,128)(2,1)S(1)}, u32[]{:S(2)}, u32[]{:S(2)}) collective-permute-start(bf16[272,128]{1,0:T(8,128)(2,1)S(1)} %pad_maximum_fusion.11), channel_id=1, source_target_pairs={{0,6},{2,4},{4,2},{6,0},{8,14},{10,12},{12,10},{14,8},{16,22},{18,... | collective-permute-start | bytes 208904 | tf_op jit(solution)/shard_map/ppermute | solution.py:37
  87.7 6.1 %collective-permute-start.23 = (bf16[272,128]{1,0:T(8,128)(2,1)S(1)}, bf16[272,128]{1,0:T(8,128)(2,1)S(1)}, u32[]{:S(2)}, u32[]{:S(2)}) collective-permute-start(bf16[272,128]{1,0:T(8,128)(2,1)S(1)} %pad_maximum_fusion.12), channel_id=1, source_target_pairs={{0,8},{2,10},{4,12},{6,14},{8,0},{10,2},{12,4},{14,6},{16,24},{18,... | collective-permute-start | bytes 208904 | tf_op jit(solution)/shard_map/ppermute | solution.py:37
  87.8 6.0 %collective-permute-start.24 = (bf16[272,128]{1,0:T(8,128)(2,1)S(1)}, bf16[272,128]{1,0:T(8,128)(2,1)S(1)}, u32[]{:S(2)}, u32[]{:S(2)}) collective-permute-start(bf16[272,128]{1,0:T(8,128)(2,1)S(1)} %pad_maximum_fusion.13), channel_id=1, source_target_pairs={{0,10},{2,8},{4,14},{6,12},{8,2},{10,0},{12,6},{14,4},{16,26},{18,... | collective-permute-start | bytes 208904 | tf_op jit(solution)/shard_map/ppermute | solution.py:37
  89.7 5.5 %collective-permute-start.25 = (bf16[272,128]{1,0:T(8,128)(2,1)S(1)}, bf16[272,128]{1,0:T(8,128)(2,1)S(1)}, u32[]{:S(2)}, u32[]{:S(2)}) collective-permute-start(bf16[272,128]{1,0:T(8,128)(2,1)S(1)} %pad_maximum_fusion.14), channel_id=1, source_target_pairs={{0,12},{2,14},{4,8},{6,10},{8,4},{10,6},{12,0},{14,2},{16,28},{18,... | collective-permute-start | bytes 208904 | tf_op jit(solution)/shard_map/ppermute | solution.py:37
  90.5 6.2 %collective-permute-start.26 = (bf16[272,128]{1,0:T(8,128)(2,1)S(1)}, bf16[272,128]{1,0:T(8,128)(2,1)S(1)}, u32[]{:S(2)}, u32[]{:S(2)}) collective-permute-start(bf16[272,128]{1,0:T(8,128)(2,1)S(1)} %pad_maximum_fusion.15), channel_id=1, source_target_pairs={{0,14},{2,12},{4,10},{6,8},{8,6},{10,4},{12,2},{14,0},{16,30},{18,... | collective-permute-start | bytes 208904 | tf_op jit(solution)/shard_map/ppermute | solution.py:37
  97.0 5.3 %collective-permute-start.27 = (bf16[272,64]{1,0:T(8,128)(2,1)S(1)}, bf16[272,64]{1,0:T(8,128)(2,1)S(1)}, u32[]{:S(2)}, u32[]{:S(2)}) collective-permute-start(bf16[272,64]{1,0:T(8,128)(2,1)S(1)} %pad_maximum_fusion.16), channel_id=1, source_target_pairs={{0,16},{2,18},{4,20},{6,22},{8,24},{10,26},{12,28},{14,30},{16,0},... | collective-permute-start | bytes 104456 | tf_op jit(solution)/shard_map/ppermute | solution.py:37
  102.5 5.3 %collective-permute-start.28 = (bf16[272,64]{1,0:T(8,128)(2,1)S(1)}, bf16[272,64]{1,0:T(8,128)(2,1)S(1)}, u32[]{:S(2)}, u32[]{:S(2)}) collective-permute-start(bf16[272,64]{1,0:T(8,128)(2,1)S(1)} %pad_maximum_fusion.17), channel_id=1, source_target_pairs={{0,16},{2,18},{4,20},{6,22},{8,24},{10,26},{12,28},{14,30},{16,0},... | collective-permute-start | bytes 104456 | tf_op jit(solution)/shard_map/ppermute | solution.py:51
  108.3 7.0 %collective-permute-start.29 = (bf16[272,128]{1,0:T(8,128)(2,1)S(1)}, bf16[272,128]{1,0:T(8,128)(2,1)S(1)}, u32[]{:S(2)}, u32[]{:S(2)}) collective-permute-start(bf16[272,128]{1,0:T(8,128)(2,1)S(1)} %dynamic_update_slice.71), channel_id=1, source_target_pairs={{0,2},{2,0},{4,6},{6,4},{8,10},{10,8},{12,14},{14,12},{16,18},{18,... | collective-permute-start | bytes 208904 | tf_op jit(solution)/shard_map/ppermute | solution.py:51
  109.2 8.1 %collective-permute-start.30 = (bf16[272,128]{1,0:T(8,128)(2,1)S(1)}, bf16[272,128]{1,0:T(8,128)(2,1)S(1)}, u32[]{:S(2)}, u32[]{:S(2)}) collective-permute-start(bf16[272,128]{1,0:T(8,128)(2,1)S(1)} %dynamic_update_slice.71), channel_id=1, source_target_pairs={{0,4},{2,6},{4,0},{6,2},{8,12},{10,14},{12,8},{14,10},{16,20},{18,... | collective-permute-start | bytes 208904 | tf_op jit(solution)/shard_map/ppermute | solution.py:51
  110.7 7.7 %collective-permute-start.31 = (bf16[272,128]{1,0:T(8,128)(2,1)S(1)}, bf16[272,128]{1,0:T(8,128)(2,1)S(1)}, u32[]{:S(2)}, u32[]{:S(2)}) collective-permute-start(bf16[272,128]{1,0:T(8,128)(2,1)S(1)} %dynamic_update_slice.71), channel_id=1, source_target_pairs={{0,6},{2,4},{4,2},{6,0},{8,14},{10,12},{12,10},{14,8},{16,22},{18,... | collective-permute-start | bytes 208904 | tf_op jit(solution)/shard_map/ppermute | solution.py:51
  111.9 6.6 %collective-permute-start.32 = (bf16[272,128]{1,0:T(8,128)(2,1)S(1)}, bf16[272,128]{1,0:T(8,128)(2,1)S(1)}, u32[]{:S(2)}, u32[]{:S(2)}) collective-permute-start(bf16[272,128]{1,0:T(8,128)(2,1)S(1)} %dynamic_update_slice.71), channel_id=1, source_target_pairs={{0,8},{2,10},{4,12},{6,14},{8,0},{10,2},{12,4},{14,6},{16,24},{18,... | collective-permute-start | bytes 208904 | tf_op jit(solution)/shard_map/ppermute | solution.py:51
  113.8 5.2 %collective-permute-start.33 = (bf16[272,128]{1,0:T(8,128)(2,1)S(1)}, bf16[272,128]{1,0:T(8,128)(2,1)S(1)}, u32[]{:S(2)}, u32[]{:S(2)}) collective-permute-start(bf16[272,128]{1,0:T(8,128)(2,1)S(1)} %dynamic_update_slice.71), channel_id=1, source_target_pairs={{0,10},{2,8},{4,14},{6,12},{8,2},{10,0},{12,6},{14,4},{16,26},{18,... | collective-permute-start | bytes 208904 | tf_op jit(solution)/shard_map/ppermute | solution.py:51
  115.3 5.3 %collective-permute-start.34 = (bf16[272,128]{1,0:T(8,128)(2,1)S(1)}, bf16[272,128]{1,0:T(8,128)(2,1)S(1)}, u32[]{:S(2)}, u32[]{:S(2)}) collective-permute-start(bf16[272,128]{1,0:T(8,128)(2,1)S(1)} %dynamic_update_slice.71), channel_id=1, source_target_pairs={{0,12},{2,14},{4,8},{6,10},{8,4},{10,6},{12,0},{14,2},{16,28},{18,... | collective-permute-start | bytes 208904 | tf_op jit(solution)/shard_map/ppermute | solution.py:51
  117.2 6.2 %collective-permute-start.35 = (bf16[272,128]{1,0:T(8,128)(2,1)S(1)}, bf16[272,128]{1,0:T(8,128)(2,1)S(1)}, u32[]{:S(2)}, u32[]{:S(2)}) collective-permute-start(bf16[272,128]{1,0:T(8,128)(2,1)S(1)} %dynamic_update_slice.71), channel_id=1, source_target_pairs={{0,14},{2,12},{4,10},{6,8},{8,6},{10,4},{12,2},{14,0},{16,30},{18,... | collective-permute-start | bytes 208904 | tf_op jit(solution)/shard_map/ppermute | solution.py:51
  123.4 7.2 %copy-start.4 = (bf16[128,3072]{1,0:T(8,128)(2,1)S(1)}, bf16[128,3072]{1,0:T(8,128)(2,1)}, u32[]{:S(2)}) copy-start(bf16[128,3072]{1,0:T(8,128)(2,1)} %copy-done.3) | copy-start | bytes 2359300
  128.1 2.5 %copy-start.2 = (bf16[256,3072]{1,0:T(8,128)(2,1)S(1)}, bf16[256,3072]{1,0:T(8,128)(2,1)}, u32[]{:S(2)}) copy-start(bf16[256,3072]{1,0:T(8,128)(2,1)} %copy-done.1) | copy-start | bytes 4718596
  128.2 2.4 %collective-permute-start.37 = (bf16[128,3072]{1,0:T(8,128)(2,1)S(1)}, bf16[128,3072]{1,0:T(8,128)(2,1)S(1)}, u32[]{:S(2)}, u32[]{:S(2)}) collective-permute-start(bf16[128,3072]{1,0:T(8,128)(2,1)S(1)} %slice.585), channel_id=1, source_target_pairs={{0,1},{1,0},{2,3},{3,2},{4,5},{5,4},{6,7},{7,6},{8,9},{9,8},{10,11... | collective-permute-start | bytes 2359304 | tf_op jit(solution)/shard_map/ppermute | solution.py:148
  128.5 2.0 %collective-permute-start.36 = (f32[128]{0:T(128)S(1)}, f32[128]{0:T(128)S(1)}, u32[]{:S(2)}, u32[]{:S(2)}) collective-permute-start(f32[128]{0:T(128)S(1)} %slice.511), channel_id=1, source_target_pairs={{0,1},{1,0},{2,3},{3,2},{4,5},{5,4},{6,7},{7,6},{8,9},{9,8},{10,11... | collective-permute-start | bytes 1544 | tf_op jit(solution)/shard_map/ppermute | solution.py:147

commit v5 on v1

--- a/solution.py
+++ b/solution.py
@@ -113,11 +113,20 @@
         def operate(vector, first=False):
             lowered = vector.astype(jnp.bfloat16)
             if pair:
-                rows = jnp.concatenate([lowered, lax.ppermute(lowered, "eig", swap)], 0)
+                arrived = lax.ppermute(lowered, "eig", swap)
+                rows = jnp.concatenate([lowered, arrived], 0)
             else:
                 rows = lax.all_gather(lowered, "eig", axis=0, tiled=True)
             if first:
                 coeff = coeff_from_table(rows)
+            elif pair:
+                coeff = jnp.concatenate(
+                    [
+                        jnp.dot(lowered, built[0], preferred_element_type=jnp.float32),
+                        jnp.dot(arrived, built[0], preferred_element_type=jnp.float32),
+                    ],
+                    0,
+                )
             else:
                 coeff = jnp.dot(rows, built[0], preferred_element_type=jnp.float32)
             sums = jnp.zeros((8, group), jnp.float32)

time: 124 us -> 125 us (level)
  matrix products: 37.8 us -> 40.8 us
  waiting for transfers between devices: 26.9 us -> 25.2 us
    dot_general x1 -> x2, matrix products: 5.07 us -> 8.06 us  [the longest x1 4.03 us: operate(): jnp.dot(lowered, built[0], preferred_element_type=jnp.float32)]
    ppermute x2, waiting for transfers between devices: 3.26 us -> 1.14 us  [operate(): arrived = lax.ppermute(lowered, 'eig', swap)]
    unnamed x26 -> x24, local copies, waits for them, and re-layouts: 3.57 us -> 3.64 us
  transfers between devices with their start and end apart: 30 -> 30, of which waited for: 15 -> 14; matrix products, arithmetic and copies ran while one was open for 19% -> 24% of each run, Pallas kernels for 0% -> 0%
where the time goes in v5:
time: 125 us
  matrix products  40.8 us (33%)
  starting transfers between devices  35.4 us (28%)
  waiting for transfers between devices  25.2 us (20%)
  local copies, waits for them, and re-layouts  12.6 us (10%)
  other arithmetic  8.94 us (7%)
  between operations  2.32 us (2%)
    ppermute x12, starting transfers between devices, vert_sum(): lax.ppermute(send, 'vert', [(i, i ^ masks[t + 1]) for i in range(n_vert)])  17.4 us
    ppermute x12, starting transfers between devices, vert_sum(): lax.ppermute(cur, 'vert', [(i, i ^ masks[t]) for i in range(n_vert)])  16 us
    dot_general x3, matrix products, work(): jnp.dot(rows, eig_table, preferred_element_type=jnp.float32)  16 us
    ppermute x12, waiting for transfers between devices, vert_sum(): lax.ppermute(send, 'vert', [(i, i ^ masks[t + 1]) for i in range(n_vert)])  14.2 us
    dot_general x2, matrix products, operate(): lax.dot_general(weights, features, (((1,), (1,)), ((), ())), preferred_el...  9.29 us
    ppermute x12, waiting for transfers between devices, vert_sum(): lax.ppermute(cur, 'vert', [(i, i ^ masks[t]) for i in range(n_vert)])  6.86 us
    dot_general x1, matrix products, coeff_from_table(): summed = jnp.dot(rows, picker, preferred_element_type=jnp.float32)  5.08 us
    dot_general x1, matrix products, operate(): jnp.dot(lowered, built[0], preferred_element_type=jnp.float32)  4.03 us
  transfers between devices with their start and end apart: 30, of which 14 were waited for; matrix products, arithmetic and copies ran while one was open for 24% of the time, Pallas kernels for 0%

profile of v5, /device:TPU:0, one launch (start us, length us, event | category | flops | bytes accessed | tf_op | source)
XLA Modules:
  0.0 125.2 jit_solution(5756371610657856638)
XLA Ops:
  1.5 1.5 %select_convert_fusion = bf16[128,3072]{1,0:T(8,128)(2,1)S(1)} fusion(f32[128,3072]{1,0:T(8,128)} %param.19, pred[3072]{0:T(1024)(128)(4,1)S(1)} %iota_compare_fusion.14), kind=kLoop, calls=%fused_computation.46 | loop fusion | flops 393216 | bytes 2362368 | tf_op jit(solution)/shard_map/convert_element_type | solution.py:114
  3.0 0.6 collective-permute-start
  3.6 0.4 fusion.15
  4.3 1.1 collective-permute-done
  5.5 5.1 %subtract_convert_fusion = (bf16[256,2048]{1,0:T(8,128)(2,1)S(1)}, bf16[256,2048]{1,0:T(8,128)(2,1)S(1)}) fusion(s32[3072]{0:T(1024)S(1)} %copy-done.6, bf16[128,3072]{1,0:T(8,128)(2,1)S(1)} %collective-permute-done, bf16[128,3072]{1,0:T(8,128)(2,1)S(1)} %select_convert_fusion), kind=kOutput, calls=%fused_computation.30 | convolution fusion | flops 3232759808 | bytes 3682304 | tf_op jit(solution)/shard_map/dot_general | solution.py:86
  10.6 2.4 %fusion.8 = f32[512,1024]{1,0:T(8,128)S(1)} fusion(bf16[2048,1024]{1,0:T(8,128)(2,1)S(1)} %copy-done.10, bf16[256,2048]{1,0:T(8,128)(2,1)S(1)} %get-tuple-element.115, bf16[256,2048]{1,0:T(8,128)(2,1)S(1)} %get-tuple-element.116), kind=kOutput, calls=%fused_computation.26 | convolution fusion | flops 2151677952 | bytes 8388608 | tf_op jit(solution)/shard_map/dot_general | solution.py:89
  13.4 2.9 %collective-permute-start.1 = (bf16[272,256]{1,0:T(8,128)(2,1)S(1)}, bf16[272,256]{1,0:T(8,128)(2,1)S(1)}, u32[]{:S(2)}, u32[]{:S(2)}) collective-permute-start(bf16[272,256]{1,0:T(8,128)(2,1)S(1)} %pad_maximum_fusion), channel_id=1, source_target_pairs={{0,2},{2,0},{4,6},{6,4},{8,10},{10,8},{12,14},{14,12},{16,18},{18,... | collective-permute-start | bytes 417800 | tf_op jit(solution)/shard_map/ppermute | solution.py:37
  16.3 1.6 %collective-permute-start.2 = (bf16[272,256]{1,0:T(8,128)(2,1)S(1)}, bf16[272,256]{1,0:T(8,128)(2,1)S(1)}, u32[]{:S(2)}, u32[]{:S(2)}) collective-permute-start(bf16[272,256]{1,0:T(8,128)(2,1)S(1)} %pad_maximum_fusion.1), channel_id=1, source_target_pairs={{0,4},{2,6},{4,0},{6,2},{8,12},{10,14},{12,8},{14,10},{16,20},{18,... | collective-permute-start | bytes 417800 | tf_op jit(solution)/shard_map/ppermute | solution.py:37
  18.0 5.0 %fusion.14 = bf16[1024,1024]{1,0:T(8,128)(2,1)S(1)} fusion(bf16[2048,1024]{1,0:T(8,128)(2,1)S(1)} %copy-done.10, s32[1024]{0:T(1024)S(1)} %get-tuple-element.65), kind=kOutput, calls=%fused_computation.33 | convolution fusion | flops 4298113024 | bytes 6295552 | tf_op jit(solution)/shard_map/dot_general | solution.py:79
  23.0 1.8 %collective-permute-done.2 = bf16[272,256]{1,0:T(8,128)(2,1)S(1)} collective-permute-done((bf16[272,256]{1,0:T(8,128)(2,1)S(1)}, bf16[272,256]{1,0:T(8,128)(2,1)S(1)}, u32[]{:S(2)}, u32[]{:S(2)}) %collective-permute-start.2) | collective-permute-done | bytes 139296 | tf_op jit(solution)/shard_map/ppermute | solution.py:37
  25.2 1.6 %collective-permute-start.4 = (bf16[272,64]{1,0:T(8,128)(2,1)S(1)}, bf16[272,64]{1,0:T(8,128)(2,1)S(1)}, u32[]{:S(2)}, u32[]{:S(2)}) collective-permute-start(bf16[272,64]{1,0:T(8,128)(2,1)S(1)} %pad_maximum_fusion.6), channel_id=1, source_target_pairs={{0,8},{2,10},{4,12},{6,14},{8,0},{10,2},{12,4},{14,6},{16,24},{18,... | collective-permute-start | bytes 104456 | tf_op jit(solution)/shard_map/ppermute | solution.py:37
  26.9 2.7 %collective-permute-start.5 = (bf16[272,64]{1,0:T(8,128)(2,1)S(1)}, bf16[272,64]{1,0:T(8,128)(2,1)S(1)}, u32[]{:S(2)}, u32[]{:S(2)}) collective-permute-start(bf16[272,64]{1,0:T(8,128)(2,1)S(1)} %pad_maximum_fusion.7), channel_id=1, source_target_pairs={{0,16},{2,18},{4,20},{6,22},{8,24},{10,26},{12,28},{14,30},{16,0},... | collective-permute-start | bytes 104456 | tf_op jit(solution)/shard_map/ppermute | solution.py:37
  29.6 0.3 collective-permute-start.6
  29.9 5.0 %fusion.13 = bf16[1024,1024]{1,0:T(8,128)(2,1)S(1)} fusion(bf16[2048,1024]{1,0:T(8,128)(2,1)S(1)} %copy-done.10, s32[1024]{0:T(1024)S(1)} %get-tuple-element.69), kind=kOutput, calls=%fused_computation.32 | convolution fusion | flops 4298113024 | bytes 6295552 | tf_op jit(solution)/shard_map/dot_general | solution.py:79
  34.8 1.5 %constant_dynamic-update-slice_fusion.2 = bf16[3072,1024]{1,0:T(8,128)(2,1)} fusion(bf16[1024,1024]{1,0:T(8,128)(2,1)S(1)} %fusion.14), kind=kLoop, calls=%fused_computation.129 | loop fusion | bytes 4194304
  36.6 0.7 collective-permute-start.7
  37.4 3.5 %collective-permute-start.8 = (bf16[272,64]{1,0:T(8,128)(2,1)S(1)}, bf16[272,64]{1,0:T(8,128)(2,1)S(1)}, u32[]{:S(2)}, u32[]{:S(2)}) collective-permute-start(bf16[272,64]{1,0:T(8,128)(2,1)S(1)} %pad_maximum_fusion.9), channel_id=1, source_target_pairs={{0,16},{2,18},{4,20},{6,22},{8,24},{10,26},{12,28},{14,30},{16,0},... | collective-permute-start | bytes 104456 | tf_op jit(solution)/shard_map/ppermute | solution.py:51
  41.1 6.0 %fusion.12 = bf16[1024,1024]{1,0:T(8,128)(2,1)} fusion(bf16[2048,1024]{1,0:T(8,128)(2,1)S(1)} %copy-done.10, s32[1024]{0:T(1024)S(1)} %get-tuple-element.73), kind=kOutput, calls=%fused_computation.31 | convolution fusion | flops 4298113024 | bytes 6295552 | tf_op jit(solution)/shard_map/dot_general | solution.py:79
  47.1 1.5 %constant_dynamic-update-slice_fusion.1 = bf16[3072,1024]{1,0:T(8,128)(2,1)} fusion(bf16[3072,1024]{1,0:T(8,128)(2,1)} %constant_dynamic-update-slice_fusion.2, bf16[1024,1024]{1,0:T(8,128)(2,1)S(1)} %fusion.13), kind=kLoop, calls=%fused_computation.128 | loop fusion | bytes 4194304
  48.6 0.3 dynamic_update_slice.48
  49.0 0.6 dynamic_update_slice.49
  49.7 0.3 dynamic_update_slice.50
  50.0 0.6 dynamic_update_slice.51
  50.5 1.2 collective-permute-start.10
  51.8 0.9 collective-permute-start.11
  52.7 1.4 %collective-permute-start.12 = (bf16[272,256]{1,0:T(8,128)(2,1)S(1)}, bf16[272,256]{1,0:T(8,128)(2,1)S(1)}, u32[]{:S(2)}, u32[]{:S(2)}) collective-permute-start(bf16[272,256]{1,0:T(8,128)(2,1)S(1)} %dynamic_update_slice.51), channel_id=1, source_target_pairs={{0,6},{2,4},{4,2},{6,0},{8,14},{10,12},{12,10},{14,8},{16,22},{18,... | collective-permute-start | bytes 417800 | tf_op jit(solution)/shard_map/ppermute | solution.py:51
  54.1 3.1 %constant_dynamic-update-slice_fusion = bf16[3072,1024]{1,0:T(8,128)(2,1)} fusion(bf16[3072,1024]{1,0:T(8,128)(2,1)} %constant_dynamic-update-slice_fusion.1, bf16[1024,1024]{1,0:T(8,128)(2,1)} %fusion.12), kind=kLoop, calls=%fused_computation.127 | loop fusion | bytes 4194304 | tf_op jit(solution)/shard_map/concatenate | solution.py:144
  57.4 1.2 collective-permute-done.12
  58.6 4.6 %convolution_convert_fusion.1 = bf16[256,3072]{1,0:T(8,128)(2,1)S(1)} fusion(bf16[3072,1024]{1,0:T(8,128)(2,1)} %constant_dynamic-update-slice_fusion, bf16[272,1024]{1,0:T(8,128)(2,1)S(1)} %constant_dynamic-update-slice_fusion.7), kind=kOutput, calls=%fused_computation.13 | convolution fusion | flops 1611399168 | bytes 8388608 | tf_op jit(solution)/shard_map/dot_general | solution.py:152
  63.6 0.6 collective-permute-start.13
  64.2 1.5 %collective-permute-done.13 = f32[128]{0:T(128)S(1)} collective-permute-done((f32[128]{0:T(128)S(1)}, f32[128]{0:T(128)S(1)}, u32[]{:S(2)}, u32[]{:S(2)}) %collective-permute-start.13) | collective-permute-done | bytes 544 | tf_op jit(solution)/shard_map/ppermute | solution.py:156
  65.7 0.6 copy-done.8
  66.3 0.9 fusion.16
  67.2 1.0 convert_element_type.364
  68.3 0.4 scatter.19
  68.7 4.0 %fusion.56 = f32[128,1024]{1,0:T(8,128)S(1)} fusion(bf16[128,3072]{1,0:T(8,128)(2,1)} %convert_element_type.364, bf16[3072,1024]{1,0:T(8,128)(2,1)} %constant_dynamic-update-slice_fusion), kind=kOutput, calls=%fused_computation.192 | convolution fusion | flops 805306368 | bytes 7602176 | tf_op jit(solution)/shard_map/dot_general | solution.py:125
  72.8 4.0 %fusion.57 = f32[128,1024]{1,0:T(8,128)S(1)} fusion(bf16[128,3072]{1,0:T(8,128)(2,1)} %collective-permute-done.15, bf16[3072,1024]{1,0:T(8,128)(2,1)} %constant_dynamic-update-slice_fusion), kind=kOutput, calls=%fused_computation.193 | convolution fusion | flops 805306368 | bytes 7602176 | tf_op jit(solution)/shard_map/dot_general | solution.py:126
  77.2 1.5 %collective-permute-start.16 = (bf16[272,256]{1,0:T(8,128)(2,1)S(1)}, bf16[272,256]{1,0:T(8,128)(2,1)S(1)}, u32[]{:S(2)}, u32[]{:S(2)}) collective-permute-start(bf16[272,256]{1,0:T(8,128)(2,1)S(1)} %pad_maximum_fusion.3), channel_id=1, source_target_pairs={{0,2},{2,0},{4,6},{6,4},{8,10},{10,8},{12,14},{14,12},{16,18},{18,... | collective-permute-start | bytes 417800 | tf_op jit(solution)/shard_map/ppermute | solution.py:37
  78.7 0.7 collective-permute-start.17
  79.4 1.5 %collective-permute-start.18 = (bf16[272,256]{1,0:T(8,128)(2,1)S(1)}, bf16[272,256]{1,0:T(8,128)(2,1)S(1)}, u32[]{:S(2)}, u32[]{:S(2)}) collective-permute-start(bf16[272,256]{1,0:T(8,128)(2,1)S(1)} %pad_maximum_fusion.5), channel_id=1, source_target_pairs={{0,6},{2,4},{4,2},{6,0},{8,14},{10,12},{12,10},{14,8},{16,22},{18,... | collective-permute-start | bytes 417800 | tf_op jit(solution)/shard_map/ppermute | solution.py:37
  80.9 2.7 %collective-permute-done.16 = bf16[272,256]{1,0:T(8,128)(2,1)S(1)} collective-permute-done((bf16[272,256]{1,0:T(8,128)(2,1)S(1)}, bf16[272,256]{1,0:T(8,128)(2,1)S(1)}, u32[]{:S(2)}, u32[]{:S(2)}) %collective-permute-start.16) | collective-permute-done | bytes 139296 | tf_op jit(solution)/shard_map/ppermute | solution.py:37
  83.6 3.8 %collective-permute-done.17 = bf16[272,256]{1,0:T(8,128)(2,1)S(1)} collective-permute-done((bf16[272,256]{1,0:T(8,128)(2,1)S(1)}, bf16[272,256]{1,0:T(8,128)(2,1)S(1)}, u32[]{:S(2)}, u32[]{:S(2)}) %collective-permute-start.17) | collective-permute-done | bytes 139296 | tf_op jit(solution)/shard_map/ppermute | solution.py:37
  87.9 0.4 collective-permute-start.19
  88.3 3.9 %collective-permute-start.20 = (bf16[272,64]{1,0:T(8,128)(2,1)S(1)}, bf16[272,64]{1,0:T(8,128)(2,1)S(1)}, u32[]{:S(2)}, u32[]{:S(2)}) collective-permute-start(bf16[272,64]{1,0:T(8,128)(2,1)S(1)} %pad_maximum_fusion.11), channel_id=1, source_target_pairs={{0,16},{2,18},{4,20},{6,22},{8,24},{10,26},{12,28},{14,30},{16,0},... | collective-permute-start | bytes 104456 | tf_op jit(solution)/shard_map/ppermute | solution.py:37
  92.2 0.3 collective-permute-start.21
  92.8 3.3 %collective-permute-done.20 = bf16[272,64]{1,0:T(8,128)(2,1)S(1)} collective-permute-done((bf16[272,64]{1,0:T(8,128)(2,1)S(1)}, bf16[272,64]{1,0:T(8,128)(2,1)S(1)}, u32[]{:S(2)}, u32[]{:S(2)}) %collective-permute-start.20) | collective-permute-done | bytes 34848 | tf_op jit(solution)/shard_map/ppermute | solution.py:37
  96.1 2.4 %collective-permute-done.21 = bf16[272,64]{1,0:T(8,128)(2,1)S(1)} collective-permute-done((bf16[272,64]{1,0:T(8,128)(2,1)S(1)}, bf16[272,64]{1,0:T(8,128)(2,1)S(1)}, u32[]{:S(2)}, u32[]{:S(2)}) %collective-permute-start.21) | collective-permute-done | bytes 34848 | tf_op jit(solution)/shard_map/ppermute | solution.py:37
  98.7 1.3 %collective-permute-start.23 = (bf16[272,64]{1,0:T(8,128)(2,1)S(1)}, bf16[272,64]{1,0:T(8,128)(2,1)S(1)}, u32[]{:S(2)}, u32[]{:S(2)}) collective-permute-start(bf16[272,64]{1,0:T(8,128)(2,1)S(1)} %pad_maximum_fusion.13), channel_id=1, source_target_pairs={{0,16},{2,18},{4,20},{6,22},{8,24},{10,26},{12,28},{14,30},{16,0},... | collective-permute-start | bytes 104456 | tf_op jit(solution)/shard_map/ppermute | solution.py:51
  100.0 3.1 %collective-permute-start.24 = (bf16[272,64]{1,0:T(8,128)(2,1)S(1)}, bf16[272,64]{1,0:T(8,128)(2,1)S(1)}, u32[]{:S(2)}, u32[]{:S(2)}) collective-permute-start(bf16[272,64]{1,0:T(8,128)(2,1)S(1)} %pad_maximum_fusion.13), channel_id=1, source_target_pairs={{0,24},{2,26},{4,28},{6,30},{8,16},{10,18},{12,20},{14,22},{16,8},... | collective-permute-start | bytes 104456 | tf_op jit(solution)/shard_map/ppermute | solution.py:51
  103.1 0.3 dynamic_update_slice.56
  103.5 1.4 %dynamic_update_slice.57 = bf16[272,256]{1,0:T(8,128)(2,1)S(1)} dynamic-update-slice(bf16[272,256]{1,0:T(8,128)(2,1)S(1)} %dynamic_update_slice.56, bf16[272,64]{1,0:T(8,128)(2,1)} %collective-permute-done.22, s32[]{:T(128)} %constant.112.clone.1, s32[]{:T(128)S(6)} %select_n.32) | dynamic-update-slice | bytes 69636 | tf_op jit(solution)/shard_map/dynamic_update_slice | solution.py:55
  104.9 0.3 dynamic_update_slice.58
  105.2 1.0 collective-permute-done.24
  106.2 0.5 dynamic_update_slice.59
  106.8 0.9 collective-permute-start.25
  107.7 1.4 %collective-permute-start.26 = (bf16[272,256]{1,0:T(8,128)(2,1)S(1)}, bf16[272,256]{1,0:T(8,128)(2,1)S(1)}, u32[]{:S(2)}, u32[]{:S(2)}) collective-permute-start(bf16[272,256]{1,0:T(8,128)(2,1)S(1)} %dynamic_update_slice.59), channel_id=1, source_target_pairs={{0,4},{2,6},{4,0},{6,2},{8,12},{10,14},{12,8},{14,10},{16,20},{18,... | collective-permute-start | bytes 417800 | tf_op jit(solution)/shard_map/ppermute | solution.py:51
  109.1 1.3 %collective-permute-start.27 = (bf16[272,256]{1,0:T(8,128)(2,1)S(1)}, bf16[272,256]{1,0:T(8,128)(2,1)S(1)}, u32[]{:S(2)}, u32[]{:S(2)}) collective-permute-start(bf16[272,256]{1,0:T(8,128)(2,1)S(1)} %dynamic_update_slice.59), channel_id=1, source_target_pairs={{0,6},{2,4},{4,2},{6,0},{8,14},{10,12},{12,10},{14,8},{16,22},{18,... | collective-permute-start | bytes 417800 | tf_op jit(solution)/shard_map/ppermute | solution.py:51
  110.4 1.5 %collective-permute-done.25 = bf16[272,256]{1,0:T(8,128)(2,1)S(1)} collective-permute-done((bf16[272,256]{1,0:T(8,128)(2,1)S(1)}, bf16[272,256]{1,0:T(8,128)(2,1)S(1)}, u32[]{:S(2)}, u32[]{:S(2)}) %collective-permute-start.25) | collective-permute-done | bytes 139296 | tf_op jit(solution)/shard_map/ppermute | solution.py:51
  111.9 0.8 collective-permute-done.26
  112.8 2.3 %collective-permute-done.27 = bf16[272,256]{1,0:T(8,128)(2,1)S(1)} collective-permute-done((bf16[272,256]{1,0:T(8,128)(2,1)S(1)}, bf16[272,256]{1,0:T(8,128)(2,1)S(1)}, u32[]{:S(2)}, u32[]{:S(2)}) %collective-permute-start.27) | collective-permute-done | bytes 139296 | tf_op jit(solution)/shard_map/ppermute | solution.py:51
  115.1 4.7 %convolution_convert_fusion = bf16[256,3072]{1,0:T(8,128)(2,1)S(1)} fusion(bf16[3072,1024]{1,0:T(8,128)(2,1)} %constant_dynamic-update-slice_fusion, bf16[272,1024]{1,0:T(8,128)(2,1)S(1)} %constant_dynamic-update-slice_fusion.3), kind=kOutput, calls=%fused_computation.12 | convolution fusion | flops 1611399168 | bytes 8388608 | tf_op jit(solution)/shard_map/dot_general | solution.py:152
  120.1 0.6 collective-permute-start.28
  120.7 1.5 %collective-permute-done.28 = f32[128]{0:T(128)S(1)} collective-permute-done((f32[128]{0:T(128)S(1)}, f32[128]{0:T(128)S(1)}, u32[]{:S(2)}, u32[]{:S(2)}) %collective-permute-start.28) | collective-permute-done | bytes 544 | tf_op jit(solution)/shard_map/ppermute | solution.py:156
  122.2 2.9 %fusion.19 = (f32[128,3072]{1,0:T(8,128)}, f32[128,3072]{1,0:T(8,128)}) fusion(f32[128,3072]{1,0:T(8,128)S(1)} %get-tuple-element.100, bf16[128,3072]{1,0:T(8,128)(2,1)S(1)} %collective-permute-done.29, bf16[128,3072]{1,0:T(8,128)(2,1)S(1)} %copy-done.4, f32[128,3072]{1,0:T(8,128)S(1)} %copy-done, bf16[256,3072]{1,0:T(8,128)(2,1)S(1)} %convolution_convert_fusion, ...), kind=kLoop, calls=%fused_computation.38 | loop fusion | flops 8650752 | bytes 9454080 | tf_op jit(solution)/shard_map/sub | solution.py:177
  (136 shorter events, 4.1 us)
Async XLA Ops:
  0.6 2.9 %copy-start = (f32[128,3072]{1,0:T(8,128)S(1)}, f32[128,3072]{1,0:T(8,128)}, u32[]{:S(2)}) copy-start(f32[128,3072]{1,0:T(8,128)} %param.19) | copy-start | bytes 4718596
  0.6 2.9 %copy-start.5 = (f32[3072]{0:T(1024)S(1)}, f32[3072]{0:T(1024)}, u32[]{:S(2)}) copy-start(f32[3072]{0:T(1024)} %param.17) | copy-start | bytes 36868
  1.4 2.8 %copy-start.7 = (f32[1024]{0:T(1024)S(1)}, f32[1024]{0:T(1024)}, u32[]{:S(2)}) copy-start(f32[1024]{0:T(1024)} %param.18) | copy-start | bytes 12292
  1.4 2.9 %copy-start.6 = (s32[3072]{0:T(1024)S(1)}, s32[3072]{0:T(1024)}, u32[]{:S(2)}) copy-start(s32[3072]{0:T(1024)} %param.15) | copy-start | bytes 36868
  3.0 2.5 %collective-permute-start = (bf16[128,3072]{1,0:T(8,128)(2,1)S(1)}, bf16[128,3072]{1,0:T(8,128)(2,1)S(1)}, u32[]{:S(2)}, u32[]{:S(2)}) collective-permute-start(bf16[128,3072]{1,0:T(8,128)(2,1)S(1)} %select_convert_fusion), channel_id=1, source_target_pairs={{0,1},{1,0},{2,3},{3,2},{4,5},{5,4},{6,7},{7,6},{8,9},{9,8},{10,11... | collective-permute-start | bytes 2359304 | tf_op jit(solution)/shard_map/ppermute | solution.py:116
  4.3 6.2 %copy-start.10 = (bf16[2048,1024]{1,0:T(8,128)(2,1)S(1)}, bf16[2048,1024]{1,0:T(8,128)(2,1)}, u32[]{:S(2)}) copy-start(bf16[2048,1024]{1,0:T(8,128)(2,1)} %param.14) | copy-start | bytes 12582916
  13.4 9.6 %collective-permute-start.1 = (bf16[272,256]{1,0:T(8,128)(2,1)S(1)}, bf16[272,256]{1,0:T(8,128)(2,1)S(1)}, u32[]{:S(2)}, u32[]{:S(2)}) collective-permute-start(bf16[272,256]{1,0:T(8,128)(2,1)S(1)} %pad_maximum_fusion), channel_id=1, source_target_pairs={{0,2},{2,0},{4,6},{6,4},{8,10},{10,8},{12,14},{14,12},{16,18},{18,... | collective-permute-start | bytes 417800 | tf_op jit(solution)/shard_map/ppermute | solution.py:37
  16.3 8.5 %collective-permute-start.2 = (bf16[272,256]{1,0:T(8,128)(2,1)S(1)}, bf16[272,256]{1,0:T(8,128)(2,1)S(1)}, u32[]{:S(2)}, u32[]{:S(2)}) collective-permute-start(bf16[272,256]{1,0:T(8,128)(2,1)S(1)} %pad_maximum_fusion.1), channel_id=1, source_target_pairs={{0,4},{2,6},{4,0},{6,2},{8,12},{10,14},{12,8},{14,10},{16,20},{18,... | collective-permute-start | bytes 417800 | tf_op jit(solution)/shard_map/ppermute | solution.py:37
  17.9 6.9 %collective-permute-start.3 = (bf16[272,256]{1,0:T(8,128)(2,1)S(1)}, bf16[272,256]{1,0:T(8,128)(2,1)S(1)}, u32[]{:S(2)}, u32[]{:S(2)}) collective-permute-start(bf16[272,256]{1,0:T(8,128)(2,1)S(1)} %pad_maximum_fusion.2), channel_id=1, source_target_pairs={{0,6},{2,4},{4,2},{6,0},{8,14},{10,12},{12,10},{14,8},{16,22},{18,... | collective-permute-start | bytes 417800 | tf_op jit(solution)/shard_map/ppermute | solution.py:37
  25.2 11.1 %collective-permute-start.4 = (bf16[272,64]{1,0:T(8,128)(2,1)S(1)}, bf16[272,64]{1,0:T(8,128)(2,1)S(1)}, u32[]{:S(2)}, u32[]{:S(2)}) collective-permute-start(bf16[272,64]{1,0:T(8,128)(2,1)S(1)} %pad_maximum_fusion.6), channel_id=1, source_target_pairs={{0,8},{2,10},{4,12},{6,14},{8,0},{10,2},{12,4},{14,6},{16,24},{18,... | collective-permute-start | bytes 104456 | tf_op jit(solution)/shard_map/ppermute | solution.py:37
  26.9 9.5 %collective-permute-start.5 = (bf16[272,64]{1,0:T(8,128)(2,1)S(1)}, bf16[272,64]{1,0:T(8,128)(2,1)S(1)}, u32[]{:S(2)}, u32[]{:S(2)}) collective-permute-start(bf16[272,64]{1,0:T(8,128)(2,1)S(1)} %pad_maximum_fusion.7), channel_id=1, source_target_pairs={{0,16},{2,18},{4,20},{6,22},{8,24},{10,26},{12,28},{14,30},{16,0},... | collective-permute-start | bytes 104456 | tf_op jit(solution)/shard_map/ppermute | solution.py:37
  29.6 6.8 %collective-permute-start.6 = (bf16[272,64]{1,0:T(8,128)(2,1)S(1)}, bf16[272,64]{1,0:T(8,128)(2,1)S(1)}, u32[]{:S(2)}, u32[]{:S(2)}) collective-permute-start(bf16[272,64]{1,0:T(8,128)(2,1)S(1)} %pad_maximum_fusion.8), channel_id=1, source_target_pairs={{0,24},{2,26},{4,28},{6,30},{8,16},{10,18},{12,20},{14,22},{16,8},... | collective-permute-start | bytes 104456 | tf_op jit(solution)/shard_map/ppermute | solution.py:37
  36.6 12.3 %collective-permute-start.7 = (bf16[272,64]{1,0:T(8,128)(2,1)S(1)}, bf16[272,64]{1,0:T(8,128)(2,1)S(1)}, u32[]{:S(2)}, u32[]{:S(2)}) collective-permute-start(bf16[272,64]{1,0:T(8,128)(2,1)S(1)} %pad_maximum_fusion.9), channel_id=1, source_target_pairs={{0,8},{2,10},{4,12},{6,14},{8,0},{10,2},{12,4},{14,6},{16,24},{18,... | collective-permute-start | bytes 104456 | tf_op jit(solution)/shard_map/ppermute | solution.py:51
  37.4 11.6 %collective-permute-start.8 = (bf16[272,64]{1,0:T(8,128)(2,1)S(1)}, bf16[272,64]{1,0:T(8,128)(2,1)S(1)}, u32[]{:S(2)}, u32[]{:S(2)}) collective-permute-start(bf16[272,64]{1,0:T(8,128)(2,1)S(1)} %pad_maximum_fusion.9), channel_id=1, source_target_pairs={{0,16},{2,18},{4,20},{6,22},{8,24},{10,26},{12,28},{14,30},{16,0},... | collective-permute-start | bytes 104456 | tf_op jit(solution)/shard_map/ppermute | solution.py:51
  40.9 8.1 %collective-permute-start.9 = (bf16[272,64]{1,0:T(8,128)(2,1)S(1)}, bf16[272,64]{1,0:T(8,128)(2,1)S(1)}, u32[]{:S(2)}, u32[]{:S(2)}) collective-permute-start(bf16[272,64]{1,0:T(8,128)(2,1)S(1)} %pad_maximum_fusion.9), channel_id=1, source_target_pairs={{0,24},{2,26},{4,28},{6,30},{8,16},{10,18},{12,20},{14,22},{16,8},... | collective-permute-start | bytes 104456 | tf_op jit(solution)/shard_map/ppermute | solution.py:51
  50.5 6.8 %collective-permute-start.10 = (bf16[272,256]{1,0:T(8,128)(2,1)S(1)}, bf16[272,256]{1,0:T(8,128)(2,1)S(1)}, u32[]{:S(2)}, u32[]{:S(2)}) collective-permute-start(bf16[272,256]{1,0:T(8,128)(2,1)S(1)} %dynamic_update_slice.51), channel_id=1, source_target_pairs={{0,2},{2,0},{4,6},{6,4},{8,10},{10,8},{12,14},{14,12},{16,18},{18,... | collective-permute-start | bytes 417800 | tf_op jit(solution)/shard_map/ppermute | solution.py:51
  51.8 5.6 %collective-permute-start.11 = (bf16[272,256]{1,0:T(8,128)(2,1)S(1)}, bf16[272,256]{1,0:T(8,128)(2,1)S(1)}, u32[]{:S(2)}, u32[]{:S(2)}) collective-permute-start(bf16[272,256]{1,0:T(8,128)(2,1)S(1)} %dynamic_update_slice.51), channel_id=1, source_target_pairs={{0,4},{2,6},{4,0},{6,2},{8,12},{10,14},{12,8},{14,10},{16,20},{18,... | collective-permute-start | bytes 417800 | tf_op jit(solution)/shard_map/ppermute | solution.py:51
  52.7 6.0 %collective-permute-start.12 = (bf16[272,256]{1,0:T(8,128)(2,1)S(1)}, bf16[272,256]{1,0:T(8,128)(2,1)S(1)}, u32[]{:S(2)}, u32[]{:S(2)}) collective-permute-start(bf16[272,256]{1,0:T(8,128)(2,1)S(1)} %dynamic_update_slice.51), channel_id=1, source_target_pairs={{0,6},{2,4},{4,2},{6,0},{8,14},{10,12},{12,10},{14,8},{16,22},{18,... | collective-permute-start | bytes 417800 | tf_op jit(solution)/shard_map/ppermute | solution.py:51
  63.3 3.9 %copy-start.1 = (bf16[256,3072]{1,0:T(8,128)(2,1)}, bf16[256,3072]{1,0:T(8,128)(2,1)S(1)}, u32[]{:S(2)}) copy-start(bf16[256,3072]{1,0:T(8,128)(2,1)S(1)} %convolution_convert_fusion.1) | copy-start | bytes 4718596
  63.3 2.9 %collective-permute-start.14 = (bf16[128,3072]{1,0:T(8,128)(2,1)S(1)}, bf16[128,3072]{1,0:T(8,128)(2,1)S(1)}, u32[]{:S(2)}, u32[]{:S(2)}) collective-permute-start(bf16[128,3072]{1,0:T(8,128)(2,1)S(1)} %slice.446), channel_id=1, source_target_pairs={{0,1},{1,0},{2,3},{3,2},{4,5},{5,4},{6,7},{7,6},{8,9},{9,8},{10,11... | collective-permute-start | bytes 2359304 | tf_op jit(solution)/shard_map/ppermute | solution.py:157
  63.6 2.0 %collective-permute-start.13 = (f32[128]{0:T(128)S(1)}, f32[128]{0:T(128)S(1)}, u32[]{:S(2)}, u32[]{:S(2)}) collective-permute-start(f32[128]{0:T(128)S(1)} %slice.386), channel_id=1, source_target_pairs={{0,1},{1,0},{2,3},{3,2},{4,5},{5,4},{6,7},{7,6},{8,9},{9,8},{10,11... | collective-permute-start | bytes 1544 | tf_op jit(solution)/shard_map/ppermute | solution.py:156
  65.7 0.6 copy-start.8
  66.3 0.9 copy-start.3
  68.2 4.6 %collective-permute-start.15 = (bf16[128,3072]{1,0:T(8,128)(2,1)}, bf16[128,3072]{1,0:T(8,128)(2,1)}, u32[]{:S(2)}, u32[]{:S(2)}) collective-permute-start(bf16[128,3072]{1,0:T(8,128)(2,1)} %convert_element_type.364), channel_id=1, source_target_pairs={{0,1},{1,0},{2,3},{3,2},{4,5},{5,4},{6,7},{7,6},{8,9},{9,8},{10,11... | collective-permute-start | bytes 2359304 | tf_op jit(solution)/shard_map/ppermute | solution.py:116
  77.2 6.4 %collective-permute-start.16 = (bf16[272,256]{1,0:T(8,128)(2,1)S(1)}, bf16[272,256]{1,0:T(8,128)(2,1)S(1)}, u32[]{:S(2)}, u32[]{:S(2)}) collective-permute-start(bf16[272,256]{1,0:T(8,128)(2,1)S(1)} %pad_maximum_fusion.3), channel_id=1, source_target_pairs={{0,2},{2,0},{4,6},{6,4},{8,10},{10,8},{12,14},{14,12},{16,18},{18,... | collective-permute-start | bytes 417800 | tf_op jit(solution)/shard_map/ppermute | solution.py:37
  78.7 8.7 %collective-permute-start.17 = (bf16[272,256]{1,0:T(8,128)(2,1)S(1)}, bf16[272,256]{1,0:T(8,128)(2,1)S(1)}, u32[]{:S(2)}, u32[]{:S(2)}) collective-permute-start(bf16[272,256]{1,0:T(8,128)(2,1)S(1)} %pad_maximum_fusion.4), channel_id=1, source_target_pairs={{0,4},{2,6},{4,0},{6,2},{8,12},{10,14},{12,8},{14,10},{16,20},{18,... | collective-permute-start | bytes 417800 | tf_op jit(solution)/shard_map/ppermute | solution.py:37
  79.4 8.1 %collective-permute-start.18 = (bf16[272,256]{1,0:T(8,128)(2,1)S(1)}, bf16[272,256]{1,0:T(8,128)(2,1)S(1)}, u32[]{:S(2)}, u32[]{:S(2)}) collective-permute-start(bf16[272,256]{1,0:T(8,128)(2,1)S(1)} %pad_maximum_fusion.5), channel_id=1, source_target_pairs={{0,6},{2,4},{4,2},{6,0},{8,14},{10,12},{12,10},{14,8},{16,22},{18,... | collective-permute-start | bytes 417800 | tf_op jit(solution)/shard_map/ppermute | solution.py:37
  87.9 4.9 %collective-permute-start.19 = (bf16[272,64]{1,0:T(8,128)(2,1)S(1)}, bf16[272,64]{1,0:T(8,128)(2,1)S(1)}, u32[]{:S(2)}, u32[]{:S(2)}) collective-permute-start(bf16[272,64]{1,0:T(8,128)(2,1)S(1)} %pad_maximum_fusion.10), channel_id=1, source_target_pairs={{0,8},{2,10},{4,12},{6,14},{8,0},{10,2},{12,4},{14,6},{16,24},{18,... | collective-permute-start | bytes 104456 | tf_op jit(solution)/shard_map/ppermute | solution.py:37
  88.3 7.7 %collective-permute-start.20 = (bf16[272,64]{1,0:T(8,128)(2,1)S(1)}, bf16[272,64]{1,0:T(8,128)(2,1)S(1)}, u32[]{:S(2)}, u32[]{:S(2)}) collective-permute-start(bf16[272,64]{1,0:T(8,128)(2,1)S(1)} %pad_maximum_fusion.11), channel_id=1, source_target_pairs={{0,16},{2,18},{4,20},{6,22},{8,24},{10,26},{12,28},{14,30},{16,0},... | collective-permute-start | bytes 104456 | tf_op jit(solution)/shard_map/ppermute | solution.py:37
  92.2 6.2 %collective-permute-start.21 = (bf16[272,64]{1,0:T(8,128)(2,1)S(1)}, bf16[272,64]{1,0:T(8,128)(2,1)S(1)}, u32[]{:S(2)}, u32[]{:S(2)}) collective-permute-start(bf16[272,64]{1,0:T(8,128)(2,1)S(1)} %pad_maximum_fusion.12), channel_id=1, source_target_pairs={{0,24},{2,26},{4,28},{6,30},{8,16},{10,18},{12,20},{14,22},{16,8},... | collective-permute-start | bytes 104456 | tf_op jit(solution)/shard_map/ppermute | solution.py:37
  98.7 4.8 %collective-permute-start.22 = (bf16[272,64]{1,0:T(8,128)(2,1)S(1)}, bf16[272,64]{1,0:T(8,128)(2,1)}, u32[]{:S(2)}, u32[]{:S(2)}) collective-permute-start(bf16[272,64]{1,0:T(8,128)(2,1)S(1)} %pad_maximum_fusion.13), channel_id=1, source_target_pairs={{0,8},{2,10},{4,12},{6,14},{8,0},{10,2},{12,4},{14,6},{16,24},{18,... | collective-permute-start | bytes 104456 | tf_op jit(solution)/shard_map/ppermute | solution.py:51
  98.7 6.2 %collective-permute-start.23 = (bf16[272,64]{1,0:T(8,128)(2,1)S(1)}, bf16[272,64]{1,0:T(8,128)(2,1)S(1)}, u32[]{:S(2)}, u32[]{:S(2)}) collective-permute-start(bf16[272,64]{1,0:T(8,128)(2,1)S(1)} %pad_maximum_fusion.13), channel_id=1, source_target_pairs={{0,16},{2,18},{4,20},{6,22},{8,24},{10,26},{12,28},{14,30},{16,0},... | collective-permute-start | bytes 104456 | tf_op jit(solution)/shard_map/ppermute | solution.py:51
  100.0 6.2 %collective-permute-start.24 = (bf16[272,64]{1,0:T(8,128)(2,1)S(1)}, bf16[272,64]{1,0:T(8,128)(2,1)S(1)}, u32[]{:S(2)}, u32[]{:S(2)}) collective-permute-start(bf16[272,64]{1,0:T(8,128)(2,1)S(1)} %pad_maximum_fusion.13), channel_id=1, source_target_pairs={{0,24},{2,26},{4,28},{6,30},{8,16},{10,18},{12,20},{14,22},{16,8},... | collective-permute-start | bytes 104456 | tf_op jit(solution)/shard_map/ppermute | solution.py:51
  106.8 5.1 %collective-permute-start.25 = (bf16[272,256]{1,0:T(8,128)(2,1)S(1)}, bf16[272,256]{1,0:T(8,128)(2,1)S(1)}, u32[]{:S(2)}, u32[]{:S(2)}) collective-permute-start(bf16[272,256]{1,0:T(8,128)(2,1)S(1)} %dynamic_update_slice.59), channel_id=1, source_target_pairs={{0,2},{2,0},{4,6},{6,4},{8,10},{10,8},{12,14},{14,12},{16,18},{18,... | collective-permute-start | bytes 417800 | tf_op jit(solution)/shard_map/ppermute | solution.py:51
  107.7 5.1 %collective-permute-start.26 = (bf16[272,256]{1,0:T(8,128)(2,1)S(1)}, bf16[272,256]{1,0:T(8,128)(2,1)S(1)}, u32[]{:S(2)}, u32[]{:S(2)}) collective-permute-start(bf16[272,256]{1,0:T(8,128)(2,1)S(1)} %dynamic_update_slice.59), channel_id=1, source_target_pairs={{0,4},{2,6},{4,0},{6,2},{8,12},{10,14},{12,8},{14,10},{16,20},{18,... | collective-permute-start | bytes 417800 | tf_op jit(solution)/shard_map/ppermute | solution.py:51
  109.1 6.0 %collective-permute-start.27 = (bf16[272,256]{1,0:T(8,128)(2,1)S(1)}, bf16[272,256]{1,0:T(8,128)(2,1)S(1)}, u32[]{:S(2)}, u32[]{:S(2)}) collective-permute-start(bf16[272,256]{1,0:T(8,128)(2,1)S(1)} %dynamic_update_slice.59), channel_id=1, source_target_pairs={{0,6},{2,4},{4,2},{6,0},{8,14},{10,12},{12,10},{14,8},{16,22},{18,... | collective-permute-start | bytes 417800 | tf_op jit(solution)/shard_map/ppermute | solution.py:51
  115.1 7.2 %copy-start.4 = (bf16[128,3072]{1,0:T(8,128)(2,1)S(1)}, bf16[128,3072]{1,0:T(8,128)(2,1)}, u32[]{:S(2)}) copy-start(bf16[128,3072]{1,0:T(8,128)(2,1)} %copy-done.3) | copy-start | bytes 2359300
  119.8 2.4 %copy-start.9 = (f32[128]{0:T(128)S(1)}, f32[128]{0:T(128)}, u32[]{:S(2)}) copy-start(f32[128]{0:T(128)} %copy-done.8) | copy-start | bytes 1540
  119.8 2.5 %copy-start.2 = (bf16[256,3072]{1,0:T(8,128)(2,1)S(1)}, bf16[256,3072]{1,0:T(8,128)(2,1)}, u32[]{:S(2)}) copy-start(bf16[256,3072]{1,0:T(8,128)(2,1)} %copy-done.1) | copy-start | bytes 4718596
  119.8 2.4 %collective-permute-start.29 = (bf16[128,3072]{1,0:T(8,128)(2,1)S(1)}, bf16[128,3072]{1,0:T(8,128)(2,1)S(1)}, u32[]{:S(2)}, u32[]{:S(2)}) collective-permute-start(bf16[128,3072]{1,0:T(8,128)(2,1)S(1)} %slice.479), channel_id=1, source_target_pairs={{0,1},{1,0},{2,3},{3,2},{4,5},{5,4},{6,7},{7,6},{8,9},{9,8},{10,11... | collective-permute-start | bytes 2359304 | tf_op jit(solution)/shard_map/ppermute | solution.py:157
  120.1 2.0 %collective-permute-start.28 = (f32[128]{0:T(128)S(1)}, f32[128]{0:T(128)S(1)}, u32[]{:S(2)}, u32[]{:S(2)}) collective-permute-start(f32[128]{0:T(128)S(1)} %slice.427), channel_id=1, source_target_pairs={{0,1},{1,0},{2,3},{3,2},{4,5},{5,4},{6,7},{7,6},{8,9},{9,8},{10,11... | collective-permute-start | bytes 1544 | tf_op jit(solution)/shard_map/ppermute | solution.py:156

commit v6 on v1

--- a/solution.py
+++ b/solution.py
@@ -140,10 +140,17 @@
             ].astype(jnp.float32)
             wide = weights.astype(jnp.float32)
             energy = jnp.sum(wide * wide / spectrum[None, :], axis=1)
-            partials = lax.dot_general(
-                weights, features, (((1,), (1,)), ((), ())), preferred_element_type=jnp.float32
-            ).astype(jnp.bfloat16)
-            if pair:
+            def image_of(rows):
+                return lax.dot_general(
+                    rows, features, (((1,), (1,)), ((), ())), preferred_element_type=jnp.float32
+                ).astype(jnp.bfloat16)
+
+            partials = image_of(weights)
+            if pair and not first:
+                energy = energy[:own] + lax.ppermute(energy[own:], "eig", swap)
+                theirs = lax.ppermute(image_of(weights[own:]), "eig", swap)
+                image = image_of(weights[:own]).astype(jnp.float32) + theirs.astype(jnp.float32)
+            elif pair:
                 energy = energy[:own] + lax.ppermute(energy[own:], "eig", swap)
                 image = partials[:own].astype(jnp.float32) + lax.ppermute(
                     partials[own:], "eig", swap

time: 124 us -> 129 us (1.040)
  matrix products: 37.8 us -> 44.7 us
  other arithmetic: 8.79 us -> 7.41 us
    dot_general x2 -> x3, matrix products: 9.3 us -> 16.2 us  [image_of(): lax.dot_general(rows, features, (((1,), (1,)), ((), ())), preferred_eleme...]
    sub x1 -> x0, other arithmetic: 2.94 us -> none  [shards(): residual = residual - step_size[:, None] * along]
    add x0 -> x1, other arithmetic: none -> 1.57 us  [shards(): solution = solution + step_size[:, None] * direction]
    unnamed x26 -> x24, local copies, waits for them, and re-layouts: 3.57 us -> 4.23 us
  transfers between devices with their start and end apart: 30 -> 30, of which waited for: 15 -> 14; matrix products, arithmetic and copies ran while one was open for 19% -> 22% of each run, Pallas kernels for 0% -> 0%
where the time goes in v6:
time: 129 us
  matrix products  44.7 us (35%)
  starting transfers between devices  35.3 us (27%)
  waiting for transfers between devices  26.1 us (20%)
  local copies, waits for them, and re-layouts  13.1 us (10%)
  other arithmetic  7.41 us (6%)
  between operations  2.27 us (2%)
    ppermute x12, starting transfers between devices, vert_sum(): lax.ppermute(send, 'vert', [(i, i ^ masks[t + 1]) for i in range(n_vert)])  17.4 us
    dot_general x3, matrix products, image_of(): lax.dot_general(rows, features, (((1,), (1,)), ((), ())), preferred_eleme...  16.2 us
    ppermute x12, starting transfers between devices, vert_sum(): lax.ppermute(cur, 'vert', [(i, i ^ masks[t]) for i in range(n_vert)])  16 us
    dot_general x3, matrix products, work(): jnp.dot(rows, eig_table, preferred_element_type=jnp.float32)  16 us
    ppermute x12, waiting for transfers between devices, vert_sum(): lax.ppermute(send, 'vert', [(i, i ^ masks[t + 1]) for i in range(n_vert)])  14.2 us
    ppermute x12, waiting for transfers between devices, vert_sum(): lax.ppermute(cur, 'vert', [(i, i ^ masks[t]) for i in range(n_vert)])  6.46 us
    dot_general x1, matrix products, coeff_from_table(): summed = jnp.dot(rows, picker, preferred_element_type=jnp.float32)  5.09 us
    dot_general x1, matrix products, operate(): coeff = jnp.dot(rows, built[0], preferred_element_type=jnp.float32)  5.07 us
  transfers between devices with their start and end apart: 30, of which 14 were waited for; matrix products, arithmetic and copies ran while one was open for 22% of the time, Pallas kernels for 0%

profile of v6, /device:TPU:0, one launch (start us, length us, event | category | flops | bytes accessed | tf_op | source)
XLA Modules:
  0.0 128.9 jit_solution(6748160206989996539)
XLA Ops:
  1.5 1.5 %select_convert_fusion = bf16[128,3072]{1,0:T(8,128)(2,1)S(1)} fusion(f32[128,3072]{1,0:T(8,128)} %param.19, pred[3072]{0:T(1024)(128)(4,1)S(1)} %iota_compare_fusion.14), kind=kLoop, calls=%fused_computation.55 | loop fusion | flops 393216 | bytes 2362368 | tf_op jit(solution)/shard_map/convert_element_type | solution.py:114
  3.0 0.6 collective-permute-start
  3.6 0.4 fusion.22
  4.3 1.1 collective-permute-done
  5.5 5.1 %subtract_convert_fusion = (bf16[256,2048]{1,0:T(8,128)(2,1)S(1)}, bf16[256,2048]{1,0:T(8,128)(2,1)S(1)}) fusion(s32[3072]{0:T(1024)S(1)} %copy-done.6, bf16[128,3072]{1,0:T(8,128)(2,1)S(1)} %collective-permute-done, bf16[128,3072]{1,0:T(8,128)(2,1)S(1)} %select_convert_fusion), kind=kOutput, calls=%fused_computation.37 | convolution fusion | flops 3232759808 | bytes 3682304 | tf_op jit(solution)/shard_map/dot_general | solution.py:86
  10.6 2.4 %fusion.15 = f32[512,1024]{1,0:T(8,128)S(1)} fusion(bf16[2048,1024]{1,0:T(8,128)(2,1)S(1)} %copy-done.10, bf16[256,2048]{1,0:T(8,128)(2,1)S(1)} %get-tuple-element.115, bf16[256,2048]{1,0:T(8,128)(2,1)S(1)} %get-tuple-element.116), kind=kOutput, calls=%fused_computation.33 | convolution fusion | flops 2151677952 | bytes 8388608 | tf_op jit(solution)/shard_map/dot_general | solution.py:89
  13.4 2.9 %collective-permute-start.1 = (bf16[272,256]{1,0:T(8,128)(2,1)S(1)}, bf16[272,256]{1,0:T(8,128)(2,1)S(1)}, u32[]{:S(2)}, u32[]{:S(2)}) collective-permute-start(bf16[272,256]{1,0:T(8,128)(2,1)S(1)} %pad_maximum_fusion), channel_id=1, source_target_pairs={{0,2},{2,0},{4,6},{6,4},{8,10},{10,8},{12,14},{14,12},{16,18},{18,... | collective-permute-start | bytes 417800 | tf_op jit(solution)/shard_map/ppermute | solution.py:37
  16.3 1.6 %collective-permute-start.2 = (bf16[272,256]{1,0:T(8,128)(2,1)S(1)}, bf16[272,256]{1,0:T(8,128)(2,1)S(1)}, u32[]{:S(2)}, u32[]{:S(2)}) collective-permute-start(bf16[272,256]{1,0:T(8,128)(2,1)S(1)} %pad_maximum_fusion.1), channel_id=1, source_target_pairs={{0,4},{2,6},{4,0},{6,2},{8,12},{10,14},{12,8},{14,10},{16,20},{18,... | collective-permute-start | bytes 417800 | tf_op jit(solution)/shard_map/ppermute | solution.py:37
  18.0 5.0 %fusion.21 = bf16[1024,1024]{1,0:T(8,128)(2,1)S(1)} fusion(bf16[2048,1024]{1,0:T(8,128)(2,1)S(1)} %copy-done.10, s32[1024]{0:T(1024)S(1)} %get-tuple-element.65), kind=kOutput, calls=%fused_computation.40 | convolution fusion | flops 4298113024 | bytes 6295552 | tf_op jit(solution)/shard_map/dot_general | solution.py:79
  23.0 1.8 %collective-permute-done.2 = bf16[272,256]{1,0:T(8,128)(2,1)S(1)} collective-permute-done((bf16[272,256]{1,0:T(8,128)(2,1)S(1)}, bf16[272,256]{1,0:T(8,128)(2,1)S(1)}, u32[]{:S(2)}, u32[]{:S(2)}) %collective-permute-start.2) | collective-permute-done | bytes 139296 | tf_op jit(solution)/shard_map/ppermute | solution.py:37
  25.2 1.6 %collective-permute-start.4 = (bf16[272,64]{1,0:T(8,128)(2,1)S(1)}, bf16[272,64]{1,0:T(8,128)(2,1)S(1)}, u32[]{:S(2)}, u32[]{:S(2)}) collective-permute-start(bf16[272,64]{1,0:T(8,128)(2,1)S(1)} %pad_maximum_fusion.6), channel_id=1, source_target_pairs={{0,8},{2,10},{4,12},{6,14},{8,0},{10,2},{12,4},{14,6},{16,24},{18,... | collective-permute-start | bytes 104456 | tf_op jit(solution)/shard_map/ppermute | solution.py:37
  26.9 2.7 %collective-permute-start.5 = (bf16[272,64]{1,0:T(8,128)(2,1)S(1)}, bf16[272,64]{1,0:T(8,128)(2,1)S(1)}, u32[]{:S(2)}, u32[]{:S(2)}) collective-permute-start(bf16[272,64]{1,0:T(8,128)(2,1)S(1)} %pad_maximum_fusion.7), channel_id=1, source_target_pairs={{0,16},{2,18},{4,20},{6,22},{8,24},{10,26},{12,28},{14,30},{16,0},... | collective-permute-start | bytes 104456 | tf_op jit(solution)/shard_map/ppermute | solution.py:37
  29.9 5.0 %fusion.20 = bf16[1024,1024]{1,0:T(8,128)(2,1)S(1)} fusion(bf16[2048,1024]{1,0:T(8,128)(2,1)S(1)} %copy-done.10, s32[1024]{0:T(1024)S(1)} %get-tuple-element.69), kind=kOutput, calls=%fused_computation.39 | convolution fusion | flops 4298113024 | bytes 6295552 | tf_op jit(solution)/shard_map/dot_general | solution.py:79
  34.8 1.5 %constant_dynamic-update-slice_fusion.2 = bf16[3072,1024]{1,0:T(8,128)(2,1)} fusion(bf16[1024,1024]{1,0:T(8,128)(2,1)S(1)} %fusion.21), kind=kLoop, calls=%fused_computation.138 | loop fusion | bytes 4194304
  36.7 0.7 collective-permute-start.7
  37.4 3.5 %collective-permute-start.8 = (bf16[272,64]{1,0:T(8,128)(2,1)S(1)}, bf16[272,64]{1,0:T(8,128)(2,1)S(1)}, u32[]{:S(2)}, u32[]{:S(2)}) collective-permute-start(bf16[272,64]{1,0:T(8,128)(2,1)S(1)} %pad_maximum_fusion.9), channel_id=1, source_target_pairs={{0,16},{2,18},{4,20},{6,22},{8,24},{10,26},{12,28},{14,30},{16,0},... | collective-permute-start | bytes 104456 | tf_op jit(solution)/shard_map/ppermute | solution.py:51
  41.1 6.0 %fusion.19 = bf16[1024,1024]{1,0:T(8,128)(2,1)} fusion(bf16[2048,1024]{1,0:T(8,128)(2,1)S(1)} %copy-done.10, s32[1024]{0:T(1024)S(1)} %get-tuple-element.73), kind=kOutput, calls=%fused_computation.38 | convolution fusion | flops 4298113024 | bytes 6295552 | tf_op jit(solution)/shard_map/dot_general | solution.py:79
  47.1 1.5 %constant_dynamic-update-slice_fusion.1 = bf16[3072,1024]{1,0:T(8,128)(2,1)} fusion(bf16[3072,1024]{1,0:T(8,128)(2,1)} %constant_dynamic-update-slice_fusion.2, bf16[1024,1024]{1,0:T(8,128)(2,1)S(1)} %fusion.20), kind=kLoop, calls=%fused_computation.137 | loop fusion | bytes 4194304
  48.6 0.3 dynamic_update_slice.48
  49.0 0.6 dynamic_update_slice.49
  49.7 0.3 dynamic_update_slice.50
  50.0 0.6 dynamic_update_slice.51
  50.5 1.2 collective-permute-start.10
  51.8 0.9 collective-permute-start.11
  52.7 1.4 %collective-permute-start.12 = (bf16[272,256]{1,0:T(8,128)(2,1)S(1)}, bf16[272,256]{1,0:T(8,128)(2,1)S(1)}, u32[]{:S(2)}, u32[]{:S(2)}) collective-permute-start(bf16[272,256]{1,0:T(8,128)(2,1)S(1)} %dynamic_update_slice.51), channel_id=1, source_target_pairs={{0,6},{2,4},{4,2},{6,0},{8,14},{10,12},{12,10},{14,8},{16,22},{18,... | collective-permute-start | bytes 417800 | tf_op jit(solution)/shard_map/ppermute | solution.py:51
  54.1 3.1 %constant_dynamic-update-slice_fusion = bf16[3072,1024]{1,0:T(8,128)(2,1)} fusion(bf16[3072,1024]{1,0:T(8,128)(2,1)} %constant_dynamic-update-slice_fusion.1, bf16[1024,1024]{1,0:T(8,128)(2,1)} %fusion.19), kind=kLoop, calls=%fused_computation.136 | loop fusion | bytes 4194304 | tf_op jit(solution)/shard_map/concatenate | solution.py:135
  57.4 1.2 collective-permute-done.12
  58.6 4.6 %convolution_convert_fusion = bf16[256,3072]{1,0:T(8,128)(2,1)S(1)} fusion(bf16[3072,1024]{1,0:T(8,128)(2,1)} %constant_dynamic-update-slice_fusion, bf16[272,1024]{1,0:T(8,128)(2,1)S(1)} %constant_dynamic-update-slice_fusion.7), kind=kOutput, calls=%fused_computation.12 | convolution fusion | flops 1611399168 | bytes 8388608 | tf_op jit(solution)/shard_map/dot_general | solution.py:144
  63.6 0.6 collective-permute-start.13
  64.2 1.5 %collective-permute-done.13 = f32[128]{0:T(128)S(1)} collective-permute-done((f32[128]{0:T(128)S(1)}, f32[128]{0:T(128)S(1)}, u32[]{:S(2)}, u32[]{:S(2)}) %collective-permute-start.13) | collective-permute-done | bytes 544 | tf_op jit(solution)/shard_map/ppermute | solution.py:154
  65.7 0.6 copy-done.8
  66.3 0.9 fusion.23
  67.2 1.0 convert_element_type.367
  68.4 0.4 scatter.19
  68.7 2.1 %collective-permute-done.15 = bf16[128,3072]{1,0:T(8,128)(2,1)} collective-permute-done((bf16[128,3072]{1,0:T(8,128)(2,1)}, bf16[128,3072]{1,0:T(8,128)(2,1)}, u32[]{:S(2)}, u32[]{:S(2)}) %collective-permute-start.15) | collective-permute-done | bytes 786464 | tf_op jit(solution)/shard_map/ppermute | solution.py:116
  70.8 5.1 %fusion.31 = f32[256,1024]{1,0:T(8,128)S(1)} fusion(bf16[3072,1024]{1,0:T(8,128)(2,1)} %constant_dynamic-update-slice_fusion, bf16[128,3072]{1,0:T(8,128)(2,1)} %collective-permute-done.15, bf16[128,3072]{1,0:T(8,128)(2,1)} %convert_element_type.367, f32[1024]{0:T(1024)S(1)} %power_multiply_fusion), kind=kOutput, calls=%fused_computation.54 | convolution fusion | flops 1614020608 | bytes 8916992 | tf_op jit(solution)/shard_map/dot_general | solution.py:122
  76.1 1.5 %collective-permute-start.16 = (bf16[272,256]{1,0:T(8,128)(2,1)S(1)}, bf16[272,256]{1,0:T(8,128)(2,1)S(1)}, u32[]{:S(2)}, u32[]{:S(2)}) collective-permute-start(bf16[272,256]{1,0:T(8,128)(2,1)S(1)} %pad_maximum_fusion.3), channel_id=1, source_target_pairs={{0,2},{2,0},{4,6},{6,4},{8,10},{10,8},{12,14},{14,12},{16,18},{18,... | collective-permute-start | bytes 417800 | tf_op jit(solution)/shard_map/ppermute | solution.py:37
  77.7 0.7 collective-permute-start.17
  78.4 1.5 %collective-permute-start.18 = (bf16[272,256]{1,0:T(8,128)(2,1)S(1)}, bf16[272,256]{1,0:T(8,128)(2,1)S(1)}, u32[]{:S(2)}, u32[]{:S(2)}) collective-permute-start(bf16[272,256]{1,0:T(8,128)(2,1)S(1)} %pad_maximum_fusion.5), channel_id=1, source_target_pairs={{0,6},{2,4},{4,2},{6,0},{8,14},{10,12},{12,10},{14,8},{16,22},{18,... | collective-permute-start | bytes 417800 | tf_op jit(solution)/shard_map/ppermute | solution.py:37
  79.8 2.5 %collective-permute-done.16 = bf16[272,256]{1,0:T(8,128)(2,1)S(1)} collective-permute-done((bf16[272,256]{1,0:T(8,128)(2,1)S(1)}, bf16[272,256]{1,0:T(8,128)(2,1)S(1)}, u32[]{:S(2)}, u32[]{:S(2)}) %collective-permute-start.16) | collective-permute-done | bytes 139296 | tf_op jit(solution)/shard_map/ppermute | solution.py:37
  82.3 3.8 %collective-permute-done.17 = bf16[272,256]{1,0:T(8,128)(2,1)S(1)} collective-permute-done((bf16[272,256]{1,0:T(8,128)(2,1)S(1)}, bf16[272,256]{1,0:T(8,128)(2,1)S(1)}, u32[]{:S(2)}, u32[]{:S(2)}) %collective-permute-start.17) | collective-permute-done | bytes 139296 | tf_op jit(solution)/shard_map/ppermute | solution.py:37
  86.6 0.4 collective-permute-start.19
  87.0 3.9 %collective-permute-start.20 = (bf16[272,64]{1,0:T(8,128)(2,1)S(1)}, bf16[272,64]{1,0:T(8,128)(2,1)S(1)}, u32[]{:S(2)}, u32[]{:S(2)}) collective-permute-start(bf16[272,64]{1,0:T(8,128)(2,1)S(1)} %pad_maximum_fusion.11), channel_id=1, source_target_pairs={{0,16},{2,18},{4,20},{6,22},{8,24},{10,26},{12,28},{14,30},{16,0},... | collective-permute-start | bytes 104456 | tf_op jit(solution)/shard_map/ppermute | solution.py:37
  91.3 3.4 %collective-permute-done.20 = bf16[272,64]{1,0:T(8,128)(2,1)S(1)} collective-permute-done((bf16[272,64]{1,0:T(8,128)(2,1)S(1)}, bf16[272,64]{1,0:T(8,128)(2,1)S(1)}, u32[]{:S(2)}, u32[]{:S(2)}) %collective-permute-start.20) | collective-permute-done | bytes 34848 | tf_op jit(solution)/shard_map/ppermute | solution.py:37
  94.7 2.7 %collective-permute-done.21 = bf16[272,64]{1,0:T(8,128)(2,1)S(1)} collective-permute-done((bf16[272,64]{1,0:T(8,128)(2,1)S(1)}, bf16[272,64]{1,0:T(8,128)(2,1)S(1)}, u32[]{:S(2)}, u32[]{:S(2)}) %collective-permute-start.21) | collective-permute-done | bytes 34848 | tf_op jit(solution)/shard_map/ppermute | solution.py:37
  97.7 1.0 collective-permute-start.23
  98.7 3.4 %collective-permute-start.24 = (bf16[272,64]{1,0:T(8,128)(2,1)S(1)}, bf16[272,64]{1,0:T(8,128)(2,1)S(1)}, u32[]{:S(2)}, u32[]{:S(2)}) collective-permute-start(bf16[272,64]{1,0:T(8,128)(2,1)S(1)} %pad_maximum_fusion.13), channel_id=1, source_target_pairs={{0,24},{2,26},{4,28},{6,30},{8,16},{10,18},{12,20},{14,22},{16,8},... | collective-permute-start | bytes 104456 | tf_op jit(solution)/shard_map/ppermute | solution.py:51
  102.1 0.3 dynamic_update_slice.56
  102.4 1.4 %dynamic_update_slice.57 = bf16[272,256]{1,0:T(8,128)(2,1)S(1)} dynamic-update-slice(bf16[272,256]{1,0:T(8,128)(2,1)S(1)} %dynamic_update_slice.56, bf16[272,64]{1,0:T(8,128)(2,1)} %collective-permute-done.22, s32[]{:T(128)} %constant.112.clone.1, s32[]{:T(128)S(6)} %select_n.32) | dynamic-update-slice | bytes 69636 | tf_op jit(solution)/shard_map/dynamic_update_slice | solution.py:55
  103.9 0.3 dynamic_update_slice.58
  104.2 1.0 collective-permute-done.24
  105.2 0.5 dynamic_update_slice.59
  105.8 0.4 collective-permute-start.25
  106.2 1.5 %collective-permute-start.26 = (bf16[272,256]{1,0:T(8,128)(2,1)S(1)}, bf16[272,256]{1,0:T(8,128)(2,1)S(1)}, u32[]{:S(2)}, u32[]{:S(2)}) collective-permute-start(bf16[272,256]{1,0:T(8,128)(2,1)S(1)} %dynamic_update_slice.59), channel_id=1, source_target_pairs={{0,4},{2,6},{4,0},{6,2},{8,12},{10,14},{12,8},{14,10},{16,20},{18,... | collective-permute-start | bytes 417800 | tf_op jit(solution)/shard_map/ppermute | solution.py:51
  107.7 1.7 %collective-permute-start.27 = (bf16[272,256]{1,0:T(8,128)(2,1)S(1)}, bf16[272,256]{1,0:T(8,128)(2,1)S(1)}, u32[]{:S(2)}, u32[]{:S(2)}) collective-permute-start(bf16[272,256]{1,0:T(8,128)(2,1)S(1)} %dynamic_update_slice.59), channel_id=1, source_target_pairs={{0,6},{2,4},{4,2},{6,0},{8,14},{10,12},{12,10},{14,8},{16,22},{18,... | collective-permute-start | bytes 417800 | tf_op jit(solution)/shard_map/ppermute | solution.py:51
  109.4 1.5 %collective-permute-done.25 = bf16[272,256]{1,0:T(8,128)(2,1)S(1)} collective-permute-done((bf16[272,256]{1,0:T(8,128)(2,1)S(1)}, bf16[272,256]{1,0:T(8,128)(2,1)S(1)}, u32[]{:S(2)}, u32[]{:S(2)}) %collective-permute-start.25) | collective-permute-done | bytes 139296 | tf_op jit(solution)/shard_map/ppermute | solution.py:51
  110.9 0.3 collective-permute-done.26
  111.2 2.4 %collective-permute-done.27 = bf16[272,256]{1,0:T(8,128)(2,1)S(1)} collective-permute-done((bf16[272,256]{1,0:T(8,128)(2,1)S(1)}, bf16[272,256]{1,0:T(8,128)(2,1)S(1)}, u32[]{:S(2)}, u32[]{:S(2)}) %collective-permute-start.27) | collective-permute-done | bytes 139296 | tf_op jit(solution)/shard_map/ppermute | solution.py:51
  113.8 5.0 %convolution_convert_fusion.1 = bf16[128,3072]{1,0:T(8,128)(2,1)S(1)} fusion(bf16[3072,1024]{1,0:T(8,128)(2,1)} %constant_dynamic-update-slice_fusion, bf16[272,1024]{1,0:T(8,128)(2,1)S(1)} %constant_dynamic-update-slice_fusion.3), kind=kOutput, calls=%fused_computation.13 | convolution fusion | flops 805699584 | bytes 7340032 | tf_op jit(solution)/shard_map/dot_general | solution.py:144
  118.9 0.5 collective-permute-start.29
  119.4 0.6 collective-permute-done.28
  120.1 1.6 %multiply_add_fusion.1 = f32[128,3072]{1,0:T(8,128)} fusion(f32[128,3072]{1,0:T(8,128)S(1)} %get-tuple-element.100, f32[128,3072]{1,0:T(8,128)S(1)} %copy-done, f32[128]{0:T(128)S(1)} %get-tuple-element.85, f32[128]{0:T(128)S(1)} %get-tuple-element.84, f32[128]{0:T(128)S(1)} %fusion.63, pred[3072]{0:T(1024)(128)(4,1)S(1)} %iota_compare_fusion.14), kind=kLoop, calls=%fused_computation.50 | loop fusion | flops 2359296 | bytes 4723200 | tf_op jit(solution)/shard_map/add | solution.py:174
  121.7 0.6 copy-done.4
  122.3 6.6 %fusion.14 = f32[128,3072]{1,0:T(8,128)} fusion(f32[128,3072]{1,0:T(8,128)S(1)} %get-tuple-element.100, bf16[3072,1024]{1,0:T(8,128)(2,1)} %constant_dynamic-update-slice_fusion, bf16[128,3072]{1,0:T(8,128)(2,1)S(1)} %collective-permute-done.29, bf16[128,3072]{1,0:T(8,128)(2,1)S(1)} %copy-done.4, f32[128,3072]{1,0:T(8,128)S(1)} %copy-done, ...), kind=kOutput, calls=%fused_computation.21 | convolution fusion | flops 812384256 | bytes 13647872 | tf_op jit(solution)/shard_map/dot_general | solution.py:144
  (134 shorter events, 4.2 us)
Async XLA Ops:
  0.6 2.9 %copy-start = (f32[128,3072]{1,0:T(8,128)S(1)}, f32[128,3072]{1,0:T(8,128)}, u32[]{:S(2)}) copy-start(f32[128,3072]{1,0:T(8,128)} %param.19) | copy-start | bytes 4718596
  0.6 2.9 %copy-start.5 = (f32[3072]{0:T(1024)S(1)}, f32[3072]{0:T(1024)}, u32[]{:S(2)}) copy-start(f32[3072]{0:T(1024)} %param.17) | copy-start | bytes 36868
  1.4 2.8 %copy-start.7 = (f32[1024]{0:T(1024)S(1)}, f32[1024]{0:T(1024)}, u32[]{:S(2)}) copy-start(f32[1024]{0:T(1024)} %param.18) | copy-start | bytes 12292
  1.4 2.8 %copy-start.6 = (s32[3072]{0:T(1024)S(1)}, s32[3072]{0:T(1024)}, u32[]{:S(2)}) copy-start(s32[3072]{0:T(1024)} %param.15) | copy-start | bytes 36868
  3.0 2.5 %collective-permute-start = (bf16[128,3072]{1,0:T(8,128)(2,1)S(1)}, bf16[128,3072]{1,0:T(8,128)(2,1)S(1)}, u32[]{:S(2)}, u32[]{:S(2)}) collective-permute-start(bf16[128,3072]{1,0:T(8,128)(2,1)S(1)} %select_convert_fusion), channel_id=1, source_target_pairs={{0,1},{1,0},{2,3},{3,2},{4,5},{5,4},{6,7},{7,6},{8,9},{9,8},{10,11... | collective-permute-start | bytes 2359304 | tf_op jit(solution)/shard_map/ppermute | solution.py:116
  4.3 6.3 %copy-start.10 = (bf16[2048,1024]{1,0:T(8,128)(2,1)S(1)}, bf16[2048,1024]{1,0:T(8,128)(2,1)}, u32[]{:S(2)}) copy-start(bf16[2048,1024]{1,0:T(8,128)(2,1)} %param.14) | copy-start | bytes 12582916
  13.4 9.6 %collective-permute-start.1 = (bf16[272,256]{1,0:T(8,128)(2,1)S(1)}, bf16[272,256]{1,0:T(8,128)(2,1)S(1)}, u32[]{:S(2)}, u32[]{:S(2)}) collective-permute-start(bf16[272,256]{1,0:T(8,128)(2,1)S(1)} %pad_maximum_fusion), channel_id=1, source_target_pairs={{0,2},{2,0},{4,6},{6,4},{8,10},{10,8},{12,14},{14,12},{16,18},{18,... | collective-permute-start | bytes 417800 | tf_op jit(solution)/shard_map/ppermute | solution.py:37
  16.3 8.5 %collective-permute-start.2 = (bf16[272,256]{1,0:T(8,128)(2,1)S(1)}, bf16[272,256]{1,0:T(8,128)(2,1)S(1)}, u32[]{:S(2)}, u32[]{:S(2)}) collective-permute-start(bf16[272,256]{1,0:T(8,128)(2,1)S(1)} %pad_maximum_fusion.1), channel_id=1, source_target_pairs={{0,4},{2,6},{4,0},{6,2},{8,12},{10,14},{12,8},{14,10},{16,20},{18,... | collective-permute-start | bytes 417800 | tf_op jit(solution)/shard_map/ppermute | solution.py:37
  17.9 6.9 %collective-permute-start.3 = (bf16[272,256]{1,0:T(8,128)(2,1)S(1)}, bf16[272,256]{1,0:T(8,128)(2,1)S(1)}, u32[]{:S(2)}, u32[]{:S(2)}) collective-permute-start(bf16[272,256]{1,0:T(8,128)(2,1)S(1)} %pad_maximum_fusion.2), channel_id=1, source_target_pairs={{0,6},{2,4},{4,2},{6,0},{8,14},{10,12},{12,10},{14,8},{16,22},{18,... | collective-permute-start | bytes 417800 | tf_op jit(solution)/shard_map/ppermute | solution.py:37
  25.2 11.1 %collective-permute-start.4 = (bf16[272,64]{1,0:T(8,128)(2,1)S(1)}, bf16[272,64]{1,0:T(8,128)(2,1)S(1)}, u32[]{:S(2)}, u32[]{:S(2)}) collective-permute-start(bf16[272,64]{1,0:T(8,128)(2,1)S(1)} %pad_maximum_fusion.6), channel_id=1, source_target_pairs={{0,8},{2,10},{4,12},{6,14},{8,0},{10,2},{12,4},{14,6},{16,24},{18,... | collective-permute-start | bytes 104456 | tf_op jit(solution)/shard_map/ppermute | solution.py:37
  26.9 9.5 %collective-permute-start.5 = (bf16[272,64]{1,0:T(8,128)(2,1)S(1)}, bf16[272,64]{1,0:T(8,128)(2,1)S(1)}, u32[]{:S(2)}, u32[]{:S(2)}) collective-permute-start(bf16[272,64]{1,0:T(8,128)(2,1)S(1)} %pad_maximum_fusion.7), channel_id=1, source_target_pairs={{0,16},{2,18},{4,20},{6,22},{8,24},{10,26},{12,28},{14,30},{16,0},... | collective-permute-start | bytes 104456 | tf_op jit(solution)/shard_map/ppermute | solution.py:37
  29.6 6.8 %collective-permute-start.6 = (bf16[272,64]{1,0:T(8,128)(2,1)S(1)}, bf16[272,64]{1,0:T(8,128)(2,1)S(1)}, u32[]{:S(2)}, u32[]{:S(2)}) collective-permute-start(bf16[272,64]{1,0:T(8,128)(2,1)S(1)} %pad_maximum_fusion.8), channel_id=1, source_target_pairs={{0,24},{2,26},{4,28},{6,30},{8,16},{10,18},{12,20},{14,22},{16,8},... | collective-permute-start | bytes 104456 | tf_op jit(solution)/shard_map/ppermute | solution.py:37
  36.7 12.3 %collective-permute-start.7 = (bf16[272,64]{1,0:T(8,128)(2,1)S(1)}, bf16[272,64]{1,0:T(8,128)(2,1)S(1)}, u32[]{:S(2)}, u32[]{:S(2)}) collective-permute-start(bf16[272,64]{1,0:T(8,128)(2,1)S(1)} %pad_maximum_fusion.9), channel_id=1, source_target_pairs={{0,8},{2,10},{4,12},{6,14},{8,0},{10,2},{12,4},{14,6},{16,24},{18,... | collective-permute-start | bytes 104456 | tf_op jit(solution)/shard_map/ppermute | solution.py:51
  37.4 11.6 %collective-permute-start.8 = (bf16[272,64]{1,0:T(8,128)(2,1)S(1)}, bf16[272,64]{1,0:T(8,128)(2,1)S(1)}, u32[]{:S(2)}, u32[]{:S(2)}) collective-permute-start(bf16[272,64]{1,0:T(8,128)(2,1)S(1)} %pad_maximum_fusion.9), channel_id=1, source_target_pairs={{0,16},{2,18},{4,20},{6,22},{8,24},{10,26},{12,28},{14,30},{16,0},... | collective-permute-start | bytes 104456 | tf_op jit(solution)/shard_map/ppermute | solution.py:51
  40.9 8.1 %collective-permute-start.9 = (bf16[272,64]{1,0:T(8,128)(2,1)S(1)}, bf16[272,64]{1,0:T(8,128)(2,1)S(1)}, u32[]{:S(2)}, u32[]{:S(2)}) collective-permute-start(bf16[272,64]{1,0:T(8,128)(2,1)S(1)} %pad_maximum_fusion.9), channel_id=1, source_target_pairs={{0,24},{2,26},{4,28},{6,30},{8,16},{10,18},{12,20},{14,22},{16,8},... | collective-permute-start | bytes 104456 | tf_op jit(solution)/shard_map/ppermute | solution.py:51
  50.5 6.8 %collective-permute-start.10 = (bf16[272,256]{1,0:T(8,128)(2,1)S(1)}, bf16[272,256]{1,0:T(8,128)(2,1)S(1)}, u32[]{:S(2)}, u32[]{:S(2)}) collective-permute-start(bf16[272,256]{1,0:T(8,128)(2,1)S(1)} %dynamic_update_slice.51), channel_id=1, source_target_pairs={{0,2},{2,0},{4,6},{6,4},{8,10},{10,8},{12,14},{14,12},{16,18},{18,... | collective-permute-start | bytes 417800 | tf_op jit(solution)/shard_map/ppermute | solution.py:51
  51.8 5.6 %collective-permute-start.11 = (bf16[272,256]{1,0:T(8,128)(2,1)S(1)}, bf16[272,256]{1,0:T(8,128)(2,1)S(1)}, u32[]{:S(2)}, u32[]{:S(2)}) collective-permute-start(bf16[272,256]{1,0:T(8,128)(2,1)S(1)} %dynamic_update_slice.51), channel_id=1, source_target_pairs={{0,4},{2,6},{4,0},{6,2},{8,12},{10,14},{12,8},{14,10},{16,20},{18,... | collective-permute-start | bytes 417800 | tf_op jit(solution)/shard_map/ppermute | solution.py:51
  52.7 6.0 %collective-permute-start.12 = (bf16[272,256]{1,0:T(8,128)(2,1)S(1)}, bf16[272,256]{1,0:T(8,128)(2,1)S(1)}, u32[]{:S(2)}, u32[]{:S(2)}) collective-permute-start(bf16[272,256]{1,0:T(8,128)(2,1)S(1)} %dynamic_update_slice.51), channel_id=1, source_target_pairs={{0,6},{2,4},{4,2},{6,0},{8,14},{10,12},{12,10},{14,8},{16,22},{18,... | collective-permute-start | bytes 417800 | tf_op jit(solution)/shard_map/ppermute | solution.py:51
  63.3 4.0 %copy-start.1 = (bf16[256,3072]{1,0:T(8,128)(2,1)}, bf16[256,3072]{1,0:T(8,128)(2,1)S(1)}, u32[]{:S(2)}) copy-start(bf16[256,3072]{1,0:T(8,128)(2,1)S(1)} %convolution_convert_fusion) | copy-start | bytes 4718596
  63.3 2.9 %collective-permute-start.14 = (bf16[128,3072]{1,0:T(8,128)(2,1)S(1)}, bf16[128,3072]{1,0:T(8,128)(2,1)S(1)}, u32[]{:S(2)}, u32[]{:S(2)}) collective-permute-start(bf16[128,3072]{1,0:T(8,128)(2,1)S(1)} %slice.448), channel_id=1, source_target_pairs={{0,1},{1,0},{2,3},{3,2},{4,5},{5,4},{6,7},{7,6},{8,9},{9,8},{10,11... | collective-permute-start | bytes 2359304 | tf_op jit(solution)/shard_map/ppermute | solution.py:155
  63.6 2.0 %collective-permute-start.13 = (f32[128]{0:T(128)S(1)}, f32[128]{0:T(128)S(1)}, u32[]{:S(2)}, u32[]{:S(2)}) collective-permute-start(f32[128]{0:T(128)S(1)} %slice.388), channel_id=1, source_target_pairs={{0,1},{1,0},{2,3},{3,2},{4,5},{5,4},{6,7},{7,6},{8,9},{9,8},{10,11... | collective-permute-start | bytes 1544 | tf_op jit(solution)/shard_map/ppermute | solution.py:154
  65.7 0.6 copy-start.8
  66.3 0.9 copy-start.3
  68.2 2.6 %collective-permute-start.15 = (bf16[128,3072]{1,0:T(8,128)(2,1)}, bf16[128,3072]{1,0:T(8,128)(2,1)}, u32[]{:S(2)}, u32[]{:S(2)}) collective-permute-start(bf16[128,3072]{1,0:T(8,128)(2,1)} %convert_element_type.367), channel_id=1, source_target_pairs={{0,1},{1,0},{2,3},{3,2},{4,5},{5,4},{6,7},{7,6},{8,9},{9,8},{10,11... | collective-permute-start | bytes 2359304 | tf_op jit(solution)/shard_map/ppermute | solution.py:116
  76.1 6.2 %collective-permute-start.16 = (bf16[272,256]{1,0:T(8,128)(2,1)S(1)}, bf16[272,256]{1,0:T(8,128)(2,1)S(1)}, u32[]{:S(2)}, u32[]{:S(2)}) collective-permute-start(bf16[272,256]{1,0:T(8,128)(2,1)S(1)} %pad_maximum_fusion.3), channel_id=1, source_target_pairs={{0,2},{2,0},{4,6},{6,4},{8,10},{10,8},{12,14},{14,12},{16,18},{18,... | collective-permute-start | bytes 417800 | tf_op jit(solution)/shard_map/ppermute | solution.py:37
  77.7 8.5 %collective-permute-start.17 = (bf16[272,256]{1,0:T(8,128)(2,1)S(1)}, bf16[272,256]{1,0:T(8,128)(2,1)S(1)}, u32[]{:S(2)}, u32[]{:S(2)}) collective-permute-start(bf16[272,256]{1,0:T(8,128)(2,1)S(1)} %pad_maximum_fusion.4), channel_id=1, source_target_pairs={{0,4},{2,6},{4,0},{6,2},{8,12},{10,14},{12,8},{14,10},{16,20},{18,... | collective-permute-start | bytes 417800 | tf_op jit(solution)/shard_map/ppermute | solution.py:37
  78.4 7.9 %collective-permute-start.18 = (bf16[272,256]{1,0:T(8,128)(2,1)S(1)}, bf16[272,256]{1,0:T(8,128)(2,1)S(1)}, u32[]{:S(2)}, u32[]{:S(2)}) collective-permute-start(bf16[272,256]{1,0:T(8,128)(2,1)S(1)} %pad_maximum_fusion.5), channel_id=1, source_target_pairs={{0,6},{2,4},{4,2},{6,0},{8,14},{10,12},{12,10},{14,8},{16,22},{18,... | collective-permute-start | bytes 417800 | tf_op jit(solution)/shard_map/ppermute | solution.py:37
  86.6 4.6 %collective-permute-start.19 = (bf16[272,64]{1,0:T(8,128)(2,1)S(1)}, bf16[272,64]{1,0:T(8,128)(2,1)S(1)}, u32[]{:S(2)}, u32[]{:S(2)}) collective-permute-start(bf16[272,64]{1,0:T(8,128)(2,1)S(1)} %pad_maximum_fusion.10), channel_id=1, source_target_pairs={{0,8},{2,10},{4,12},{6,14},{8,0},{10,2},{12,4},{14,6},{16,24},{18,... | collective-permute-start | bytes 104456 | tf_op jit(solution)/shard_map/ppermute | solution.py:37
  87.0 7.7 %collective-permute-start.20 = (bf16[272,64]{1,0:T(8,128)(2,1)S(1)}, bf16[272,64]{1,0:T(8,128)(2,1)S(1)}, u32[]{:S(2)}, u32[]{:S(2)}) collective-permute-start(bf16[272,64]{1,0:T(8,128)(2,1)S(1)} %pad_maximum_fusion.11), channel_id=1, source_target_pairs={{0,16},{2,18},{4,20},{6,22},{8,24},{10,26},{12,28},{14,30},{16,0},... | collective-permute-start | bytes 104456 | tf_op jit(solution)/shard_map/ppermute | solution.py:37
  91.0 6.5 %collective-permute-start.21 = (bf16[272,64]{1,0:T(8,128)(2,1)S(1)}, bf16[272,64]{1,0:T(8,128)(2,1)S(1)}, u32[]{:S(2)}, u32[]{:S(2)}) collective-permute-start(bf16[272,64]{1,0:T(8,128)(2,1)S(1)} %pad_maximum_fusion.12), channel_id=1, source_target_pairs={{0,24},{2,26},{4,28},{6,30},{8,16},{10,18},{12,20},{14,22},{16,8},... | collective-permute-start | bytes 104456 | tf_op jit(solution)/shard_map/ppermute | solution.py:37
  97.6 4.8 %collective-permute-start.22 = (bf16[272,64]{1,0:T(8,128)(2,1)S(1)}, bf16[272,64]{1,0:T(8,128)(2,1)}, u32[]{:S(2)}, u32[]{:S(2)}) collective-permute-start(bf16[272,64]{1,0:T(8,128)(2,1)S(1)} %pad_maximum_fusion.13), channel_id=1, source_target_pairs={{0,8},{2,10},{4,12},{6,14},{8,0},{10,2},{12,4},{14,6},{16,24},{18,... | collective-permute-start | bytes 104456 | tf_op jit(solution)/shard_map/ppermute | solution.py:51
  97.7 6.2 %collective-permute-start.23 = (bf16[272,64]{1,0:T(8,128)(2,1)S(1)}, bf16[272,64]{1,0:T(8,128)(2,1)S(1)}, u32[]{:S(2)}, u32[]{:S(2)}) collective-permute-start(bf16[272,64]{1,0:T(8,128)(2,1)S(1)} %pad_maximum_fusion.13), channel_id=1, source_target_pairs={{0,16},{2,18},{4,20},{6,22},{8,24},{10,26},{12,28},{14,30},{16,0},... | collective-permute-start | bytes 104456 | tf_op jit(solution)/shard_map/ppermute | solution.py:51
  98.7 6.5 %collective-permute-start.24 = (bf16[272,64]{1,0:T(8,128)(2,1)S(1)}, bf16[272,64]{1,0:T(8,128)(2,1)S(1)}, u32[]{:S(2)}, u32[]{:S(2)}) collective-permute-start(bf16[272,64]{1,0:T(8,128)(2,1)S(1)} %pad_maximum_fusion.13), channel_id=1, source_target_pairs={{0,24},{2,26},{4,28},{6,30},{8,16},{10,18},{12,20},{14,22},{16,8},... | collective-permute-start | bytes 104456 | tf_op jit(solution)/shard_map/ppermute | solution.py:51
  105.8 5.1 %collective-permute-start.25 = (bf16[272,256]{1,0:T(8,128)(2,1)S(1)}, bf16[272,256]{1,0:T(8,128)(2,1)S(1)}, u32[]{:S(2)}, u32[]{:S(2)}) collective-permute-start(bf16[272,256]{1,0:T(8,128)(2,1)S(1)} %dynamic_update_slice.59), channel_id=1, source_target_pairs={{0,2},{2,0},{4,6},{6,4},{8,10},{10,8},{12,14},{14,12},{16,18},{18,... | collective-permute-start | bytes 417800 | tf_op jit(solution)/shard_map/ppermute | solution.py:51
  106.2 5.1 %collective-permute-start.26 = (bf16[272,256]{1,0:T(8,128)(2,1)S(1)}, bf16[272,256]{1,0:T(8,128)(2,1)S(1)}, u32[]{:S(2)}, u32[]{:S(2)}) collective-permute-start(bf16[272,256]{1,0:T(8,128)(2,1)S(1)} %dynamic_update_slice.59), channel_id=1, source_target_pairs={{0,4},{2,6},{4,0},{6,2},{8,12},{10,14},{12,8},{14,10},{16,20},{18,... | collective-permute-start | bytes 417800 | tf_op jit(solution)/shard_map/ppermute | solution.py:51
  107.7 6.0 %collective-permute-start.27 = (bf16[272,256]{1,0:T(8,128)(2,1)S(1)}, bf16[272,256]{1,0:T(8,128)(2,1)S(1)}, u32[]{:S(2)}, u32[]{:S(2)}) collective-permute-start(bf16[272,256]{1,0:T(8,128)(2,1)S(1)} %dynamic_update_slice.59), channel_id=1, source_target_pairs={{0,6},{2,4},{4,2},{6,0},{8,14},{10,12},{12,10},{14,8},{16,22},{18,... | collective-permute-start | bytes 417800 | tf_op jit(solution)/shard_map/ppermute | solution.py:51
  113.8 6.2 %copy-start.9 = (f32[128]{0:T(128)S(1)}, f32[128]{0:T(128)}, u32[]{:S(2)}) copy-start(f32[128]{0:T(128)} %copy-done.8) | copy-start | bytes 1540
  118.8 1.2 collective-permute-start.28
  118.9 2.7 %collective-permute-start.29 = (bf16[128,3072]{1,0:T(8,128)(2,1)S(1)}, bf16[128,3072]{1,0:T(8,128)(2,1)S(1)}, u32[]{:S(2)}, u32[]{:S(2)}) collective-permute-start(bf16[128,3072]{1,0:T(8,128)(2,1)S(1)} %convolution_convert_fusion.1), channel_id=1, source_target_pairs={{0,1},{1,0},{2,3},{3,2},{4,5},{5,4},{6,7},{7,6},{8,9},{9,8},{10,11... | collective-permute-start | bytes 2359304 | tf_op jit(solution)/shard_map/ppermute | solution.py:151
  120.1 1.6 %copy-start.2 = (bf16[256,3072]{1,0:T(8,128)(2,1)S(1)}, bf16[256,3072]{1,0:T(8,128)(2,1)}, u32[]{:S(2)}) copy-start(bf16[256,3072]{1,0:T(8,128)(2,1)} %copy-done.1) | copy-start | bytes 4718596
  120.1 2.2 %copy-start.4 = (bf16[128,3072]{1,0:T(8,128)(2,1)S(1)}, bf16[128,3072]{1,0:T(8,128)(2,1)}, u32[]{:S(2)}) copy-start(bf16[128,3072]{1,0:T(8,128)(2,1)} %copy-done.3) | copy-start | bytes 2359300

commit v7 on v1

--- a/solution.py
+++ b/solution.py
@@ -144,10 +144,14 @@
                 weights, features, (((1,), (1,)), ((), ())), preferred_element_type=jnp.float32
             ).astype(jnp.bfloat16)
             if pair:
-                energy = energy[:own] + lax.ppermute(energy[own:], "eig", swap)
-                image = partials[:own].astype(jnp.float32) + lax.ppermute(
-                    partials[own:], "eig", swap
-                ).astype(jnp.float32)
+                high = energy[own:].astype(jnp.bfloat16)
+                low = (energy[own:] - high.astype(jnp.float32)).astype(jnp.bfloat16)
+                extra = jnp.zeros((16, capacity), jnp.bfloat16).at[0, :own].set(high).at[1, :own].set(low)
+                got = lax.ppermute(jnp.concatenate([partials[own:], extra], 0), "eig", swap)
+                energy = energy[:own] + (
+                    got[own, :own].astype(jnp.float32) + got[own + 1, :own].astype(jnp.float32)
+                )
+                image = partials[:own].astype(jnp.float32) + got[:own].astype(jnp.float32)
             else:
                 energy = lax.psum_scatter(energy, "eig", scatter_dimension=0, tiled=True)
                 image = lax.psum_scatter(

time: 124 us -> 137 us (1.10)
  waiting for transfers between devices: 26.9 us -> 35.1 us
  other arithmetic: 8.79 us -> 12.2 us
  local copies, waits for them, and re-layouts: 12.5 us -> 15.2 us
    ppermute x12, waiting for transfers between devices: 14.3 us -> 19 us  [vert_sum(): lax.ppermute(send, 'vert', [(i, i ^ masks[t + 1]) for i in range(n_vert)])]
    ppermute x12, waiting for transfers between devices: 6.46 us -> 8.68 us  [vert_sum(): lax.ppermute(cur, 'vert', [(i, i ^ masks[t]) for i in range(n_vert)])]
    unnamed x26, local copies, waits for them, and re-layouts: 3.57 us -> 5.12 us
    concatenate x0 -> x2, other arithmetic: none -> 1.37 us  [operate(): got = lax.ppermute(jnp.concatenate([partials[own:], extra], 0), 'eig', swap)]
    ppermute x4 -> x2, waiting for transfers between devices: 2.96 us -> 4.07 us  [operate(): got = lax.ppermute(jnp.concatenate([partials[own:], extra], 0), 'eig', swap)]
  transfers between devices with their start and end apart: 30 -> 28, of which waited for: 15 -> 19; matrix products, arithmetic and copies ran while one was open for 19% -> 18% of each run, Pallas kernels for 0% -> 0%
where the time goes in v7:
time: 137 us
  matrix products  37.9 us (28%)
  waiting for transfers between devices  35.1 us (26%)
  starting transfers between devices  34.1 us (25%)
  local copies, waits for them, and re-layouts  15.2 us (11%)
  other arithmetic  12.2 us (9%)
  between operations  2.34 us (2%)
    ppermute x12, waiting for transfers between devices, vert_sum(): lax.ppermute(send, 'vert', [(i, i ^ masks[t + 1]) for i in range(n_vert)])  19 us
    ppermute x12, starting transfers between devices, vert_sum(): lax.ppermute(send, 'vert', [(i, i ^ masks[t + 1]) for i in range(n_vert)])  17.2 us
    ppermute x12, starting transfers between devices, vert_sum(): lax.ppermute(cur, 'vert', [(i, i ^ masks[t]) for i in range(n_vert)])  16 us
    dot_general x3, matrix products, work(): jnp.dot(rows, eig_table, preferred_element_type=jnp.float32)  16 us
    dot_general x2, matrix products, operate(): lax.dot_general(weights, features, (((1,), (1,)), ((), ())), preferred_el...  9.42 us
    ppermute x12, waiting for transfers between devices, vert_sum(): lax.ppermute(cur, 'vert', [(i, i ^ masks[t]) for i in range(n_vert)])  8.68 us
    unnamed x26, local copies, waits for them, and re-layouts  5.12 us
    dot_general x1, matrix products, coeff_from_table(): summed = jnp.dot(rows, picker, preferred_element_type=jnp.float32)  5.09 us
  transfers between devices with their start and end apart: 28, of which 19 were waited for; matrix products, arithmetic and copies ran while one was open for 18% of the time, Pallas kernels for 0%

profile of v7, /device:TPU:0, one launch (start us, length us, event | category | flops | bytes accessed | tf_op | source)
XLA Modules:
  0.0 136.8 jit_solution(13579821396046777045)
XLA Ops:
  1.5 1.5 %select_convert_fusion = bf16[128,3072]{1,0:T(8,128)(2,1)S(1)} fusion(f32[128,3072]{1,0:T(8,128)} %param.27, pred[3072]{0:T(1024)(128)(4,1)S(1)} %iota_compare_fusion.14), kind=kLoop, calls=%fused_computation.51 | loop fusion | flops 393216 | bytes 2362368 | tf_op jit(solution)/shard_map/convert_element_type | solution.py:114
  3.0 0.6 collective-permute-start
  3.6 0.4 fusion.15
  4.3 1.2 collective-permute-done
  5.5 5.1 %subtract_convert_fusion = (bf16[256,2048]{1,0:T(8,128)(2,1)S(1)}, bf16[256,2048]{1,0:T(8,128)(2,1)S(1)}) fusion(s32[3072]{0:T(1024)S(1)} %copy-done.9, bf16[128,3072]{1,0:T(8,128)(2,1)S(1)} %collective-permute-done, bf16[128,3072]{1,0:T(8,128)(2,1)S(1)} %select_convert_fusion), kind=kOutput, calls=%fused_computation.30 | convolution fusion | flops 3232759808 | bytes 3682304 | tf_op jit(solution)/shard_map/dot_general | solution.py:86
  10.6 2.4 %fusion.8 = f32[512,1024]{1,0:T(8,128)S(1)} fusion(bf16[2048,1024]{1,0:T(8,128)(2,1)S(1)} %copy-done.11, bf16[256,2048]{1,0:T(8,128)(2,1)S(1)} %get-tuple-element.165, bf16[256,2048]{1,0:T(8,128)(2,1)S(1)} %get-tuple-element.166), kind=kOutput, calls=%fused_computation.26 | convolution fusion | flops 2151677952 | bytes 8388608 | tf_op jit(solution)/shard_map/dot_general | solution.py:89
  13.4 2.9 %collective-permute-start.1 = (bf16[272,256]{1,0:T(8,128)(2,1)S(1)}, bf16[272,256]{1,0:T(8,128)(2,1)S(1)}, u32[]{:S(2)}, u32[]{:S(2)}) collective-permute-start(bf16[272,256]{1,0:T(8,128)(2,1)S(1)} %pad_maximum_fusion.2), channel_id=1, source_target_pairs={{0,2},{2,0},{4,6},{6,4},{8,10},{10,8},{12,14},{14,12},{16,18},{18,... | collective-permute-start | bytes 417800 | tf_op jit(solution)/shard_map/ppermute | solution.py:37
  16.3 1.6 %collective-permute-start.3 = (bf16[272,256]{1,0:T(8,128)(2,1)S(1)}, bf16[272,256]{1,0:T(8,128)(2,1)S(1)}, u32[]{:S(2)}, u32[]{:S(2)}) collective-permute-start(bf16[272,256]{1,0:T(8,128)(2,1)S(1)} %pad_maximum_fusion.4), channel_id=1, source_target_pairs={{0,6},{2,4},{4,2},{6,0},{8,14},{10,12},{12,10},{14,8},{16,22},{18,... | collective-permute-start | bytes 417800 | tf_op jit(solution)/shard_map/ppermute | solution.py:37
  18.0 5.0 %fusion.14 = bf16[1024,1024]{1,0:T(8,128)(2,1)S(1)} fusion(bf16[2048,1024]{1,0:T(8,128)(2,1)S(1)} %copy-done.11, s32[1024]{0:T(1024)S(1)} %get-tuple-element.113), kind=kOutput, calls=%fused_computation.33 | convolution fusion | flops 4298113024 | bytes 6295552 | tf_op jit(solution)/shard_map/dot_general | solution.py:79
  23.0 1.6 %collective-permute-done.3 = bf16[272,256]{1,0:T(8,128)(2,1)S(1)} collective-permute-done((bf16[272,256]{1,0:T(8,128)(2,1)S(1)}, bf16[272,256]{1,0:T(8,128)(2,1)S(1)}, u32[]{:S(2)}, u32[]{:S(2)}) %collective-permute-start.3) | collective-permute-done | bytes 139296 | tf_op jit(solution)/shard_map/ppermute | solution.py:37
  24.6 1.5 %collective-permute-done.2 = bf16[272,256]{1,0:T(8,128)(2,1)S(1)} collective-permute-done((bf16[272,256]{1,0:T(8,128)(2,1)S(1)}, bf16[272,256]{1,0:T(8,128)(2,1)S(1)}, u32[]{:S(2)}, u32[]{:S(2)}) %collective-permute-start.2) | collective-permute-done | bytes 139296 | tf_op jit(solution)/shard_map/ppermute | solution.py:37
  26.5 1.6 %collective-permute-start.4 = (bf16[272,64]{1,0:T(8,128)(2,1)S(1)}, bf16[272,64]{1,0:T(8,128)(2,1)S(1)}, u32[]{:S(2)}, u32[]{:S(2)}) collective-permute-start(bf16[272,64]{1,0:T(8,128)(2,1)S(1)} %pad_maximum_fusion.8), channel_id=1, source_target_pairs={{0,8},{2,10},{4,12},{6,14},{8,0},{10,2},{12,4},{14,6},{16,24},{18,... | collective-permute-start | bytes 104456 | tf_op jit(solution)/shard_map/ppermute | solution.py:37
  28.2 5.0 %fusion.13 = bf16[1024,1024]{1,0:T(8,128)(2,1)S(1)} fusion(bf16[2048,1024]{1,0:T(8,128)(2,1)S(1)} %copy-done.11, s32[1024]{0:T(1024)S(1)} %get-tuple-element.117), kind=kOutput, calls=%fused_computation.32 | convolution fusion | flops 4298113024 | bytes 6295552 | tf_op jit(solution)/shard_map/dot_general | solution.py:79
  33.2 2.5 %collective-permute-start.6 = (bf16[272,64]{1,0:T(8,128)(2,1)S(1)}, bf16[272,64]{1,0:T(8,128)(2,1)S(1)}, u32[]{:S(2)}, u32[]{:S(2)}) collective-permute-start(bf16[272,64]{1,0:T(8,128)(2,1)S(1)} %pad_maximum_fusion.10), channel_id=1, source_target_pairs={{0,24},{2,26},{4,28},{6,30},{8,16},{10,18},{12,20},{14,22},{16,8},... | collective-permute-start | bytes 104456 | tf_op jit(solution)/shard_map/ppermute | solution.py:37
  36.1 3.5 %collective-permute-done.6 = bf16[272,64]{1,0:T(8,128)(2,1)S(1)} collective-permute-done((bf16[272,64]{1,0:T(8,128)(2,1)S(1)}, bf16[272,64]{1,0:T(8,128)(2,1)S(1)}, u32[]{:S(2)}, u32[]{:S(2)}) %collective-permute-start.6) | collective-permute-done | bytes 34848 | tf_op jit(solution)/shard_map/ppermute | solution.py:37
  39.6 2.3 %collective-permute-done.5 = bf16[272,64]{1,0:T(8,128)(2,1)S(1)} collective-permute-done((bf16[272,64]{1,0:T(8,128)(2,1)S(1)}, bf16[272,64]{1,0:T(8,128)(2,1)S(1)}, u32[]{:S(2)}, u32[]{:S(2)}) %collective-permute-start.5) | collective-permute-done | bytes 34848 | tf_op jit(solution)/shard_map/ppermute | solution.py:37
  42.2 2.9 %collective-permute-start.8 = (bf16[272,64]{1,0:T(8,128)(2,1)S(1)}, bf16[272,64]{1,0:T(8,128)(2,1)S(1)}, u32[]{:S(2)}, u32[]{:S(2)}) collective-permute-start(bf16[272,64]{1,0:T(8,128)(2,1)S(1)} %pad_maximum_fusion.11), channel_id=1, source_target_pairs={{0,16},{2,18},{4,20},{6,22},{8,24},{10,26},{12,28},{14,30},{16,0},... | collective-permute-start | bytes 104456 | tf_op jit(solution)/shard_map/ppermute | solution.py:51
  45.2 1.4 %collective-permute-start.9 = (bf16[272,64]{1,0:T(8,128)(2,1)S(1)}, bf16[272,64]{1,0:T(8,128)(2,1)S(1)}, u32[]{:S(2)}, u32[]{:S(2)}) collective-permute-start(bf16[272,64]{1,0:T(8,128)(2,1)S(1)} %pad_maximum_fusion.11), channel_id=1, source_target_pairs={{0,24},{2,26},{4,28},{6,30},{8,16},{10,18},{12,20},{14,22},{16,8},... | collective-permute-start | bytes 104456 | tf_op jit(solution)/shard_map/ppermute | solution.py:51
  46.6 6.0 %fusion.12 = bf16[1024,1024]{1,0:T(8,128)(2,1)} fusion(bf16[2048,1024]{1,0:T(8,128)(2,1)S(1)} %copy-done.11, s32[1024]{0:T(1024)S(1)} %get-tuple-element.121), kind=kOutput, calls=%fused_computation.31 | convolution fusion | flops 4298113024 | bytes 6295552 | tf_op jit(solution)/shard_map/dot_general | solution.py:79
  52.8 2.7 %copy-done.7 = bf16[3072,1024]{1,0:T(8,128)(2,1)} copy-done((bf16[3072,1024]{1,0:T(8,128)(2,1)}, bf16[3072,1024]{1,0:T(8,128)(2,1)S(1)}, u32[]{:S(2)}) %copy-start.7) | copy-done | bytes 6291480
  55.8 0.6 dynamic_update_slice.49
  56.8 0.6 dynamic_update_slice.51
  57.4 1.6 %collective-permute-start.10 = (bf16[272,256]{1,0:T(8,128)(2,1)S(1)}, bf16[272,256]{1,0:T(8,128)(2,1)S(1)}, u32[]{:S(2)}, u32[]{:S(2)}) collective-permute-start(bf16[272,256]{1,0:T(8,128)(2,1)S(1)} %dynamic_update_slice.51), channel_id=1, source_target_pairs={{0,2},{2,0},{4,6},{6,4},{8,10},{10,8},{12,14},{14,12},{16,18},{18,... | collective-permute-start | bytes 417800 | tf_op jit(solution)/shard_map/ppermute | solution.py:51
  58.9 0.5 collective-permute-start.11
  59.4 1.5 %collective-permute-start.12 = (bf16[272,256]{1,0:T(8,128)(2,1)S(1)}, bf16[272,256]{1,0:T(8,128)(2,1)S(1)}, u32[]{:S(2)}, u32[]{:S(2)}) collective-permute-start(bf16[272,256]{1,0:T(8,128)(2,1)S(1)} %dynamic_update_slice.51), channel_id=1, source_target_pairs={{0,6},{2,4},{4,2},{6,0},{8,14},{10,12},{12,10},{14,8},{16,22},{18,... | collective-permute-start | bytes 417800 | tf_op jit(solution)/shard_map/ppermute | solution.py:51
  60.9 3.1 %constant_dynamic-update-slice_fusion = bf16[3072,1024]{1,0:T(8,128)(2,1)} fusion(bf16[3072,1024]{1,0:T(8,128)(2,1)} %copy-done.7, bf16[1024,1024]{1,0:T(8,128)(2,1)} %fusion.12), kind=kLoop, calls=%fused_computation.133 | loop fusion | bytes 4194304 | tf_op jit(solution)/shard_map/concatenate | solution.py:135
  64.2 1.3 collective-permute-done.11
  65.8 4.6 %convolution_convert_fusion.1 = bf16[256,3072]{1,0:T(8,128)(2,1)S(1)} fusion(bf16[3072,1024]{1,0:T(8,128)(2,1)} %constant_dynamic-update-slice_fusion, bf16[272,1024]{1,0:T(8,128)(2,1)S(1)} %constant_dynamic-update-slice_fusion.7), kind=kOutput, calls=%fused_computation.13 | convolution fusion | flops 1611399168 | bytes 8388608 | tf_op jit(solution)/shard_map/dot_general | solution.py:143
  70.5 1.1 copy-done.1
  72.0 2.4 %collective-permute-done.13 = bf16[144,3072]{1,0:T(8,128)(2,1)S(1)} collective-permute-done((bf16[144,3072]{1,0:T(8,128)(2,1)S(1)}, bf16[144,3072]{1,0:T(8,128)(2,1)S(1)}, u32[]{:S(2)}, u32[]{:S(2)}) %collective-permute-start.13) | collective-permute-done | bytes 884768 | tf_op jit(solution)/shard_map/ppermute | solution.py:150
  74.4 0.9 fusion.16
  75.4 1.0 convert_element_type.403
  76.9 2.1 %collective-permute-done.14 = bf16[128,3072]{1,0:T(8,128)(2,1)} collective-permute-done((bf16[128,3072]{1,0:T(8,128)(2,1)}, bf16[128,3072]{1,0:T(8,128)(2,1)}, u32[]{:S(2)}, u32[]{:S(2)}) %collective-permute-start.14) | collective-permute-done | bytes 786464 | tf_op jit(solution)/shard_map/ppermute | solution.py:116
  79.0 5.1 %fusion.27 = f32[256,1024]{1,0:T(8,128)S(1)} fusion(bf16[3072,1024]{1,0:T(8,128)(2,1)} %constant_dynamic-update-slice_fusion, bf16[128,3072]{1,0:T(8,128)(2,1)} %collective-permute-done.14, bf16[128,3072]{1,0:T(8,128)(2,1)} %convert_element_type.403, f32[1024]{0:T(1024)S(1)} %power_multiply_fusion), kind=kOutput, calls=%fused_computation.50 | convolution fusion | flops 1614020608 | bytes 8916992 | tf_op jit(solution)/shard_map/dot_general | solution.py:122
  84.2 1.4 %collective-permute-start.17 = (bf16[272,256]{1,0:T(8,128)(2,1)S(1)}, bf16[272,256]{1,0:T(8,128)(2,1)S(1)}, u32[]{:S(2)}, u32[]{:S(2)}) collective-permute-start(bf16[272,256]{1,0:T(8,128)(2,1)S(1)} %pad_maximum_fusion.7), channel_id=1, source_target_pairs={{0,6},{2,4},{4,2},{6,0},{8,14},{10,12},{12,10},{14,8},{16,22},{18,... | collective-permute-start | bytes 417800 | tf_op jit(solution)/shard_map/ppermute | solution.py:37
  85.7 0.7 collective-permute-start.16
  86.3 1.7 %collective-permute-start.15 = (bf16[272,256]{1,0:T(8,128)(2,1)S(1)}, bf16[272,256]{1,0:T(8,128)(2,1)S(1)}, u32[]{:S(2)}, u32[]{:S(2)}) collective-permute-start(bf16[272,256]{1,0:T(8,128)(2,1)S(1)} %pad_maximum_fusion.5), channel_id=1, source_target_pairs={{0,2},{2,0},{4,6},{6,4},{8,10},{10,8},{12,14},{14,12},{16,18},{18,... | collective-permute-start | bytes 417800 | tf_op jit(solution)/shard_map/ppermute | solution.py:37
  88.0 3.8 %collective-permute-done.17 = bf16[272,256]{1,0:T(8,128)(2,1)S(1)} collective-permute-done((bf16[272,256]{1,0:T(8,128)(2,1)S(1)}, bf16[272,256]{1,0:T(8,128)(2,1)S(1)}, u32[]{:S(2)}, u32[]{:S(2)}) %collective-permute-start.17) | collective-permute-done | bytes 139296 | tf_op jit(solution)/shard_map/ppermute | solution.py:37
  91.8 2.1 %collective-permute-done.16 = bf16[272,256]{1,0:T(8,128)(2,1)S(1)} collective-permute-done((bf16[272,256]{1,0:T(8,128)(2,1)S(1)}, bf16[272,256]{1,0:T(8,128)(2,1)S(1)}, u32[]{:S(2)}, u32[]{:S(2)}) %collective-permute-start.16) | collective-permute-done | bytes 139296 | tf_op jit(solution)/shard_map/ppermute | solution.py:37
  94.4 2.7 %collective-permute-start.20 = (bf16[272,64]{1,0:T(8,128)(2,1)S(1)}, bf16[272,64]{1,0:T(8,128)(2,1)S(1)}, u32[]{:S(2)}, u32[]{:S(2)}) collective-permute-start(bf16[272,64]{1,0:T(8,128)(2,1)S(1)} %pad_maximum_fusion.14), channel_id=1, source_target_pairs={{0,24},{2,26},{4,28},{6,30},{8,16},{10,18},{12,20},{14,22},{16,8},... | collective-permute-start | bytes 104456 | tf_op jit(solution)/shard_map/ppermute | solution.py:37
  97.2 1.8 %collective-permute-start.18 = (bf16[272,64]{1,0:T(8,128)(2,1)S(1)}, bf16[272,64]{1,0:T(8,128)(2,1)S(1)}, u32[]{:S(2)}, u32[]{:S(2)}) collective-permute-start(bf16[272,64]{1,0:T(8,128)(2,1)S(1)} %pad_maximum_fusion.12), channel_id=1, source_target_pairs={{0,8},{2,10},{4,12},{6,14},{8,0},{10,2},{12,4},{14,6},{16,24},{18,... | collective-permute-start | bytes 104456 | tf_op jit(solution)/shard_map/ppermute | solution.py:37
  99.0 2.2 %collective-permute-done.20 = bf16[272,64]{1,0:T(8,128)(2,1)S(1)} collective-permute-done((bf16[272,64]{1,0:T(8,128)(2,1)S(1)}, bf16[272,64]{1,0:T(8,128)(2,1)S(1)}, u32[]{:S(2)}, u32[]{:S(2)}) %collective-permute-start.20) | collective-permute-done | bytes 34848 | tf_op jit(solution)/shard_map/ppermute | solution.py:37
  101.2 2.1 %collective-permute-done.19 = bf16[272,64]{1,0:T(8,128)(2,1)S(1)} collective-permute-done((bf16[272,64]{1,0:T(8,128)(2,1)S(1)}, bf16[272,64]{1,0:T(8,128)(2,1)S(1)}, u32[]{:S(2)}, u32[]{:S(2)}) %collective-permute-start.19) | collective-permute-done | bytes 34848 | tf_op jit(solution)/shard_map/ppermute | solution.py:37
  103.5 0.9 collective-permute-start.21
  104.4 2.4 %collective-permute-start.22 = (bf16[272,64]{1,0:T(8,128)(2,1)S(1)}, bf16[272,64]{1,0:T(8,128)(2,1)S(1)}, u32[]{:S(2)}, u32[]{:S(2)}) collective-permute-start(bf16[272,64]{1,0:T(8,128)(2,1)S(1)} %pad_maximum_fusion.15), channel_id=1, source_target_pairs={{0,16},{2,18},{4,20},{6,22},{8,24},{10,26},{12,28},{14,30},{16,0},... | collective-permute-start | bytes 104456 | tf_op jit(solution)/shard_map/ppermute | solution.py:51
  106.8 1.2 collective-permute-start.23
  108.4 0.4 collective-permute-done.21
  108.8 1.4 %dynamic_update_slice.57 = bf16[272,256]{1,0:T(8,128)(2,1)S(1)} dynamic-update-slice(bf16[272,256]{1,0:T(8,128)(2,1)S(1)} %dynamic_update_slice.56, bf16[272,64]{1,0:T(8,128)(2,1)} %collective-permute-done.21, s32[]{:T(128)} %constant.191.clone.1, s32[]{:T(128)S(6)} %select_n.32) | dynamic-update-slice | bytes 69636 | tf_op jit(solution)/shard_map/dynamic_update_slice | solution.py:55
  110.2 2.0 %collective-permute-done.22 = bf16[272,64]{1,0:T(8,128)(2,1)S(1)} collective-permute-done((bf16[272,64]{1,0:T(8,128)(2,1)S(1)}, bf16[272,64]{1,0:T(8,128)(2,1)S(1)}, u32[]{:S(2)}, u32[]{:S(2)}) %collective-permute-start.22) | collective-permute-done | bytes 34848 | tf_op jit(solution)/shard_map/ppermute | solution.py:51
  112.5 0.5 collective-permute-done.23
  113.0 0.5 dynamic_update_slice.59
  113.5 0.7 collective-permute-start.24
  114.2 1.4 %collective-permute-start.25 = (bf16[272,256]{1,0:T(8,128)(2,1)S(1)}, bf16[272,256]{1,0:T(8,128)(2,1)S(1)}, u32[]{:S(2)}, u32[]{:S(2)}) collective-permute-start(bf16[272,256]{1,0:T(8,128)(2,1)S(1)} %dynamic_update_slice.59), channel_id=1, source_target_pairs={{0,4},{2,6},{4,0},{6,2},{8,12},{10,14},{12,8},{14,10},{16,20},{18,... | collective-permute-start | bytes 417800 | tf_op jit(solution)/shard_map/ppermute | solution.py:51
  115.6 1.5 %collective-permute-start.26 = (bf16[272,256]{1,0:T(8,128)(2,1)S(1)}, bf16[272,256]{1,0:T(8,128)(2,1)S(1)}, u32[]{:S(2)}, u32[]{:S(2)}) collective-permute-start(bf16[272,256]{1,0:T(8,128)(2,1)S(1)} %dynamic_update_slice.59), channel_id=1, source_target_pairs={{0,6},{2,4},{4,2},{6,0},{8,14},{10,12},{12,10},{14,8},{16,22},{18,... | collective-permute-start | bytes 417800 | tf_op jit(solution)/shard_map/ppermute | solution.py:51
  117.2 1.7 %collective-permute-done.24 = bf16[272,256]{1,0:T(8,128)(2,1)S(1)} collective-permute-done((bf16[272,256]{1,0:T(8,128)(2,1)S(1)}, bf16[272,256]{1,0:T(8,128)(2,1)S(1)}, u32[]{:S(2)}, u32[]{:S(2)}) %collective-permute-start.24) | collective-permute-done | bytes 139296 | tf_op jit(solution)/shard_map/ppermute | solution.py:51
  118.9 1.0 collective-permute-done.25
  119.9 1.7 %collective-permute-done.26 = bf16[272,256]{1,0:T(8,128)(2,1)S(1)} collective-permute-done((bf16[272,256]{1,0:T(8,128)(2,1)S(1)}, bf16[272,256]{1,0:T(8,128)(2,1)S(1)}, u32[]{:S(2)}, u32[]{:S(2)}) %collective-permute-start.26) | collective-permute-done | bytes 139296 | tf_op jit(solution)/shard_map/ppermute | solution.py:51
  121.6 4.8 %convolution_convert_fusion = bf16[256,3072]{1,0:T(8,128)(2,1)S(1)} fusion(bf16[3072,1024]{1,0:T(8,128)(2,1)} %constant_dynamic-update-slice_fusion, bf16[272,1024]{1,0:T(8,128)(2,1)S(1)} %constant_dynamic-update-slice_fusion.3), kind=kOutput, calls=%fused_computation.12 | convolution fusion | flops 1611399168 | bytes 8388608 | tf_op jit(solution)/shard_map/dot_general | solution.py:143
  126.7 0.9 copy-done.6
  127.6 0.9 slice.573
  128.7 1.3 pad_maximum_fusion.1
  130.1 0.7 convert_add_fusion
  130.9 1.7 %collective-permute-done.27 = bf16[144,3072]{1,0:T(8,128)(2,1)S(1)} collective-permute-done((bf16[144,3072]{1,0:T(8,128)(2,1)S(1)}, bf16[144,3072]{1,0:T(8,128)(2,1)S(1)}, u32[]{:S(2)}, u32[]{:S(2)}) %collective-permute-start.27) | collective-permute-done | bytes 884768 | tf_op jit(solution)/shard_map/ppermute | solution.py:150
  132.6 4.3 %fusion.19 = (f32[128,3072]{1,0:T(8,128)}, f32[128,3072]{1,0:T(8,128)}) fusion(f32[128,3072]{1,0:T(8,128)S(1)} %get-tuple-element.148, f32[128,3072]{1,0:T(8,128)S(1)} %copy-done, bf16[144,3072]{1,0:T(8,128)(2,1)S(1)} %collective-permute-done.27, bf16[256,3072]{1,0:T(8,128)(2,1)} %copy-done.6, f32[128]{0:T(128)S(1)} %get-tuple-element.133, ...), kind=kLoop, calls=%fused_computation.38 | loop fusion | flops 8650752 | bytes 9454080 | tf_op jit(solution)/shard_map/sub | solution.py:172
  (140 shorter events, 6.1 us)
Async XLA Ops:
  0.6 2.9 %copy-start = (f32[128,3072]{1,0:T(8,128)S(1)}, f32[128,3072]{1,0:T(8,128)}, u32[]{:S(2)}) copy-start(f32[128,3072]{1,0:T(8,128)} %param.27) | copy-start | bytes 4718596
  0.6 2.9 %copy-start.8 = (f32[3072]{0:T(1024)S(1)}, f32[3072]{0:T(1024)}, u32[]{:S(2)}) copy-start(f32[3072]{0:T(1024)} %param.25) | copy-start | bytes 36868
  1.4 2.8 %copy-start.10 = (f32[1024]{0:T(1024)S(1)}, f32[1024]{0:T(1024)}, u32[]{:S(2)}) copy-start(f32[1024]{0:T(1024)} %param.26) | copy-start | bytes 12292
  1.4 2.8 %copy-start.9 = (s32[3072]{0:T(1024)S(1)}, s32[3072]{0:T(1024)}, u32[]{:S(2)}) copy-start(s32[3072]{0:T(1024)} %param.23) | copy-start | bytes 36868
  3.0 2.5 %collective-permute-start = (bf16[128,3072]{1,0:T(8,128)(2,1)S(1)}, bf16[128,3072]{1,0:T(8,128)(2,1)S(1)}, u32[]{:S(2)}, u32[]{:S(2)}) collective-permute-start(bf16[128,3072]{1,0:T(8,128)(2,1)S(1)} %select_convert_fusion), channel_id=1, source_target_pairs={{0,1},{1,0},{2,3},{3,2},{4,5},{5,4},{6,7},{7,6},{8,9},{9,8},{10,11... | collective-permute-start | bytes 2359304 | tf_op jit(solution)/shard_map/ppermute | solution.py:116
  4.3 6.3 %copy-start.11 = (bf16[2048,1024]{1,0:T(8,128)(2,1)S(1)}, bf16[2048,1024]{1,0:T(8,128)(2,1)}, u32[]{:S(2)}) copy-start(bf16[2048,1024]{1,0:T(8,128)(2,1)} %param.22) | copy-start | bytes 12582916
  13.4 12.7 %collective-permute-start.1 = (bf16[272,256]{1,0:T(8,128)(2,1)S(1)}, bf16[272,256]{1,0:T(8,128)(2,1)S(1)}, u32[]{:S(2)}, u32[]{:S(2)}) collective-permute-start(bf16[272,256]{1,0:T(8,128)(2,1)S(1)} %pad_maximum_fusion.2), channel_id=1, source_target_pairs={{0,2},{2,0},{4,6},{6,4},{8,10},{10,8},{12,14},{14,12},{16,18},{18,... | collective-permute-start | bytes 417800 | tf_op jit(solution)/shard_map/ppermute | solution.py:37
  16.3 8.3 %collective-permute-start.3 = (bf16[272,256]{1,0:T(8,128)(2,1)S(1)}, bf16[272,256]{1,0:T(8,128)(2,1)S(1)}, u32[]{:S(2)}, u32[]{:S(2)}) collective-permute-start(bf16[272,256]{1,0:T(8,128)(2,1)S(1)} %pad_maximum_fusion.4), channel_id=1, source_target_pairs={{0,6},{2,4},{4,2},{6,0},{8,14},{10,12},{12,10},{14,8},{16,22},{18,... | collective-permute-start | bytes 417800 | tf_op jit(solution)/shard_map/ppermute | solution.py:37
  17.9 8.2 %collective-permute-start.2 = (bf16[272,256]{1,0:T(8,128)(2,1)S(1)}, bf16[272,256]{1,0:T(8,128)(2,1)S(1)}, u32[]{:S(2)}, u32[]{:S(2)}) collective-permute-start(bf16[272,256]{1,0:T(8,128)(2,1)S(1)} %pad_maximum_fusion.3), channel_id=1, source_target_pairs={{0,4},{2,6},{4,0},{6,2},{8,12},{10,14},{12,8},{14,10},{16,20},{18,... | collective-permute-start | bytes 417800 | tf_op jit(solution)/shard_map/ppermute | solution.py:37
  26.5 15.3 %collective-permute-start.4 = (bf16[272,64]{1,0:T(8,128)(2,1)S(1)}, bf16[272,64]{1,0:T(8,128)(2,1)S(1)}, u32[]{:S(2)}, u32[]{:S(2)}) collective-permute-start(bf16[272,64]{1,0:T(8,128)(2,1)S(1)} %pad_maximum_fusion.8), channel_id=1, source_target_pairs={{0,8},{2,10},{4,12},{6,14},{8,0},{10,2},{12,4},{14,6},{16,24},{18,... | collective-permute-start | bytes 104456 | tf_op jit(solution)/shard_map/ppermute | solution.py:37
  33.2 6.4 %collective-permute-start.6 = (bf16[272,64]{1,0:T(8,128)(2,1)S(1)}, bf16[272,64]{1,0:T(8,128)(2,1)S(1)}, u32[]{:S(2)}, u32[]{:S(2)}) collective-permute-start(bf16[272,64]{1,0:T(8,128)(2,1)S(1)} %pad_maximum_fusion.10), channel_id=1, source_target_pairs={{0,24},{2,26},{4,28},{6,30},{8,16},{10,18},{12,20},{14,22},{16,8},... | collective-permute-start | bytes 104456 | tf_op jit(solution)/shard_map/ppermute | solution.py:37
  35.7 6.1 %collective-permute-start.5 = (bf16[272,64]{1,0:T(8,128)(2,1)S(1)}, bf16[272,64]{1,0:T(8,128)(2,1)S(1)}, u32[]{:S(2)}, u32[]{:S(2)}) collective-permute-start(bf16[272,64]{1,0:T(8,128)(2,1)S(1)} %pad_maximum_fusion.9), channel_id=1, source_target_pairs={{0,16},{2,18},{4,20},{6,22},{8,24},{10,26},{12,28},{14,30},{16,0},... | collective-permute-start | bytes 104456 | tf_op jit(solution)/shard_map/ppermute | solution.py:37
  42.1 13.7 %collective-permute-start.7 = (bf16[272,64]{1,0:T(8,128)(2,1)S(1)}, bf16[272,64]{1,0:T(8,128)(2,1)S(1)}, u32[]{:S(2)}, u32[]{:S(2)}) collective-permute-start(bf16[272,64]{1,0:T(8,128)(2,1)S(1)} %pad_maximum_fusion.11), channel_id=1, source_target_pairs={{0,8},{2,10},{4,12},{6,14},{8,0},{10,2},{12,4},{14,6},{16,24},{18,... | collective-permute-start | bytes 104456 | tf_op jit(solution)/shard_map/ppermute | solution.py:51
  42.2 13.6 %collective-permute-start.8 = (bf16[272,64]{1,0:T(8,128)(2,1)S(1)}, bf16[272,64]{1,0:T(8,128)(2,1)S(1)}, u32[]{:S(2)}, u32[]{:S(2)}) collective-permute-start(bf16[272,64]{1,0:T(8,128)(2,1)S(1)} %pad_maximum_fusion.11), channel_id=1, source_target_pairs={{0,16},{2,18},{4,20},{6,22},{8,24},{10,26},{12,28},{14,30},{16,0},... | collective-permute-start | bytes 104456 | tf_op jit(solution)/shard_map/ppermute | solution.py:51
  45.2 10.7 %collective-permute-start.9 = (bf16[272,64]{1,0:T(8,128)(2,1)S(1)}, bf16[272,64]{1,0:T(8,128)(2,1)S(1)}, u32[]{:S(2)}, u32[]{:S(2)}) collective-permute-start(bf16[272,64]{1,0:T(8,128)(2,1)S(1)} %pad_maximum_fusion.11), channel_id=1, source_target_pairs={{0,24},{2,26},{4,28},{6,30},{8,16},{10,18},{12,20},{14,22},{16,8},... | collective-permute-start | bytes 104456 | tf_op jit(solution)/shard_map/ppermute | solution.py:51
  52.8 2.7 %copy-start.7 = (bf16[3072,1024]{1,0:T(8,128)(2,1)}, bf16[3072,1024]{1,0:T(8,128)(2,1)S(1)}, u32[]{:S(2)}) copy-start(bf16[3072,1024]{1,0:T(8,128)(2,1)S(1)} %constant_dynamic-update-slice_fusion.1) | copy-start | bytes 18874372
  57.4 6.8 %collective-permute-start.10 = (bf16[272,256]{1,0:T(8,128)(2,1)S(1)}, bf16[272,256]{1,0:T(8,128)(2,1)S(1)}, u32[]{:S(2)}, u32[]{:S(2)}) collective-permute-start(bf16[272,256]{1,0:T(8,128)(2,1)S(1)} %dynamic_update_slice.51), channel_id=1, source_target_pairs={{0,2},{2,0},{4,6},{6,4},{8,10},{10,8},{12,14},{14,12},{16,18},{18,... | collective-permute-start | bytes 417800 | tf_op jit(solution)/shard_map/ppermute | solution.py:51
  58.9 6.6 %collective-permute-start.11 = (bf16[272,256]{1,0:T(8,128)(2,1)S(1)}, bf16[272,256]{1,0:T(8,128)(2,1)S(1)}, u32[]{:S(2)}, u32[]{:S(2)}) collective-permute-start(bf16[272,256]{1,0:T(8,128)(2,1)S(1)} %dynamic_update_slice.51), channel_id=1, source_target_pairs={{0,4},{2,6},{4,0},{6,2},{8,12},{10,14},{12,8},{14,10},{16,20},{18,... | collective-permute-start | bytes 417800 | tf_op jit(solution)/shard_map/ppermute | solution.py:51
  59.4 6.1 %collective-permute-start.12 = (bf16[272,256]{1,0:T(8,128)(2,1)S(1)}, bf16[272,256]{1,0:T(8,128)(2,1)S(1)}, u32[]{:S(2)}, u32[]{:S(2)}) collective-permute-start(bf16[272,256]{1,0:T(8,128)(2,1)S(1)} %dynamic_update_slice.51), channel_id=1, source_target_pairs={{0,6},{2,4},{4,2},{6,0},{8,14},{10,12},{12,10},{14,8},{16,22},{18,... | collective-permute-start | bytes 417800 | tf_op jit(solution)/shard_map/ppermute | solution.py:51
  70.4 1.1 copy-start.1
  71.8 2.6 %copy-start.2 = (bf16[256,3072]{1,0:T(8,128)(2,1)S(1)}, bf16[256,3072]{1,0:T(8,128)(2,1)}, u32[]{:S(2)}) copy-start(bf16[256,3072]{1,0:T(8,128)(2,1)} %copy-done.1) | copy-start | bytes 4718596
  71.9 2.5 %collective-permute-start.13 = (bf16[144,3072]{1,0:T(8,128)(2,1)S(1)}, bf16[144,3072]{1,0:T(8,128)(2,1)S(1)}, u32[]{:S(2)}, u32[]{:S(2)}) collective-permute-start(bf16[144,3072]{1,0:T(8,128)(2,1)S(1)} %pad_maximum_fusion), channel_id=1, source_target_pairs={{0,1},{1,0},{2,3},{3,2},{4,5},{5,4},{6,7},{7,6},{8,9},{9,8},{10,11... | collective-permute-start | bytes 2654216 | tf_op jit(solution)/shard_map/ppermute | solution.py:150
  74.4 1.0 copy-start.4
  76.4 2.6 %collective-permute-start.14 = (bf16[128,3072]{1,0:T(8,128)(2,1)}, bf16[128,3072]{1,0:T(8,128)(2,1)}, u32[]{:S(2)}, u32[]{:S(2)}) collective-permute-start(bf16[128,3072]{1,0:T(8,128)(2,1)} %convert_element_type.403), channel_id=1, source_target_pairs={{0,1},{1,0},{2,3},{3,2},{4,5},{5,4},{6,7},{7,6},{8,9},{9,8},{10,11... | collective-permute-start | bytes 2359304 | tf_op jit(solution)/shard_map/ppermute | solution.py:116
  84.2 7.6 %collective-permute-start.17 = (bf16[272,256]{1,0:T(8,128)(2,1)S(1)}, bf16[272,256]{1,0:T(8,128)(2,1)S(1)}, u32[]{:S(2)}, u32[]{:S(2)}) collective-permute-start(bf16[272,256]{1,0:T(8,128)(2,1)S(1)} %pad_maximum_fusion.7), channel_id=1, source_target_pairs={{0,6},{2,4},{4,2},{6,0},{8,14},{10,12},{12,10},{14,8},{16,22},{18,... | collective-permute-start | bytes 417800 | tf_op jit(solution)/shard_map/ppermute | solution.py:37
  85.7 8.2 %collective-permute-start.16 = (bf16[272,256]{1,0:T(8,128)(2,1)S(1)}, bf16[272,256]{1,0:T(8,128)(2,1)S(1)}, u32[]{:S(2)}, u32[]{:S(2)}) collective-permute-start(bf16[272,256]{1,0:T(8,128)(2,1)S(1)} %pad_maximum_fusion.6), channel_id=1, source_target_pairs={{0,4},{2,6},{4,0},{6,2},{8,12},{10,14},{12,8},{14,10},{16,20},{18,... | collective-permute-start | bytes 417800 | tf_op jit(solution)/shard_map/ppermute | solution.py:37
  86.3 7.6 %collective-permute-start.15 = (bf16[272,256]{1,0:T(8,128)(2,1)S(1)}, bf16[272,256]{1,0:T(8,128)(2,1)S(1)}, u32[]{:S(2)}, u32[]{:S(2)}) collective-permute-start(bf16[272,256]{1,0:T(8,128)(2,1)S(1)} %pad_maximum_fusion.5), channel_id=1, source_target_pairs={{0,2},{2,0},{4,6},{6,4},{8,10},{10,8},{12,14},{14,12},{16,18},{18,... | collective-permute-start | bytes 417800 | tf_op jit(solution)/shard_map/ppermute | solution.py:37
  94.4 6.8 %collective-permute-start.20 = (bf16[272,64]{1,0:T(8,128)(2,1)S(1)}, bf16[272,64]{1,0:T(8,128)(2,1)S(1)}, u32[]{:S(2)}, u32[]{:S(2)}) collective-permute-start(bf16[272,64]{1,0:T(8,128)(2,1)S(1)} %pad_maximum_fusion.14), channel_id=1, source_target_pairs={{0,24},{2,26},{4,28},{6,30},{8,16},{10,18},{12,20},{14,22},{16,8},... | collective-permute-start | bytes 104456 | tf_op jit(solution)/shard_map/ppermute | solution.py:37
  97.1 6.2 %collective-permute-start.19 = (bf16[272,64]{1,0:T(8,128)(2,1)S(1)}, bf16[272,64]{1,0:T(8,128)(2,1)S(1)}, u32[]{:S(2)}, u32[]{:S(2)}) collective-permute-start(bf16[272,64]{1,0:T(8,128)(2,1)S(1)} %pad_maximum_fusion.13), channel_id=1, source_target_pairs={{0,16},{2,18},{4,20},{6,22},{8,24},{10,26},{12,28},{14,30},{16,0},... | collective-permute-start | bytes 104456 | tf_op jit(solution)/shard_map/ppermute | solution.py:37
  97.2 6.2 %collective-permute-start.18 = (bf16[272,64]{1,0:T(8,128)(2,1)S(1)}, bf16[272,64]{1,0:T(8,128)(2,1)S(1)}, u32[]{:S(2)}, u32[]{:S(2)}) collective-permute-start(bf16[272,64]{1,0:T(8,128)(2,1)S(1)} %pad_maximum_fusion.12), channel_id=1, source_target_pairs={{0,8},{2,10},{4,12},{6,14},{8,0},{10,2},{12,4},{14,6},{16,24},{18,... | collective-permute-start | bytes 104456 | tf_op jit(solution)/shard_map/ppermute | solution.py:37
  103.5 5.2 %collective-permute-start.21 = (bf16[272,64]{1,0:T(8,128)(2,1)S(1)}, bf16[272,64]{1,0:T(8,128)(2,1)}, u32[]{:S(2)}, u32[]{:S(2)}) collective-permute-start(bf16[272,64]{1,0:T(8,128)(2,1)S(1)} %pad_maximum_fusion.15), channel_id=1, source_target_pairs={{0,8},{2,10},{4,12},{6,14},{8,0},{10,2},{12,4},{14,6},{16,24},{18,... | collective-permute-start | bytes 104456 | tf_op jit(solution)/shard_map/ppermute | solution.py:51
  104.4 7.8 %collective-permute-start.22 = (bf16[272,64]{1,0:T(8,128)(2,1)S(1)}, bf16[272,64]{1,0:T(8,128)(2,1)S(1)}, u32[]{:S(2)}, u32[]{:S(2)}) collective-permute-start(bf16[272,64]{1,0:T(8,128)(2,1)S(1)} %pad_maximum_fusion.15), channel_id=1, source_target_pairs={{0,16},{2,18},{4,20},{6,22},{8,24},{10,26},{12,28},{14,30},{16,0},... | collective-permute-start | bytes 104456 | tf_op jit(solution)/shard_map/ppermute | solution.py:51
  106.8 6.2 %collective-permute-start.23 = (bf16[272,64]{1,0:T(8,128)(2,1)S(1)}, bf16[272,64]{1,0:T(8,128)(2,1)S(1)}, u32[]{:S(2)}, u32[]{:S(2)}) collective-permute-start(bf16[272,64]{1,0:T(8,128)(2,1)S(1)} %pad_maximum_fusion.15), channel_id=1, source_target_pairs={{0,24},{2,26},{4,28},{6,30},{8,16},{10,18},{12,20},{14,22},{16,8},... | collective-permute-start | bytes 104456 | tf_op jit(solution)/shard_map/ppermute | solution.py:51
  113.5 5.3 %collective-permute-start.24 = (bf16[272,256]{1,0:T(8,128)(2,1)S(1)}, bf16[272,256]{1,0:T(8,128)(2,1)S(1)}, u32[]{:S(2)}, u32[]{:S(2)}) collective-permute-start(bf16[272,256]{1,0:T(8,128)(2,1)S(1)} %dynamic_update_slice.59), channel_id=1, source_target_pairs={{0,2},{2,0},{4,6},{6,4},{8,10},{10,8},{12,14},{14,12},{16,18},{18,... | collective-permute-start | bytes 417800 | tf_op jit(solution)/shard_map/ppermute | solution.py:51
  114.2 5.7 %collective-permute-start.25 = (bf16[272,256]{1,0:T(8,128)(2,1)S(1)}, bf16[272,256]{1,0:T(8,128)(2,1)S(1)}, u32[]{:S(2)}, u32[]{:S(2)}) collective-permute-start(bf16[272,256]{1,0:T(8,128)(2,1)S(1)} %dynamic_update_slice.59), channel_id=1, source_target_pairs={{0,4},{2,6},{4,0},{6,2},{8,12},{10,14},{12,8},{14,10},{16,20},{18,... | collective-permute-start | bytes 417800 | tf_op jit(solution)/shard_map/ppermute | solution.py:51
  115.6 6.0 %collective-permute-start.26 = (bf16[272,256]{1,0:T(8,128)(2,1)S(1)}, bf16[272,256]{1,0:T(8,128)(2,1)S(1)}, u32[]{:S(2)}, u32[]{:S(2)}) collective-permute-start(bf16[272,256]{1,0:T(8,128)(2,1)S(1)} %dynamic_update_slice.59), channel_id=1, source_target_pairs={{0,6},{2,4},{4,2},{6,0},{8,14},{10,12},{12,10},{14,8},{16,22},{18,... | collective-permute-start | bytes 417800 | tf_op jit(solution)/shard_map/ppermute | solution.py:51
  121.6 4.8 %copy-start.5 = (bf16[272,1024]{1,0:T(8,128)(2,1)}, bf16[272,1024]{1,0:T(8,128)(2,1)S(1)}, u32[]{:S(2)}) copy-start(bf16[272,1024]{1,0:T(8,128)(2,1)S(1)} %constant_dynamic-update-slice_fusion.3) | copy-start | bytes 1671172
  126.4 1.2 copy-start.6
  128.7 3.8 %copy-start.3 = (bf16[256,3072]{1,0:T(8,128)(2,1)S(1)}, bf16[256,3072]{1,0:T(8,128)(2,1)}, u32[]{:S(2)}) copy-start(bf16[256,3072]{1,0:T(8,128)(2,1)} %copy-done.1) | copy-start | bytes 4718596
  130.1 2.5 %collective-permute-start.27 = (bf16[144,3072]{1,0:T(8,128)(2,1)S(1)}, bf16[144,3072]{1,0:T(8,128)(2,1)S(1)}, u32[]{:S(2)}, u32[]{:S(2)}) collective-permute-start(bf16[144,3072]{1,0:T(8,128)(2,1)S(1)} %pad_maximum_fusion.1), channel_id=1, source_target_pairs={{0,1},{1,0},{2,3},{3,2},{4,5},{5,4},{6,7},{7,6},{8,9},{9,8},{10,11... | collective-permute-start | bytes 2654216 | tf_op jit(solution)/shard_map/ppermute | solution.py:150
